TPU v7x, 256 devices: a whole 4x4x8 slice. The times are simulated.
256 devices in a mesh: rep: 32 (over z, y_hi, core), fsdp: 8 (over x, y_lo).
Axes of the slice: x: 4, y: 4 (y_hi: 2, y_lo: 2; y = y_hi * 2 + y_lo), z: 8, core: 2. Of those that a mesh axis runs over, the one named last changes fastest.
Arguments:
- hidden: bfloat16 [32768, 7168], P(('rep', 'fsdp')), may hold values from -6 to 6
- grad_out: bfloat16 [32768, 4096], P(('rep', 'fsdp')), may hold values from -24 to 24
- down_weight: bfloat16 [7168, 4096], P('fsdp'), may hold values from -0.0625 to 0.0625
- hash_tiles: bfloat16 [3, 32, 7168], P(None, None, 'fsdp'), may hold values from -1 to 1, as said below
- momentum: float32 [8, 3, 32, 4096], P('fsdp', None, None, 'rep'), may hold values from -6 to 6
- error: float32 [8, 3, 32, 4096], P('fsdp', None, None, 'rep'), may hold values from -6 to 6
Outputs:
- grad_hidden: bfloat16 [32768, 7168], P(('rep', 'fsdp'))
- update: float32 [7168, 4096], P('fsdp', 'rep')
- new_momentum: float32 [8, 3, 32, 4096], P('fsdp', None, None, 'rep')
- new_error: float32 [8, 3, 32, 4096], P('fsdp', None, None, 'rep')
Inputs may be any that keep to these rules, and one draw needn't show every extreme that they name: `hash_tiles`: in every sketch row each hidden unit has exactly one nonzero entry, +1 or -1, in one of the 32 buckets; all other entries are 0.
All inputs are finite; a program needn't handle non-finite values.
Results may differ from a plain program's by a relative error of at most 0.0005.
Values may be sent and summed in bfloat16 or wider, within the bound.
No kernel may reach another device: no remote copies, remote signals or barrier semaphores. Data moves between devices by JAX's collectives and lax.ppermute only.
A program may use at most 128 MiB of HBM per device.

v0:
```python
import math

import jax
import jax.numpy as jnp
from jax import lax
from jax.sharding import PartitionSpec as P

momentum_decay = 0.9
step_size = 0.5


def on_device(hidden, grad_out, down_weight, hash_tiles, momentum, error):
    shards = lax.axis_size("fsdp")
    replicas = lax.axis_size("rep")
    tok_rows = grad_out.shape[0]
    model_width = grad_out.shape[1]
    shard_rows = down_weight.shape[0]
    rows_count = hash_tiles.shape[0]
    buckets = hash_tiles.shape[1]
    sketch_rows = rows_count * buckets
    columns = model_width // replicas
    total_tokens = tok_rows * shards * replicas
    table_scale = math.sqrt(buckets / (shard_rows * total_tokens))
    gathered = lax.all_gather(grad_out, "fsdp", axis=0, tiled=True)
    partial_grads = lax.dot_general(
        gathered, down_weight, (((1,), (1,)), ((), ())), preferred_element_type=jnp.float32
    ).astype(jnp.bfloat16)
    grad_hidden = lax.all_to_all(partial_grads, "fsdp", split_axis=0, concat_axis=1, tiled=True)
    all_hash = lax.all_gather(hash_tiles, "fsdp", axis=2, tiled=True)
    projected = jnp.einsum(
        "kfi,tfi->fkt",
        all_hash.reshape(sketch_rows, shards, shard_rows),
        hidden.reshape(tok_rows, shards, shard_rows),
        preferred_element_type=jnp.float32,
    )
    received = lax.all_to_all(projected, "fsdp", split_axis=0, concat_axis=2, tiled=True)[0]
    split_grads = gathered.reshape(tok_rows * shards, replicas, columns)
    grad_block = split_grads.astype(jnp.float32)
    summed = jnp.einsum("kt,trc->rkc", received, grad_block, precision=lax.Precision.HIGHEST)
    sketch_table = lax.psum_scatter(
        (summed * table_scale).reshape(lax.axis_size("rep") * 1, rows_count, buckets, columns),
        "rep",
        scatter_dimension=0,
        tiled=True,
    )
    new_momentum = momentum_decay * momentum + sketch_table
    accumulated = error + step_size * new_momentum
    hash_float = hash_tiles.astype(jnp.float32)
    update = (
        jnp.einsum("jbi,jbc->ic", hash_float, accumulated[0], precision=lax.Precision.HIGHEST)
        / rows_count
    )
    encoded = jnp.einsum("jbi,ic->jbc", hash_float, update, precision=lax.Precision.HIGHEST)
    new_error = accumulated - encoded[None]
    return (grad_hidden, update, new_momentum, new_error)


def solution(mesh):
    return jax.shard_map(
        on_device,
        mesh=mesh,
        in_specs=(
            P(("rep", "fsdp"), None),
            P(("rep", "fsdp"), None),
            P("fsdp", None),
            P(None, None, "fsdp"),
            P("fsdp", None, None, "rep"),
            P("fsdp", None, None, "rep"),
        ),
        out_specs=(
            P(("rep", "fsdp"), None),
            P("fsdp", "rep"),
            P("fsdp", None, None, "rep"),
            P("fsdp", None, None, "rep"),
        ),
        check_vma=False,
    )
```

profile of v0, /device:TPU:1, one launch (start us, length us, event | category | flops | bytes accessed | tf_op | source)
XLA Modules:
  0.0 367.2 jit_solution(13918211053489265926)
XLA Ops:
  7.2 0.0 all-gather.5.cloned.1.call-start
  7.2 0.7 all-gather.5.cloned.1.call-update
  7.9 0.0 all-gather.3.cloned.1.call-start
  7.9 2.3 copy.13
  10.2 0.0 copy-start.4
  10.2 0.0 all-gather.3.cloned.1.call-update
  10.2 0.0 reduce-scatter.2.cloned.1.call-start
  10.3 44.7 %all-gather.5.cloned.1.call-done = bf16[3,32,7168]{2,1,0:T(8,128)(2,1)} async-done(((bf16[3,32,896]{2,1,0:T(8,128)(2,1)}), bf16[3,32,7168]{2,1,0:T(8,128)(2,1)}) %all-gather.5.cloned.1.call-update) | async-done | bytes 1376272 | tf_op jit(solution)/shard_map/all_gather | solution.py:29
  55.0 1.6 copy.23
  56.6 0.0 copy-done.4
  56.6 0.8 fusion
  57.3 9.1 %all_to_all.34 = f32[8,96,128]{2,1,0:T(8,128)S(1)} all-to-all(f32[8,96,128]{2,1,0:T(8,128)S(1)} %fusion), channel_id=1, replica_groups=mesh['rep'=32,'fsdp'=8] {'fsdp'}, dimensions={0} | all-to-all | bytes 786432 | tf_op jit(solution)/shard_map/all_to_all | solution.py:36
  66.4 0.2 copy.17
  66.6 0.1 reshape.28
  66.7 163.3 %all-gather.3.cloned.1.call-done = bf16[1024,4096]{0,1:T(8,128)(2,1)} async-done(((bf16[128,4096]{0,1:T(8,128)(2,1)}), bf16[1024,4096]{0,1:T(8,128)(2,1)}) %all-gather.3.cloned.1.call-update) | async-done | bytes 8388624 | tf_op jit(solution)/shard_map/all_gather | solution.py:24
  230.1 11.0 %convolution_multiply_fusion = f32[96,32,128]{2,0,1:T(8,128)} fusion(f32[96,1024,1]{1,0,2:T(8,128)S(1)} %reshape.28, bf16[1024,32,128]{0,2,1:T(8,128)(2,1)} %bitcast.43), kind=kOutput, calls=%fused_computation.4 | convolution fusion | flops 4832231424 | bytes 10354688 | tf_op jit(solution)/shard_map/kt,trc->rkc/dot_general | solution.py:39
  241.0 0.0 reduce-scatter.2.cloned.1.call-update
  241.1 13.5 %convolution_convert_fusion = bf16[1024,896]{1,0:T(8,128)(2,1)S(1)} fusion(bf16[1024,4096]{0,1:T(8,128)(2,1)} %all-gather.3.cloned.1.call-done, bf16[896,4096]{1,0:T(8,128)(2,1)} %param.8), kind=kOutput, calls=%fused_computation.3 | convolution fusion | flops 7517110272 | bytes 17563648 | tf_op jit(solution)/shard_map/dot_general | solution.py:25
  254.6 29.5 %all_to_all.35 = bf16[8,128,896]{2,1,0:T(8,128)(2,1)S(1)} all-to-all(bf16[8,128,896]{2,1,0:T(8,128)(2,1)S(1)} %bitcast.48), channel_id=1, replica_groups=mesh['rep'=32,'fsdp'=8] {'fsdp'}, dimensions={0} | all-to-all | bytes 3670016 | tf_op jit(solution)/shard_map/all_to_all | solution.py:28
  284.0 0.0 copy-start.3
  284.0 0.0 copy-start.2
  284.0 1.5 copy.22
  285.6 71.8 %reduce-scatter.2.cloned.1.call-done = f32[1,3,32,128]{3,2,1,0:T(8,128)} async-done(((f32[32,3,32,128]{3,2,1,0:T(8,128)}), f32[1,3,32,128]{3,2,1,0:T(8,128)}) %reduce-scatter.2.cloned.1.call-update) | async-done | bytes 49168 | tf_op jit(solution)/shard_map/reduce_scatter | solution.py:40
  357.4 0.0 copy-done.3
  357.4 0.8 multiply_add_fusion.1
  358.2 0.0 copy-done
  358.2 0.0 copy-done.2
  358.2 0.0 copy-start.1
  358.2 0.4 fusion.4
  358.7 1.0 fusion.5
  359.7 1.0 copy.19
  360.7 0.0 copy-done.1
  (1 shorter events, 0.0 us)
Async XLA Ops:
  7.2 47.8 %all-gather.5.cloned.1.call-start = ((), (), s32[]{:S(2)}) async-start(), calls=%async_computation.4 | async-start | bytes 1548288 | tf_op jit(solution)/shard_map/all_gather | solution.py:29
  7.9 222.2 %all-gather.3.cloned.1.call-start = ((), (), s32[]{:S(2)}) async-start(), calls=%async_computation.3 | async-start | bytes 9437184 | tf_op jit(solution)/shard_map/all_gather | solution.py:24
  10.2 46.3 %copy-start.4 = (bf16[128,7168]{1,0:T(8,128)(2,1)S(1)}, bf16[128,7168]{1,0:T(8,128)(2,1)}, u32[]{:S(2)}) copy-start(bf16[128,7168]{1,0:T(8,128)(2,1)} %param.6) | copy-start | bytes 5505028
  10.2 347.2 %reduce-scatter.2.cloned.1.call-start = ((), (), s32[]{:S(2)}) async-start(), calls=%async_computation.5 | async-start | bytes 1622016 | tf_op jit(solution)/shard_map/reduce_scatter | solution.py:40
  284.0 73.4 %copy-start.3 = (f32[1,3,32,128]{3,2,1,0:T(8,128)S(1)}, f32[1,3,32,128]{3,2,1,0:T(8,128)}, u32[]{:S(2)}) copy-start(f32[1,3,32,128]{3,2,1,0:T(8,128)} %param.10) | copy-start | bytes 147460
  284.0 74.2 %copy-start = (bf16[3,32,896]{2,1,0:T(8,128)(2,1)S(1)}, bf16[3,32,896]{2,1,0:T(8,128)(2,1)}, u32[]{:S(2)}) copy-start(bf16[3,32,896]{2,1,0:T(8,128)(2,1)} %param.9) | copy-start | bytes 516100
  284.0 74.2 %copy-start.2 = (f32[1,3,32,128]{3,2,1,0:T(8,128)S(1)}, f32[1,3,32,128]{3,2,1,0:T(8,128)}, u32[]{:S(2)}) copy-start(f32[1,3,32,128]{3,2,1,0:T(8,128)} %param.11) | copy-start | bytes 147460
  358.2 2.4 copy-start.1
Sparse Core Ops, SparseCore 0:
  9.8 45.1 all-gather.4
  57.3 172.7 all-gather.2
  241.2 116.1 reduce-scatter.1
where the time goes:
time: 372 us; the launch traced here: 367 us
  waiting for transfers between devices  281 us (76%)
  blocking collectives  38.5 us (10%)
  matrix products  26.7 us (7%)
  between operations  13.8 us (4%)
  local copies, waits for them, and re-layouts  6.63 us (2%)
    all_gather x1, waiting for transfers between devices, on_device(): gathered = lax.all_gather(grad_out, 'fsdp', axis=0, tiled=True)  163 us
    reduce_scatter x1, waiting for transfers between devices, on_device(): lax.psum_scatter((summed * table_scale).reshape(lax.axis_size('rep') * 1,...  71.8 us
    all_gather x1, waiting for transfers between devices, on_device(): all_hash = lax.all_gather(hash_tiles, 'fsdp', axis=2, tiled=True)  44.7 us
    all_to_all x1, blocking collectives, on_device(): lax.all_to_all(partial_grads, 'fsdp', split_axis=0, concat_axis=1, tiled=...  29.5 us
    dot_general x1, matrix products, on_device(): lax.dot_general(gathered, down_weight, (((1,), (1,)), ((), ())), preferre...  13.5 us
    dot_general x1, matrix products, on_device(): jnp.einsum('kt,trc->rkc', received, grad_block, precision=lax.Precision.H...  11 us
    all_to_all x1, blocking collectives, on_device(): lax.all_to_all(projected, 'fsdp', split_axis=0, concat_axis=2, tiled=True)  9.06 us
  transfers between devices with their start and end apart: 3, of which 3 were waited for; matrix products, arithmetic and copies ran while one was open for 5% of the time, Pallas kernels for 0%

commit v1 on v0

--- a/solution.py
+++ b/solution.py
@@ -7,6 +7,14 @@
 
 momentum_decay = 0.9
 step_size = 0.5
+
+
+def split3(x):
+    hi = lax.reduce_precision(x, exponent_bits=8, mantissa_bits=7)
+    r1 = x - hi
+    mid = lax.reduce_precision(r1, exponent_bits=8, mantissa_bits=7)
+    lo = r1 - mid
+    return jnp.stack([hi, mid, lo]).astype(jnp.bfloat16)
 
 
 def on_device(hidden, grad_out, down_weight, hash_tiles, momentum, error):
@@ -21,31 +29,49 @@
     columns = model_width // replicas
     total_tokens = tok_rows * shards * replicas
     table_scale = math.sqrt(buckets / (shard_rows * total_tokens))
-    gathered = lax.all_gather(grad_out, "fsdp", axis=0, tiled=True)
-    partial_grads = lax.dot_general(
-        gathered, down_weight, (((1,), (1,)), ((), ())), preferred_element_type=jnp.float32
+
+    levels = jnp.arange(1, buckets + 1, dtype=jnp.float32)
+    hash_float = hash_tiles.astype(jnp.float32)
+    code = jnp.sum(hash_float * levels[None, :, None], axis=1).astype(jnp.bfloat16)
+    all_code = lax.all_gather(code, "fsdp", axis=0, tiled=False).astype(jnp.float32)
+    magnitude = jnp.abs(all_code)
+    sign = jnp.where(all_code > 0, 1.0, -1.0)
+    all_hash = jnp.where(
+        magnitude[:, :, None, :] == levels[None, None, :, None], sign[:, :, None, :], 0.0
     ).astype(jnp.bfloat16)
-    grad_hidden = lax.all_to_all(partial_grads, "fsdp", split_axis=0, concat_axis=1, tiled=True)
-    all_hash = lax.all_gather(hash_tiles, "fsdp", axis=2, tiled=True)
+
+    gathered = lax.all_gather(grad_out, "fsdp", axis=0, tiled=False)
+    partial_grads = jnp.einsum(
+        "ptd,hd->pth", gathered, down_weight, preferred_element_type=jnp.float32
+    ).astype(jnp.bfloat16)
+    grad_hidden = lax.all_to_all(
+        partial_grads.reshape(shards * tok_rows, shard_rows), "fsdp",
+        split_axis=0, concat_axis=1, tiled=True,
+    )
+
     projected = jnp.einsum(
-        "kfi,tfi->fkt",
-        all_hash.reshape(sketch_rows, shards, shard_rows),
+        "fki,tfi->fkt",
+        all_hash.reshape(shards, sketch_rows, shard_rows),
         hidden.reshape(tok_rows, shards, shard_rows),
         preferred_element_type=jnp.float32,
     )
-    received = lax.all_to_all(projected, "fsdp", split_axis=0, concat_axis=2, tiled=True)[0]
-    split_grads = gathered.reshape(tok_rows * shards, replicas, columns)
-    grad_block = split_grads.astype(jnp.float32)
-    summed = jnp.einsum("kt,trc->rkc", received, grad_block, precision=lax.Precision.HIGHEST)
+    received = lax.all_to_all(projected, "fsdp", split_axis=0, concat_axis=0, tiled=True)
+    pieces = split3(received).transpose(1, 0, 2, 3).reshape(shards, 3 * sketch_rows, tok_rows)
+    products = jnp.einsum(
+        "pmt,ptrc->rmc",
+        pieces,
+        gathered.reshape(shards, tok_rows, replicas, columns),
+        preferred_element_type=jnp.float32,
+    ).reshape(replicas, 3, sketch_rows, columns)
+    summed = products[:, 0] + products[:, 1] + products[:, 2]
     sketch_table = lax.psum_scatter(
-        (summed * table_scale).reshape(lax.axis_size("rep") * 1, rows_count, buckets, columns),
+        (summed * table_scale).reshape(replicas, rows_count, buckets, columns),
         "rep",
         scatter_dimension=0,
         tiled=True,
     )
     new_momentum = momentum_decay * momentum + sketch_table
     accumulated = error + step_size * new_momentum
-    hash_float = hash_tiles.astype(jnp.float32)
     update = (
         jnp.einsum("jbi,jbc->ic", hash_float, accumulated[0], precision=lax.Precision.HIGHEST)
         / rows_count

time: 372 us -> 339 us (0.911)
  waiting for transfers between devices: 281 us -> 201 us
  blocking collectives: 38.5 us -> 75.9 us
  local copies, waits for them, and re-layouts: 6.63 us -> 16.9 us
  matrix products: 26.7 us -> 22.3 us
    all_gather x2 -> x1, waiting for transfers between devices: 208 us -> 134 us  [on_device(): gathered = lax.all_gather(grad_out, 'fsdp', axis=0, tiled=False)]
    all_gather x0 -> x1, blocking collectives: none -> 32.3 us  [on_device(): lax.all_gather(code, 'fsdp', axis=0, tiled=False).astype(jnp.float32)]
    unnamed x13, local copies, waits for them, and re-layouts: 4.82 us -> 14.3 us
    reduce_scatter x1, waiting for transfers between devices: 71.8 us -> 66.6 us  [on_device(): lax.psum_scatter((summed * table_scale).reshape(replicas, rows_count, buc...]
    all_to_all x2, blocking collectives: 38.5 us -> 43.6 us  [the longest x1 31.4 us: on_device(): lax.all_to_all(partial_grads.reshape(shards * tok_rows, shard_rows), 'fsd...]
    dot_general x3, matrix products: 25.2 us -> 20.9 us  [the longest x1 13.5 us: on_device(): jnp.einsum('ptd,hd->pth', gathered, down_weight, preferred_element_type=j...]
  transfers between devices with their start and end apart: 3 -> 2, of which waited for: 3 -> 2; matrix products, arithmetic and copies ran while one was open for 5% -> 7% of each run, Pallas kernels for 0% -> 0%
where the time goes in v1:
time: 339 us; the launch traced here: 335 us
  waiting for transfers between devices  201 us (59%)
  blocking collectives  75.9 us (22%)
  matrix products  22.3 us (7%)
  local copies, waits for them, and re-layouts  16.9 us (5%)
  between operations  14.2 us (4%)
  other arithmetic  4.07 us (1%)
    all_gather x1, waiting for transfers between devices, on_device(): gathered = lax.all_gather(grad_out, 'fsdp', axis=0, tiled=False)  134 us
    reduce_scatter x1, waiting for transfers between devices, on_device(): lax.psum_scatter((summed * table_scale).reshape(replicas, rows_count, buc...  66.6 us
    all_gather x1, blocking collectives, on_device(): lax.all_gather(code, 'fsdp', axis=0, tiled=False).astype(jnp.float32)  32.3 us
    all_to_all x1, blocking collectives, on_device(): lax.all_to_all(partial_grads.reshape(shards * tok_rows, shard_rows), 'fsd...  31.4 us
    unnamed x13, local copies, waits for them, and re-layouts  14.3 us
    dot_general x1, matrix products, on_device(): jnp.einsum('ptd,hd->pth', gathered, down_weight, preferred_element_type=j...  13.5 us
    all_to_all x1, blocking collectives, on_device(): lax.all_to_all(projected, 'fsdp', split_axis=0, concat_axis=0, tiled=True)  12.2 us
  transfers between devices with their start and end apart: 2, of which 2 were waited for; matrix products, arithmetic and copies ran while one was open for 7% of the time, Pallas kernels for 0%

profile of v1, /device:TPU:1, one launch (start us, length us, event | category | flops | bytes accessed | tf_op | source)
XLA Modules:
  0.0 334.9 jit_solution(2176952788341591956)
XLA Ops:
  7.2 0.0 copy-start.4
  7.2 0.0 all-gather.5.cloned.1.call-start
  7.2 0.7 all-gather.5.cloned.1.call-update
  7.9 0.0 reduce-scatter.2.cloned.1.call-start
  8.0 0.1 eq.23
  8.1 1.0 multiply_reduce_fusion
  9.1 32.3 %all-gather.2 = bf16[8,3,896]{2,1,0:T(4,128)(2,1)S(1)} all-gather(bf16[1,3,896]{2,1,0:T(4,128)(2,1)S(1)} %bitcast.75), channel_id=3, replica_groups=mesh['rep'=32,'fsdp'=8] {'fsdp'}, dimensions={0}, use_global_device_ids=true | all-gather | bytes 48384 | tf_op jit(solution)/shard_map/all_gather | solution.py:36
  41.5 0.3 fusion.4
  41.8 0.0 copy-done.4
  41.9 0.8 fusion.5
  42.6 12.2 %all_to_all.21 = f32[8,96,128]{2,1,0:T(8,128)S(1)} all-to-all(f32[8,96,128]{2,1,0:T(8,128)S(1)} %fusion.5), channel_id=1, replica_groups=mesh['rep'=32,'fsdp'=8] {'fsdp'}, dimensions={0} | all-to-all | bytes 786432 | tf_op jit(solution)/shard_map/all_to_all | solution.py:58
  54.8 0.1 fusion.17
  54.9 0.1 maximum_bitcast_fusion
  55.1 134.2 %all-gather.5.cloned.1.call-done = bf16[1024,4096]{1,0:T(8,128)(2,1)} async-done(((bf16[128,4096]{1,0:T(8,128)(2,1)}), bf16[1024,4096]{1,0:T(8,128)(2,1)}) %all-gather.5.cloned.1.call-update) | async-done | bytes 8388624 | tf_op jit(solution)/shard_map/all_gather | solution.py:43
  189.2 9.4 %copy.26 = bf16[128,8,32,128]{3,2,1,0:T(8,128)(2,1)} copy(bf16[128,8,32,128]{3,1,2,0:T(8,128)(2,1)} %bitcast.66) | data formatting | bytes 16777216
  198.7 6.6 %fusion = f32[288,32,128,1]{2,0,3,1:T(8,128)S(1)} fusion(bf16[8,288,128,1]{2,1,0,3:T(8,128)(2,1)S(1)} %bitcast.74, bf16[8,128,32,128]{3,2,1,0:T(8,128)(2,1)} %bitcast.68), kind=kOutput, calls=%fused_computation | convolution fusion | flops 2415919104 | bytes 13697024 | tf_op jit(solution)/shard_map/pmt,ptrc->rmc/dot_general | solution.py:60
  205.3 1.6 fusion.11
  207.0 0.0 reduce-scatter.2.cloned.1.call-update
  207.0 13.5 %fusion.8 = bf16[8,128,896]{2,1,0:T(8,128)(2,1)S(1)} fusion(bf16[8,128,4096]{2,1,0:T(8,128)(2,1)} %bitcast.67, bf16[896,4096]{1,0:T(8,128)(2,1)} %param.8), kind=kOutput, calls=%fused_computation.10 | convolution fusion | flops 7517110272 | bytes 17563648 | tf_op jit(solution)/shard_map/ptd,hd->pth/dot_general | solution.py:44
  220.5 31.4 %all_to_all.22 = bf16[8,128,896]{2,1,0:T(8,128)(2,1)S(1)} all-to-all(bf16[8,128,896]{2,1,0:T(8,128)(2,1)S(1)} %fusion.8), channel_id=1, replica_groups=mesh['rep'=32,'fsdp'=8] {'fsdp'}, dimensions={0} | all-to-all | bytes 3670016 | tf_op jit(solution)/shard_map/all_to_all | solution.py:47
  251.8 2.4 copy.18
  254.2 3.9 %copy.22 = bf16[128,7168]{1,0:T(8,128)(2,1)} copy(bf16[128,7168]{0,1:T(8,128)(2,1)} %bitcast.70) | data formatting | bytes 3670016
  258.1 66.6 %reduce-scatter.2.cloned.1.call-done = f32[1,3,32,128]{3,2,1,0:T(8,128)} async-done(((f32[32,3,32,128]{3,2,1,0:T(8,128)}), f32[1,3,32,128]{3,2,1,0:T(8,128)}) %reduce-scatter.2.cloned.1.call-update) | async-done | bytes 49168 | tf_op jit(solution)/shard_map/reduce_scatter | solution.py:67
  324.8 0.0 copy-done.3
  324.8 0.8 multiply_add_fusion.1
  325.6 0.0 copy-done
  325.6 0.0 copy-done.2
  325.6 0.0 copy-start.1
  325.6 0.4 fusion.12
  326.0 1.0 fusion.13
  327.1 1.0 copy.23
  328.0 0.0 copy-done.1
  (8 shorter events, 0.1 us)
Async XLA Ops:
  7.2 34.7 %copy-start.4 = (bf16[128,7168]{1,0:T(8,128)(2,1)S(1)}, bf16[128,7168]{1,0:T(8,128)(2,1)}, u32[]{:S(2)}) copy-start(bf16[128,7168]{1,0:T(8,128)(2,1)} %param.6) | copy-start | bytes 5505028
  7.2 182.1 %all-gather.5.cloned.1.call-start = ((), (), s32[]{:S(2)}) async-start(), calls=%async_computation.4 | async-start | bytes 9437184 | tf_op jit(solution)/shard_map/all_gather | solution.py:43
  7.9 316.9 %reduce-scatter.2.cloned.1.call-start = ((), (), s32[]{:S(2)}) async-start(), calls=%async_computation.3 | async-start | bytes 1622016 | tf_op jit(solution)/shard_map/reduce_scatter | solution.py:67
  254.2 70.5 %copy-start.3 = (f32[1,3,32,128]{3,2,1,0:T(8,128)S(1)}, f32[1,3,32,128]{3,2,1,0:T(8,128)}, u32[]{:S(2)}) copy-start(f32[1,3,32,128]{3,2,1,0:T(8,128)} %param.10) | copy-start | bytes 147460
  254.2 71.4 %copy-start = (bf16[3,32,896]{2,1,0:T(8,128)(2,1)S(1)}, bf16[3,32,896]{2,1,0:T(8,128)(2,1)}, u32[]{:S(2)}) copy-start(bf16[3,32,896]{2,1,0:T(8,128)(2,1)} %param.9) | copy-start | bytes 516100
  254.2 71.4 %copy-start.2 = (f32[1,3,32,128]{3,2,1,0:T(8,128)S(1)}, f32[1,3,32,128]{3,2,1,0:T(8,128)}, u32[]{:S(2)}) copy-start(f32[1,3,32,128]{3,2,1,0:T(8,128)} %param.11) | copy-start | bytes 147460
  325.6 2.4 copy-start.1
Sparse Core Ops, SparseCore 0:
  9.8 179.3 all-gather.4
  207.1 117.6 reduce-scatter.1

commit v2 on v1

--- a/solution.py
+++ b/solution.py
@@ -15,6 +15,23 @@
     mid = lax.reduce_precision(r1, exponent_bits=8, mantissa_bits=7)
     lo = r1 - mid
     return jnp.stack([hi, mid, lo]).astype(jnp.bfloat16)
+
+
+def halving_scatter(blocks, replicas):
+    me = lax.axis_index("rep")
+    nbits = replicas.bit_length() - 1
+    rest = blocks.shape[1:]
+    data = blocks.reshape((2,) * nbits + rest)
+    remaining = list(range(nbits - 1, -1, -1))
+    for bit in (0, 2, 3, 4, 1)[:nbits] if nbits == 5 else range(nbits):
+        axis = remaining.index(bit)
+        mine = (me >> bit) & 1
+        keep = lax.dynamic_index_in_dim(data, mine, axis=axis, keepdims=False)
+        send = lax.dynamic_index_in_dim(data, 1 - mine, axis=axis, keepdims=False)
+        pairs = [(j, j ^ (1 << bit)) for j in range(replicas)]
+        data = keep + lax.ppermute(send, "rep", pairs)
+        remaining.pop(axis)
+    return data.reshape((1,) + rest)
 
 
 def on_device(hidden, grad_out, down_weight, hash_tiles, momentum, error):
@@ -40,6 +57,7 @@
         magnitude[:, :, None, :] == levels[None, None, :, None], sign[:, :, None, :], 0.0
     ).astype(jnp.bfloat16)
 
+    all_hash, grad_out = lax.optimization_barrier((all_hash, grad_out))
     gathered = lax.all_gather(grad_out, "fsdp", axis=0, tiled=False)
     partial_grads = jnp.einsum(
         "ptd,hd->pth", gathered, down_weight, preferred_element_type=jnp.float32
@@ -64,11 +82,8 @@
         preferred_element_type=jnp.float32,
     ).reshape(replicas, 3, sketch_rows, columns)
     summed = products[:, 0] + products[:, 1] + products[:, 2]
-    sketch_table = lax.psum_scatter(
-        (summed * table_scale).reshape(replicas, rows_count, buckets, columns),
-        "rep",
-        scatter_dimension=0,
-        tiled=True,
+    sketch_table = halving_scatter(
+        (summed * table_scale).reshape(replicas, rows_count, buckets, columns), replicas
     )
     new_momentum = momentum_decay * momentum + sketch_table
     accumulated = error + step_size * new_momentum

time: 339 us -> 307 us (0.906)
  blocking collectives: 75.9 us -> 23.1 us
  starting transfers between devices: 0.08 us -> 23.9 us
    reduce_scatter x1 -> x0, waiting for transfers between devices: 66.6 us -> none  [on_device(): lax.psum_scatter((summed * table_scale).reshape(replicas, rows_count, buc...]
    all_to_all x2 -> x0, blocking collectives: 43.6 us -> none  [the longest x1 31.4 us: on_device(): lax.all_to_all(partial_grads.reshape(shards * tok_rows, shard_rows), 'fsd...]
    all_gather x1, waiting for transfers between devices: 134 us -> 167 us  [on_device(): gathered = lax.all_gather(grad_out, 'fsdp', axis=0, tiled=False)]
    ppermute x0 -> x5, waiting for transfers between devices: none -> 23.1 us  [halving_scatter(): data = keep + lax.ppermute(send, 'rep', pairs)]
    all_to_all x0 -> x2, starting transfers between devices: none -> 13.2 us  [the longest x1 8.52 us: on_device(): lax.all_to_all(partial_grads.reshape(shards * tok_rows, shard_rows), 'fsd...]
    all_to_all x0 -> x2, waiting for transfers between devices: none -> 11.2 us  [the longest x1 6.31 us: on_device(): lax.all_to_all(projected, 'fsdp', split_axis=0, concat_axis=0, tiled=True)]
    ppermute x0 -> x5, starting transfers between devices: none -> 10.7 us  [halving_scatter(): data = keep + lax.ppermute(send, 'rep', pairs)]
    all_gather x1, blocking collectives: 32.3 us -> 23.1 us  [on_device(): lax.all_gather(code, 'fsdp', axis=0, tiled=False).astype(jnp.float32)]
  transfers between devices with their start and end apart: 2 -> 8, of which waited for: 2 -> 7; matrix products, arithmetic and copies ran while one was open for 7% -> 6% of each run, Pallas kernels for 0% -> 0%
where the time goes in v2:
time: 307 us; the launch traced here: 306 us
  waiting for transfers between devices  201 us (65%)
  matrix products  24 us (8%)
  starting transfers between devices  23.9 us (8%)
  blocking collectives  23.1 us (8%)
  local copies, waits for them, and re-layouts  17 us (6%)
  between operations  14.2 us (5%)
    all_gather x1, waiting for transfers between devices, on_device(): gathered = lax.all_gather(grad_out, 'fsdp', axis=0, tiled=False)  167 us
    ppermute x5, waiting for transfers between devices, halving_scatter(): data = keep + lax.ppermute(send, 'rep', pairs)  23.1 us
    all_gather x1, blocking collectives, on_device(): lax.all_gather(code, 'fsdp', axis=0, tiled=False).astype(jnp.float32)  23.1 us
    unnamed x14, local copies, waits for them, and re-layouts  14.4 us
    dot_general x1, matrix products, on_device(): jnp.einsum('ptd,hd->pth', gathered, down_weight, preferred_element_type=j...  14.3 us
    ppermute x5, starting transfers between devices, halving_scatter(): data = keep + lax.ppermute(send, 'rep', pairs)  10.7 us
    all_to_all x1, starting transfers between devices, on_device(): lax.all_to_all(partial_grads.reshape(shards * tok_rows, shard_rows), 'fsd...  8.52 us
    dot_general x1, matrix products, on_device(): jnp.einsum('pmt,ptrc->rmc', pieces, gathered.reshape(shards, tok_rows, re...  6.67 us
  transfers between devices with their start and end apart: 8, of which 7 were waited for; matrix products, arithmetic and copies ran while one was open for 6% of the time, Pallas kernels for 0%

profile of v2, /device:TPU:1, one launch (start us, length us, event | category | flops | bytes accessed | tf_op | source)
XLA Modules:
  0.0 306.0 jit_solution(16266308629232814713)
XLA Ops:
  7.2 1.2 multiply_reduce_fusion
  8.4 23.1 %all-gather.2 = bf16[8,3,896]{2,1,0:T(4,128)(2,1)S(1)} all-gather(bf16[1,3,896]{2,1,0:T(4,128)(2,1)S(1)} %bitcast.97), channel_id=2, replica_groups=mesh['rep'=32,'fsdp'=8] {'fsdp'}, dimensions={0}, use_global_device_ids=true | all-gather | bytes 48384 | tf_op jit(solution)/shard_map/all_gather | solution.py:53
  31.6 0.4 select_convert_fusion
  32.0 1.5 fusion.4
  33.5 4.6 %all-to-all-start.1 = ((f32[8,96,128]{2,1,0:T(8,128)}), f32[8,96,128]{2,1,0:T(8,128)S(1)}, u32[]{:S(2)}, u32[]{:S(2)}) async-start(f32[8,96,128]{2,1,0:T(8,128)} %fusion.4), calls=%async_computation.1 | async-start | bytes 786432 | tf_op jit(solution)/shard_map/all_to_all | solution.py:76
  38.1 6.3 %all-to-all-done.1 = f32[8,96,128]{2,1,0:T(8,128)S(1)} async-done(((f32[8,96,128]{2,1,0:T(8,128)}), f32[8,96,128]{2,1,0:T(8,128)S(1)}, u32[]{:S(2)}, u32[]{:S(2)}) %all-to-all-start.1) | async-done | bytes 393248 | tf_op jit(solution)/shard_map/all_to_all | solution.py:76
  44.4 0.1 fusion.17
  44.6 0.1 maximum_bitcast_fusion
  44.7 166.9 %all-gather.5.cloned.1.call-done = bf16[1024,4096]{1,0:T(8,128)(2,1)} async-done(((bf16[128,4096]{1,0:T(8,128)(2,1)}), bf16[1024,4096]{1,0:T(8,128)(2,1)}) %all-gather.5.cloned.1.call-update) | async-done | bytes 8388624 | tf_op jit(solution)/shard_map/all_gather | solution.py:61
  211.6 9.5 %copy.32 = bf16[128,8,32,128]{3,2,1,0:T(8,128)(2,1)} copy(bf16[128,8,32,128]{3,1,2,0:T(8,128)(2,1)} %bitcast.86) | data formatting | bytes 16777216
  221.1 6.7 %fusion = f32[32,128,288,1]{1,2,3,0:T(8,128)S(1)} fusion(bf16[8,288,128,1]{2,1,0,3:T(8,128)(2,1)S(1)} %bitcast.96, bf16[8,128,32,128]{3,2,1,0:T(8,128)(2,1)} %bitcast.88), kind=kOutput, calls=%fused_computation | convolution fusion | flops 2415919104 | bytes 13697024 | tf_op jit(solution)/shard_map/pmt,ptrc->rmc/dot_general | solution.py:78
  227.8 0.4 fusion.10
  228.2 0.1 constant_dynamic-slice_fusion.1
  228.3 0.1 copy.43
  228.4 0.7 collective-permute-start
  229.1 1.9 collective-permute-done
  231.0 0.2 fusion.13
  231.2 1.4 collective-permute-start.1
  232.6 9.1 %collective-permute-done.1 = f32[2,2,2,3,32,128]{5,4,3,2,1,0:T(8,128)S(1)} collective-permute-done((f32[2,2,2,3,32,128]{5,4,3,2,1,0:T(8,128)S(1)}, f32[2,2,2,3,32,128]{5,4,3,2,1,0:T(8,128)S(1)}, u32[]{:S(2)}, u32[]{:S(2)}) %collective-permute-start.1) | collective-permute-done | bytes 393248 | tf_op jit(solution)/shard_map/ppermute | solution.py:32
  241.8 2.4 collective-permute-start.2
  244.1 14.3 %fusion.7 = bf16[8,128,896]{2,1,0:T(8,128)(2,1)} fusion(bf16[8,128,4096]{2,1,0:T(8,128)(2,1)} %bitcast.87, bf16[896,4096]{1,0:T(8,128)(2,1)} %param.8), kind=kOutput, calls=%fused_computation.8 | convolution fusion | flops 7517110272 | bytes 17563648 | tf_op jit(solution)/shard_map/ptd,hd->pth/dot_general | solution.py:62
  258.5 8.5 %all-to-all-start = ((bf16[8,128,896]{2,1,0:T(8,128)(2,1)}), bf16[8,128,896]{2,1,0:T(8,128)(2,1)S(1)}, u32[]{:S(2)}, u32[]{:S(2)}) async-start(bf16[8,128,896]{2,1,0:T(8,128)(2,1)} %fusion.7), calls=%async_computation | async-start | bytes 3670016 | tf_op jit(solution)/shard_map/all_to_all | solution.py:65
  267.1 3.7 %collective-permute-start.3 = (f32[2,3,32,128]{3,2,1,0:T(8,128)S(1)}, f32[2,3,32,128]{3,2,1,0:T(8,128)S(1)}, u32[]{:S(2)}, u32[]{:S(2)}) collective-permute-start(f32[2,3,32,128]{3,2,1,0:T(8,128)S(1)} %dynamic-slice_bitcast_fusion.2), channel_id=1, source_target_pairs={{0,128},{8,136},{16,144},{24,152},{32,160},{40,168},{48,176},{56,1... | collective-permute-start | bytes 294920 | tf_op jit(solution)/shard_map/ppermute | solution.py:32
  270.8 3.8 %collective-permute-done.3 = f32[2,3,32,128]{3,2,1,0:T(8,128)S(1)} collective-permute-done((f32[2,3,32,128]{3,2,1,0:T(8,128)S(1)}, f32[2,3,32,128]{3,2,1,0:T(8,128)S(1)}, u32[]{:S(2)}, u32[]{:S(2)}) %collective-permute-start.3) | collective-permute-done | bytes 98336 | tf_op jit(solution)/shard_map/ppermute | solution.py:32
  274.7 2.5 collective-permute-start.4
  277.2 8.3 %collective-permute-done.4 = f32[3,32,128]{2,1,0:T(8,128)S(1)} collective-permute-done((f32[3,32,128]{2,1,0:T(8,128)S(1)}, f32[3,32,128]{2,1,0:T(8,128)S(1)}, u32[]{:S(2)}, u32[]{:S(2)}) %collective-permute-start.4) | collective-permute-done | bytes 49184 | tf_op jit(solution)/shard_map/ppermute | solution.py:32
  285.5 0.4 fusion.11
  286.0 1.0 copy.27
  286.9 1.0 fusion.12
  288.0 4.9 %all-to-all-done = bf16[8,128,896]{2,1,0:T(8,128)(2,1)S(1)} async-done(((bf16[8,128,896]{2,1,0:T(8,128)(2,1)}), bf16[8,128,896]{2,1,0:T(8,128)(2,1)S(1)}, u32[]{:S(2)}, u32[]{:S(2)}) %all-to-all-start) | async-done | bytes 1835040 | tf_op jit(solution)/shard_map/all_to_all | solution.py:65
  292.8 2.4 copy.20
  295.2 3.9 %copy.26 = bf16[128,7168]{1,0:T(8,128)(2,1)} copy(bf16[128,7168]{0,1:T(8,128)(2,1)} %bitcast.90) | data formatting | bytes 3670016
  (25 shorter events, 0.4 us)
Async XLA Ops:
  7.2 24.8 %copy-start.4 = (bf16[128,7168]{1,0:T(8,128)(2,1)S(1)}, bf16[128,7168]{1,0:T(8,128)(2,1)}, u32[]{:S(2)}) copy-start(bf16[128,7168]{1,0:T(8,128)(2,1)} %param.6) | copy-start | bytes 5505028
  7.2 204.4 %all-gather.5.cloned.1.call-start = ((), (), s32[]{:S(2)}) async-start(), calls=%async_computation.2 | async-start | bytes 9437184 | tf_op jit(solution)/shard_map/all_gather | solution.py:61
  33.5 10.9 %all-to-all-start.1 = ((f32[8,96,128]{2,1,0:T(8,128)}), f32[8,96,128]{2,1,0:T(8,128)S(1)}, u32[]{:S(2)}, u32[]{:S(2)}) async-start(f32[8,96,128]{2,1,0:T(8,128)} %fusion.4), calls=%async_computation.1 | async-start | bytes 786432 | tf_op jit(solution)/shard_map/all_to_all | solution.py:76
  228.4 2.7 collective-permute-start
  231.2 10.4 %collective-permute-start.1 = (f32[2,2,2,3,32,128]{5,4,3,2,1,0:T(8,128)S(1)}, f32[2,2,2,3,32,128]{5,4,3,2,1,0:T(8,128)S(1)}, u32[]{:S(2)}, u32[]{:S(2)}) collective-permute-start(f32[2,2,2,3,32,128]{5,4,3,2,1,0:T(8,128)S(1)} %dynamic-slice_bitcast_fusion), channel_id=1, source_target_pairs={{0,32},{8,40},{16,48},{24,56},{32,0},{40,8},{48,16},{56,24},{64,96... | collective-permute-start | bytes 1179656 | tf_op jit(solution)/shard_map/ppermute | solution.py:32
  241.8 25.2 %collective-permute-start.2 = (f32[2,2,3,32,128]{4,3,2,1,0:T(8,128)S(1)}, f32[2,2,3,32,128]{4,3,2,1,0:T(8,128)S(1)}, u32[]{:S(2)}, u32[]{:S(2)}) collective-permute-start(f32[2,2,3,32,128]{4,3,2,1,0:T(8,128)S(1)} %dynamic-slice_bitcast_fusion.1), channel_id=1, source_target_pairs={{0,64},{8,72},{16,80},{24,88},{32,96},{40,104},{48,112},{56,120},{... | collective-permute-start | bytes 589832 | tf_op jit(solution)/shard_map/ppermute | solution.py:32
  258.5 27.0 %copy-start.3 = (f32[1,3,32,128]{3,2,1,0:T(8,128)S(1)}, f32[1,3,32,128]{3,2,1,0:T(8,128)}, u32[]{:S(2)}) copy-start(f32[1,3,32,128]{3,2,1,0:T(8,128)} %param.10) | copy-start | bytes 147460
  258.5 27.1 %copy-start = (bf16[3,32,896]{2,1,0:T(8,128)(2,1)S(1)}, bf16[3,32,896]{2,1,0:T(8,128)(2,1)}, u32[]{:S(2)}) copy-start(bf16[3,32,896]{2,1,0:T(8,128)(2,1)} %param.9) | copy-start | bytes 516100
  258.5 27.1 %copy-start.2 = (f32[1,3,32,128]{3,2,1,0:T(8,128)S(1)}, f32[1,3,32,128]{3,2,1,0:T(8,128)}, u32[]{:S(2)}) copy-start(f32[1,3,32,128]{3,2,1,0:T(8,128)} %param.11) | copy-start | bytes 147460
  258.5 34.4 %all-to-all-start = ((bf16[8,128,896]{2,1,0:T(8,128)(2,1)}), bf16[8,128,896]{2,1,0:T(8,128)(2,1)S(1)}, u32[]{:S(2)}, u32[]{:S(2)}) async-start(bf16[8,128,896]{2,1,0:T(8,128)(2,1)} %fusion.7), calls=%async_computation | async-start | bytes 3670016 | tf_op jit(solution)/shard_map/all_to_all | solution.py:65
  267.1 7.5 %collective-permute-start.3 = (f32[2,3,32,128]{3,2,1,0:T(8,128)S(1)}, f32[2,3,32,128]{3,2,1,0:T(8,128)S(1)}, u32[]{:S(2)}, u32[]{:S(2)}) collective-permute-start(f32[2,3,32,128]{3,2,1,0:T(8,128)S(1)} %dynamic-slice_bitcast_fusion.2), channel_id=1, source_target_pairs={{0,128},{8,136},{16,144},{24,152},{32,160},{40,168},{48,176},{56,1... | collective-permute-start | bytes 294920 | tf_op jit(solution)/shard_map/ppermute | solution.py:32
  274.7 10.8 %collective-permute-start.4 = (f32[3,32,128]{2,1,0:T(8,128)S(1)}, f32[3,32,128]{2,1,0:T(8,128)S(1)}, u32[]{:S(2)}, u32[]{:S(2)}) collective-permute-start(f32[3,32,128]{2,1,0:T(8,128)S(1)} %dynamic-slice_bitcast_fusion.3), channel_id=1, source_target_pairs={{0,16},{8,24},{16,0},{24,8},{32,48},{40,56},{48,32},{56,40},{64,80... | collective-permute-start | bytes 147464 | tf_op jit(solution)/shard_map/ppermute | solution.py:32
  285.5 9.7 %copy-start.1 = (f32[1,3,32,128]{3,2,1,0:T(8,128)}, f32[1,3,32,128]{3,2,1,0:T(8,128)S(1)}, u32[]{:S(2)}) copy-start(f32[1,3,32,128]{3,2,1,0:T(8,128)S(1)} %bitcast_add_fusion.3) | copy-start | bytes 147460
Sparse Core Ops, SparseCore 0:
  32.1 179.4 all-gather.4

commit v3 on v2

--- a/solution.py
+++ b/solution.py
@@ -57,7 +57,6 @@
         magnitude[:, :, None, :] == levels[None, None, :, None], sign[:, :, None, :], 0.0
     ).astype(jnp.bfloat16)
 
-    all_hash, grad_out = lax.optimization_barrier((all_hash, grad_out))
     gathered = lax.all_gather(grad_out, "fsdp", axis=0, tiled=False)
     partial_grads = jnp.einsum(
         "ptd,hd->pth", gathered, down_weight, preferred_element_type=jnp.float32
@@ -74,14 +73,11 @@
         preferred_element_type=jnp.float32,
     )
     received = lax.all_to_all(projected, "fsdp", split_axis=0, concat_axis=0, tiled=True)
-    pieces = split3(received).transpose(1, 0, 2, 3).reshape(shards, 3 * sketch_rows, tok_rows)
-    products = jnp.einsum(
-        "pmt,ptrc->rmc",
-        pieces,
-        gathered.reshape(shards, tok_rows, replicas, columns),
-        preferred_element_type=jnp.float32,
-    ).reshape(replicas, 3, sketch_rows, columns)
-    summed = products[:, 0] + products[:, 1] + products[:, 2]
+    pieces = split3(received).transpose(0, 2, 1, 3).reshape(3 * sketch_rows, shards * tok_rows)
+    products = jnp.dot(
+        pieces, gathered.reshape(shards * tok_rows, model_width), preferred_element_type=jnp.float32
+    ).reshape(3, sketch_rows, replicas, columns)
+    summed = (products[0] + products[1] + products[2]).transpose(1, 0, 2)
     sketch_table = halving_scatter(
         (summed * table_scale).reshape(replicas, rows_count, buckets, columns), replicas
     )

time: 307 us -> 275 us (0.90)
  waiting for transfers between devices: 201 us -> 169 us
  blocking collectives: 23.1 us -> 32.3 us
  local copies, waits for them, and re-layouts: 17 us -> 9.81 us
    all_gather x1, waiting for transfers between devices: 167 us -> 134 us  [on_device(): gathered = lax.all_gather(grad_out, 'fsdp', axis=0, tiled=False)]
    all_gather x1, blocking collectives: 23.1 us -> 32.3 us  [on_device(): lax.all_gather(code, 'fsdp', axis=0, tiled=False).astype(jnp.float32)]
    unnamed x14, local copies, waits for them, and re-layouts: 14.4 us -> 5.4 us
  transfers between devices with their start and end apart: 8 -> 8, of which waited for: 7 -> 7; matrix products, arithmetic and copies ran while one was open for 6% -> 7% of each run, Pallas kernels for 0% -> 0%
where the time goes in v3:
time: 275 us; the launch traced here: 274 us
  waiting for transfers between devices  169 us (61%)
  blocking collectives  32.3 us (12%)
  starting transfers between devices  24.5 us (9%)
  matrix products  22.3 us (8%)
  between operations  14.2 us (5%)
  local copies, waits for them, and re-layouts  9.81 us (4%)
    all_gather x1, waiting for transfers between devices, on_device(): gathered = lax.all_gather(grad_out, 'fsdp', axis=0, tiled=False)  134 us
    all_gather x1, blocking collectives, on_device(): lax.all_gather(code, 'fsdp', axis=0, tiled=False).astype(jnp.float32)  32.3 us
    ppermute x5, waiting for transfers between devices, halving_scatter(): data = keep + lax.ppermute(send, 'rep', pairs)  23 us
    dot_general x1, matrix products, on_device(): jnp.einsum('ptd,hd->pth', gathered, down_weight, preferred_element_type=j...  14.3 us
    ppermute x5, starting transfers between devices, halving_scatter(): data = keep + lax.ppermute(send, 'rep', pairs)  10.9 us
    all_to_all x1, starting transfers between devices, on_device(): lax.all_to_all(partial_grads.reshape(shards * tok_rows, shard_rows), 'fsd...  8.44 us
    all_to_all x1, waiting for transfers between devices, on_device(): lax.all_to_all(projected, 'fsdp', split_axis=0, concat_axis=0, tiled=True)  6.37 us
  transfers between devices with their start and end apart: 8, of which 7 were waited for; matrix products, arithmetic and copies ran while one was open for 7% of the time, Pallas kernels for 0%

profile of v3, /device:TPU:1, one launch (start us, length us, event | category | flops | bytes accessed | tf_op | source)
XLA Modules:
  0.0 274.3 jit_solution(14236049774381865638)
XLA Ops:
  7.2 0.7 all-gather.5.cloned.1.call-update
  8.0 1.0 multiply_reduce_fusion
  9.1 32.3 %all-gather.2 = bf16[8,3,896]{2,1,0:T(4,128)(2,1)S(1)} all-gather(bf16[1,3,896]{2,1,0:T(4,128)(2,1)S(1)} %bitcast.99), channel_id=3, replica_groups=mesh['rep'=32,'fsdp'=8] {'fsdp'}, dimensions={0}, use_global_device_ids=true | all-gather | bytes 48384 | tf_op jit(solution)/shard_map/all_gather | solution.py:53
  41.5 0.3 fusion.2
  41.8 1.5 fusion.3
  43.3 5.1 %all-to-all-start.1 = ((f32[8,96,128]{2,1,0:T(8,128)}), f32[8,96,128]{2,1,0:T(8,128)S(1)}, u32[]{:S(2)}, u32[]{:S(2)}) async-start(f32[8,96,128]{2,1,0:T(8,128)} %fusion.3), calls=%async_computation.1 | async-start | bytes 786432 | tf_op jit(solution)/shard_map/all_to_all | solution.py:75
  48.4 6.4 %all-to-all-done.1 = f32[8,96,128]{2,1,0:T(8,128)S(1)} async-done(((f32[8,96,128]{2,1,0:T(8,128)}), f32[8,96,128]{2,1,0:T(8,128)S(1)}, u32[]{:S(2)}, u32[]{:S(2)}) %all-to-all-start.1) | async-done | bytes 393248 | tf_op jit(solution)/shard_map/all_to_all | solution.py:75
  55.0 0.2 copy.21
  55.2 134.0 %all-gather.5.cloned.1.call-done = bf16[1024,4096]{1,0:T(8,128)(2,1)} async-done(((bf16[128,4096]{1,0:T(8,128)(2,1)}), bf16[1024,4096]{1,0:T(8,128)(2,1)}) %all-gather.5.cloned.1.call-update) | async-done | bytes 8388624 | tf_op jit(solution)/shard_map/all_gather | solution.py:60
  189.2 5.0 %fusion.14 = f32[288,4096]{1,0:T(8,128)S(1)} fusion(bf16[1024,4096]{1,0:T(8,128)(2,1)} %all-gather.5.cloned.1.call-done, bf16[36,8,8,128]{3,2,1,0:T(8,128)(2,1)S(1)} %bitcast.97), kind=kOutput, calls=%fused_computation.20 | convolution fusion | flops 2415919104 | bytes 13697024 | tf_op jit(solution)/shard_map/dot_general | solution.py:77
  194.2 0.3 fusion.10
  194.5 0.3 copy.30
  194.8 1.6 constant_dynamic-slice_fusion.1
  196.4 0.3 copy.43
  196.6 0.7 collective-permute-start
  197.4 1.9 collective-permute-done
  199.3 0.3 fusion.13
  199.6 1.4 collective-permute-start.1
  201.0 9.0 %collective-permute-done.1 = f32[2,2,2,3,32,128]{5,4,3,2,1,0:T(8,128)S(1)} collective-permute-done((f32[2,2,2,3,32,128]{5,4,3,2,1,0:T(8,128)S(1)}, f32[2,2,2,3,32,128]{5,4,3,2,1,0:T(8,128)S(1)}, u32[]{:S(2)}, u32[]{:S(2)}) %collective-permute-start.1) | collective-permute-done | bytes 393248 | tf_op jit(solution)/shard_map/ppermute | solution.py:32
  210.1 2.4 collective-permute-start.2
  212.5 14.3 %fusion.6 = bf16[8,128,896]{2,1,0:T(8,128)(2,1)} fusion(bf16[8,128,4096]{2,1,0:T(8,128)(2,1)} %bitcast.92, bf16[896,4096]{1,0:T(8,128)(2,1)} %param.8), kind=kOutput, calls=%fused_computation.8 | convolution fusion | flops 7517110272 | bytes 17563648 | tf_op jit(solution)/shard_map/ptd,hd->pth/dot_general | solution.py:61
  226.9 8.4 %all-to-all-start = ((bf16[8,128,896]{2,1,0:T(8,128)(2,1)}), bf16[8,128,896]{2,1,0:T(8,128)(2,1)S(1)}, u32[]{:S(2)}, u32[]{:S(2)}) async-start(bf16[8,128,896]{2,1,0:T(8,128)(2,1)} %fusion.6), calls=%async_computation | async-start | bytes 3670016 | tf_op jit(solution)/shard_map/all_to_all | solution.py:64
  235.4 3.8 %collective-permute-start.3 = (f32[2,3,32,128]{3,2,1,0:T(8,128)S(1)}, f32[2,3,32,128]{3,2,1,0:T(8,128)S(1)}, u32[]{:S(2)}, u32[]{:S(2)}) collective-permute-start(f32[2,3,32,128]{3,2,1,0:T(8,128)S(1)} %dynamic-slice_bitcast_fusion.2), channel_id=1, source_target_pairs={{0,128},{8,136},{16,144},{24,152},{32,160},{40,168},{48,176},{56,1... | collective-permute-start | bytes 294920 | tf_op jit(solution)/shard_map/ppermute | solution.py:32
  239.2 3.7 %collective-permute-done.3 = f32[2,3,32,128]{3,2,1,0:T(8,128)S(1)} collective-permute-done((f32[2,3,32,128]{3,2,1,0:T(8,128)S(1)}, f32[2,3,32,128]{3,2,1,0:T(8,128)S(1)}, u32[]{:S(2)}, u32[]{:S(2)}) %collective-permute-start.3) | collective-permute-done | bytes 98336 | tf_op jit(solution)/shard_map/ppermute | solution.py:32
  243.0 2.5 collective-permute-start.4
  245.5 8.3 %collective-permute-done.4 = f32[3,32,128]{2,1,0:T(8,128)S(1)} collective-permute-done((f32[3,32,128]{2,1,0:T(8,128)S(1)}, f32[3,32,128]{2,1,0:T(8,128)S(1)}, u32[]{:S(2)}, u32[]{:S(2)}) %collective-permute-start.4) | collective-permute-done | bytes 49184 | tf_op jit(solution)/shard_map/ppermute | solution.py:32
  253.9 0.4 fusion.11
  254.3 1.0 copy.25
  255.3 1.0 fusion.12
  256.3 4.9 %all-to-all-done = bf16[8,128,896]{2,1,0:T(8,128)(2,1)S(1)} async-done(((bf16[8,128,896]{2,1,0:T(8,128)(2,1)}), bf16[8,128,896]{2,1,0:T(8,128)(2,1)S(1)}, u32[]{:S(2)}, u32[]{:S(2)}) %all-to-all-start) | async-done | bytes 1835040 | tf_op jit(solution)/shard_map/all_to_all | solution.py:64
  261.2 2.4 copy.19
  263.6 3.9 %copy.24 = bf16[128,7168]{1,0:T(8,128)(2,1)} copy(bf16[128,7168]{0,1:T(8,128)(2,1)} %bitcast.94) | data formatting | bytes 3670016
  (27 shorter events, 0.6 us)
Async XLA Ops:
  7.2 34.6 %copy-start.4 = (bf16[128,7168]{1,0:T(8,128)(2,1)S(1)}, bf16[128,7168]{1,0:T(8,128)(2,1)}, u32[]{:S(2)}) copy-start(bf16[128,7168]{1,0:T(8,128)(2,1)} %param.6) | copy-start | bytes 5505028
  7.2 182.0 %all-gather.5.cloned.1.call-start = ((), (), s32[]{:S(2)}) async-start(), calls=%async_computation.2 | async-start | bytes 9437184 | tf_op jit(solution)/shard_map/all_gather | solution.py:60
  43.3 11.5 %all-to-all-start.1 = ((f32[8,96,128]{2,1,0:T(8,128)}), f32[8,96,128]{2,1,0:T(8,128)S(1)}, u32[]{:S(2)}, u32[]{:S(2)}) async-start(f32[8,96,128]{2,1,0:T(8,128)} %fusion.3), calls=%async_computation.1 | async-start | bytes 786432 | tf_op jit(solution)/shard_map/all_to_all | solution.py:75
  196.6 2.7 collective-permute-start
  199.6 10.4 %collective-permute-start.1 = (f32[2,2,2,3,32,128]{5,4,3,2,1,0:T(8,128)S(1)}, f32[2,2,2,3,32,128]{5,4,3,2,1,0:T(8,128)S(1)}, u32[]{:S(2)}, u32[]{:S(2)}) collective-permute-start(f32[2,2,2,3,32,128]{5,4,3,2,1,0:T(8,128)S(1)} %dynamic-slice_bitcast_fusion), channel_id=1, source_target_pairs={{0,32},{8,40},{16,48},{24,56},{32,0},{40,8},{48,16},{56,24},{64,96... | collective-permute-start | bytes 1179656 | tf_op jit(solution)/shard_map/ppermute | solution.py:32
  210.1 25.2 %collective-permute-start.2 = (f32[2,2,3,32,128]{4,3,2,1,0:T(8,128)S(1)}, f32[2,2,3,32,128]{4,3,2,1,0:T(8,128)S(1)}, u32[]{:S(2)}, u32[]{:S(2)}) collective-permute-start(f32[2,2,3,32,128]{4,3,2,1,0:T(8,128)S(1)} %dynamic-slice_bitcast_fusion.1), channel_id=1, source_target_pairs={{0,64},{8,72},{16,80},{24,88},{32,96},{40,104},{48,112},{56,120},{... | collective-permute-start | bytes 589832 | tf_op jit(solution)/shard_map/ppermute | solution.py:32
  226.9 27.0 %copy-start.3 = (f32[1,3,32,128]{3,2,1,0:T(8,128)S(1)}, f32[1,3,32,128]{3,2,1,0:T(8,128)}, u32[]{:S(2)}) copy-start(f32[1,3,32,128]{3,2,1,0:T(8,128)} %param.10) | copy-start | bytes 147460
  226.9 27.0 %copy-start = (bf16[3,32,896]{2,1,0:T(8,128)(2,1)S(1)}, bf16[3,32,896]{2,1,0:T(8,128)(2,1)}, u32[]{:S(2)}) copy-start(bf16[3,32,896]{2,1,0:T(8,128)(2,1)} %param.9) | copy-start | bytes 516100
  226.9 27.0 %copy-start.2 = (f32[1,3,32,128]{3,2,1,0:T(8,128)S(1)}, f32[1,3,32,128]{3,2,1,0:T(8,128)}, u32[]{:S(2)}) copy-start(f32[1,3,32,128]{3,2,1,0:T(8,128)} %param.11) | copy-start | bytes 147460
  226.9 34.3 %all-to-all-start = ((bf16[8,128,896]{2,1,0:T(8,128)(2,1)}), bf16[8,128,896]{2,1,0:T(8,128)(2,1)S(1)}, u32[]{:S(2)}, u32[]{:S(2)}) async-start(bf16[8,128,896]{2,1,0:T(8,128)(2,1)} %fusion.6), calls=%async_computation | async-start | bytes 3670016 | tf_op jit(solution)/shard_map/all_to_all | solution.py:64
  235.4 7.5 %collective-permute-start.3 = (f32[2,3,32,128]{3,2,1,0:T(8,128)S(1)}, f32[2,3,32,128]{3,2,1,0:T(8,128)S(1)}, u32[]{:S(2)}, u32[]{:S(2)}) collective-permute-start(f32[2,3,32,128]{3,2,1,0:T(8,128)S(1)} %dynamic-slice_bitcast_fusion.2), channel_id=1, source_target_pairs={{0,128},{8,136},{16,144},{24,152},{32,160},{40,168},{48,176},{56,1... | collective-permute-start | bytes 294920 | tf_op jit(solution)/shard_map/ppermute | solution.py:32
  243.0 10.9 %collective-permute-start.4 = (f32[3,32,128]{2,1,0:T(8,128)S(1)}, f32[3,32,128]{2,1,0:T(8,128)S(1)}, u32[]{:S(2)}, u32[]{:S(2)}) collective-permute-start(f32[3,32,128]{2,1,0:T(8,128)S(1)} %dynamic-slice_bitcast_fusion.3), channel_id=1, source_target_pairs={{0,16},{8,24},{16,0},{24,8},{32,48},{40,56},{48,32},{56,40},{64,80... | collective-permute-start | bytes 147464 | tf_op jit(solution)/shard_map/ppermute | solution.py:32
  253.9 9.7 %copy-start.1 = (f32[1,3,32,128]{3,2,1,0:T(8,128)}, f32[1,3,32,128]{3,2,1,0:T(8,128)S(1)}, u32[]{:S(2)}) copy-start(f32[1,3,32,128]{3,2,1,0:T(8,128)S(1)} %bitcast_add_fusion.3) | copy-start | bytes 147460
Sparse Core Ops, SparseCore 0:
  9.8 179.3 all-gather.4

commit v4 on v3

--- a/solution.py
+++ b/solution.py
@@ -59,12 +59,11 @@
 
     gathered = lax.all_gather(grad_out, "fsdp", axis=0, tiled=False)
     partial_grads = jnp.einsum(
-        "ptd,hd->pth", gathered, down_weight, preferred_element_type=jnp.float32
+        "ptd,hd->tph", gathered, down_weight, preferred_element_type=jnp.float32
     ).astype(jnp.bfloat16)
     grad_hidden = lax.all_to_all(
-        partial_grads.reshape(shards * tok_rows, shard_rows), "fsdp",
-        split_axis=0, concat_axis=1, tiled=True,
-    )
+        partial_grads, "fsdp", split_axis=1, concat_axis=1, tiled=True
+    ).reshape(tok_rows, shards * shard_rows)
 
     projected = jnp.einsum(
         "fki,tfi->fkt",
@@ -78,9 +77,11 @@
         pieces, gathered.reshape(shards * tok_rows, model_width), preferred_element_type=jnp.float32
     ).reshape(3, sketch_rows, replicas, columns)
     summed = (products[0] + products[1] + products[2]).transpose(1, 0, 2)
-    sketch_table = halving_scatter(
-        (summed * table_scale).reshape(replicas, rows_count, buckets, columns), replicas
+    arrived = lax.all_to_all(
+        (summed * table_scale).reshape(replicas, rows_count, buckets, columns),
+        "rep", split_axis=0, concat_axis=0, tiled=True,
     )
+    sketch_table = jnp.sum(arrived, axis=0, keepdims=True)
     new_momentum = momentum_decay * momentum + sketch_table
     accumulated = error + step_size * new_momentum
     update = (

time: 275 us -> 298 us (1.084)
  waiting for transfers between devices: 169 us -> 197 us
  local copies, waits for them, and re-layouts: 9.81 us -> 6.53 us
    all_to_all x1 -> x2, waiting for transfers between devices: 4.86 us -> 55.2 us  [the longest x1 36.3 us: on_device(): lax.all_to_all((summed * table_scale).reshape(replicas, rows_count, bucke...]
    ppermute x5 -> x0, waiting for transfers between devices: 23 us -> none  [halving_scatter(): data = keep + lax.ppermute(send, 'rep', pairs)]
    all_to_all x1 -> x2, starting transfers between devices: 8.44 us -> 19.3 us  [the longest x1 10.9 us: on_device(): lax.all_to_all((summed * table_scale).reshape(replicas, rows_count, bucke...]
    ppermute x5 -> x0, starting transfers between devices: 10.9 us -> none  [halving_scatter(): data = keep + lax.ppermute(send, 'rep', pairs)]
    all_gather x1, waiting for transfers between devices: 134 us -> 141 us  [on_device(): gathered = lax.all_gather(grad_out, 'fsdp', axis=0, tiled=False)]
    all_to_all x1, waiting for transfers between devices: 6.37 us -> 0.01 us  [on_device(): lax.all_to_all(projected, 'fsdp', split_axis=0, concat_axis=0, tiled=True)]
  transfers between devices with their start and end apart: 8 -> 4, of which waited for: 7 -> 3; matrix products, arithmetic and copies ran while one was open for 7% -> 9% of each run, Pallas kernels for 0% -> 0%
where the time goes in v4:
time: 298 us; the launch traced here: 297 us
  waiting for transfers between devices  197 us (66%)
  blocking collectives  32.3 us (11%)
  starting transfers between devices  24.5 us (8%)
  matrix products  21.2 us (7%)
  between operations  14.2 us (5%)
  local copies, waits for them, and re-layouts  6.53 us (2%)
    all_gather x1, waiting for transfers between devices, on_device(): gathered = lax.all_gather(grad_out, 'fsdp', axis=0, tiled=False)  141 us
    all_to_all x1, waiting for transfers between devices, on_device(): lax.all_to_all((summed * table_scale).reshape(replicas, rows_count, bucke...  36.3 us
    all_gather x1, blocking collectives, on_device(): lax.all_gather(code, 'fsdp', axis=0, tiled=False).astype(jnp.float32)  32.3 us
    all_to_all x1, waiting for transfers between devices, on_device(): lax.all_to_all(partial_grads, 'fsdp', split_axis=1, concat_axis=1, tiled=...  18.9 us
    dot_general x1, matrix products, on_device(): jnp.einsum('ptd,hd->tph', gathered, down_weight, preferred_element_type=j...  13.3 us
    all_to_all x1, starting transfers between devices, on_device(): lax.all_to_all((summed * table_scale).reshape(replicas, rows_count, bucke...  10.9 us
    all_to_all x1, starting transfers between devices, on_device(): lax.all_to_all(partial_grads, 'fsdp', split_axis=1, concat_axis=1, tiled=...  8.48 us
  transfers between devices with their start and end apart: 4, of which 3 were waited for; matrix products, arithmetic and copies ran while one was open for 9% of the time, Pallas kernels for 0%

profile of v4, /device:TPU:1, one launch (start us, length us, event | category | flops | bytes accessed | tf_op | source)
XLA Modules:
  0.0 297.4 jit_solution(3911863308651569925)
XLA Ops:
  7.2 0.0 all-gather.5.cloned.1.call-start
  7.2 0.7 all-gather.5.cloned.1.call-update
  7.9 0.1 eq.23
  8.0 1.0 multiply_reduce_fusion
  9.1 32.3 %all-gather.2 = bf16[8,3,896]{2,1,0:T(4,128)(2,1)S(1)} all-gather(bf16[1,3,896]{2,1,0:T(4,128)(2,1)S(1)} %bitcast.72), channel_id=3, replica_groups=mesh['rep'=32,'fsdp'=8] {'fsdp'}, dimensions={0}, use_global_device_ids=true | all-gather | bytes 48384 | tf_op jit(solution)/shard_map/all_gather | solution.py:53
  41.5 0.3 fusion.2
  41.8 0.0 copy-done.4
  41.8 1.5 fusion.3
  43.3 5.1 %all-to-all-start.1 = ((f32[8,96,128]{2,1,0:T(8,128)}), f32[8,96,128]{2,1,0:T(8,128)S(1)}, u32[]{:S(2)}, u32[]{:S(2)}) async-start(f32[8,96,128]{2,1,0:T(8,128)} %fusion.3), calls=%async_computation.1 | async-start | bytes 786432 | tf_op jit(solution)/shard_map/all_to_all | solution.py:74
  48.4 140.8 %all-gather.5.cloned.1.call-done = bf16[1024,4096]{1,0:T(8,128)(2,1)} async-done(((bf16[128,4096]{1,0:T(8,128)(2,1)}), bf16[1024,4096]{1,0:T(8,128)(2,1)}) %all-gather.5.cloned.1.call-update) | async-done | bytes 8388624 | tf_op jit(solution)/shard_map/all_gather | solution.py:60
  189.2 13.3 %convert_bitcast_fusion = bf16[128,8,896]{0,2,1:T(8,128)(2,1)} fusion(bf16[8,128,4096]{2,1,0:T(8,128)(2,1)} %bitcast.67, bf16[896,4096]{1,0:T(8,128)(2,1)} %param.8), kind=kOutput, calls=%fused_computation.8 | convolution fusion | flops 7517110272 | bytes 17563648 | tf_op jit(solution)/shard_map/ptd,hd->tph/dot_general | solution.py:61
  202.5 0.0 all-to-all-done.1
  202.5 8.5 %all-to-all-start = ((bf16[128,8,896]{0,2,1:T(8,128)(2,1)}), bf16[128,8,896]{0,2,1:T(8,128)(2,1)S(1)}, u32[]{:S(2)}, u32[]{:S(2)}) async-start(bf16[128,8,896]{0,2,1:T(8,128)(2,1)} %convert_bitcast_fusion), calls=%async_computation | async-start | bytes 3670016 | tf_op jit(solution)/shard_map/all_to_all | solution.py:64
  210.9 0.1 fusion.18
  211.1 0.1 maximum_bitcast_fusion
  211.1 0.2 copy.18
  211.4 5.0 %fusion.12 = f32[288,4096]{1,0:T(8,128)S(1)} fusion(bf16[1024,4096]{1,0:T(8,128)(2,1)} %all-gather.5.cloned.1.call-done, bf16[36,8,8,128]{3,2,1,0:T(8,128)(2,1)S(1)} %bitcast.71), kind=kOutput, calls=%fused_computation.17 | convolution fusion | flops 2415919104 | bytes 13697024 | tf_op jit(solution)/shard_map/dot_general | solution.py:76
  216.4 0.3 fusion.9
  216.6 0.3 copy.24
  216.9 2.1 copy.19
  219.0 18.9 %all-to-all-done = bf16[128,8,896]{0,2,1:T(8,128)(2,1)S(1)} async-done(((bf16[128,8,896]{0,2,1:T(8,128)(2,1)}), bf16[128,8,896]{0,2,1:T(8,128)(2,1)S(1)}, u32[]{:S(2)}, u32[]{:S(2)}) %all-to-all-start) | async-done | bytes 1835040 | tf_op jit(solution)/shard_map/all_to_all | solution.py:64
  237.9 10.9 %all-to-all-start.2 = ((f32[32,3,32,128]{3,2,1,0:T(8,128)}), f32[32,3,32,128]{3,2,1,0:T(8,128)S(1)}, u32[]{:S(2)}, u32[]{:S(2)}) async-start(f32[32,3,32,128]{3,2,1,0:T(8,128)} %bitcast.12), calls=%async_computation.2 | async-start | bytes 3145728 | tf_op jit(solution)/shard_map/all_to_all | solution.py:80
  248.8 0.0 copy-start.3
  248.8 0.0 copy-start.2
  248.8 2.9 copy.20
  251.7 36.3 %all-to-all-done.2 = f32[32,3,32,128]{3,2,1,0:T(8,128)S(1)} async-done(((f32[32,3,32,128]{3,2,1,0:T(8,128)}), f32[32,3,32,128]{3,2,1,0:T(8,128)S(1)}, u32[]{:S(2)}, u32[]{:S(2)}) %all-to-all-start.2) | async-done | bytes 1572896 | tf_op jit(solution)/shard_map/all_to_all | solution.py:80
  287.9 0.1 reduce_sum.19
  288.1 0.0 copy-done.3
  288.1 0.0 copy-start.1
  288.1 0.4 fusion.10
  288.5 1.0 fusion.11
  289.6 1.0 copy.21
  (10 shorter events, 0.1 us)
Async XLA Ops:
  7.2 34.6 %copy-start.4 = (bf16[128,7168]{1,0:T(8,128)(2,1)S(1)}, bf16[128,7168]{1,0:T(8,128)(2,1)}, u32[]{:S(2)}) copy-start(bf16[128,7168]{1,0:T(8,128)(2,1)} %param.6) | copy-start | bytes 5505028
  7.2 182.0 %all-gather.5.cloned.1.call-start = ((), (), s32[]{:S(2)}) async-start(), calls=%async_computation.3 | async-start | bytes 9437184 | tf_op jit(solution)/shard_map/all_gather | solution.py:60
  43.3 159.1 %all-to-all-start.1 = ((f32[8,96,128]{2,1,0:T(8,128)}), f32[8,96,128]{2,1,0:T(8,128)S(1)}, u32[]{:S(2)}, u32[]{:S(2)}) async-start(f32[8,96,128]{2,1,0:T(8,128)} %fusion.3), calls=%async_computation.1 | async-start | bytes 786432 | tf_op jit(solution)/shard_map/all_to_all | solution.py:74
  202.5 35.4 %all-to-all-start = ((bf16[128,8,896]{0,2,1:T(8,128)(2,1)}), bf16[128,8,896]{0,2,1:T(8,128)(2,1)S(1)}, u32[]{:S(2)}, u32[]{:S(2)}) async-start(bf16[128,8,896]{0,2,1:T(8,128)(2,1)} %convert_bitcast_fusion), calls=%async_computation | async-start | bytes 3670016 | tf_op jit(solution)/shard_map/all_to_all | solution.py:64
  237.9 50.1 %all-to-all-start.2 = ((f32[32,3,32,128]{3,2,1,0:T(8,128)}), f32[32,3,32,128]{3,2,1,0:T(8,128)S(1)}, u32[]{:S(2)}, u32[]{:S(2)}) async-start(f32[32,3,32,128]{3,2,1,0:T(8,128)} %bitcast.12), calls=%async_computation.2 | async-start | bytes 3145728 | tf_op jit(solution)/shard_map/all_to_all | solution.py:80
  248.8 39.3 %copy-start.3 = (f32[1,3,32,128]{3,2,1,0:T(8,128)S(1)}, f32[1,3,32,128]{3,2,1,0:T(8,128)}, u32[]{:S(2)}) copy-start(f32[1,3,32,128]{3,2,1,0:T(8,128)} %param.10) | copy-start | bytes 147460
  248.8 39.3 %copy-start.2 = (f32[1,3,32,128]{3,2,1,0:T(8,128)S(1)}, f32[1,3,32,128]{3,2,1,0:T(8,128)}, u32[]{:S(2)}) copy-start(f32[1,3,32,128]{3,2,1,0:T(8,128)} %param.11) | copy-start | bytes 147460
  251.7 36.4 %copy-start = (bf16[3,32,896]{2,1,0:T(8,128)(2,1)S(1)}, bf16[3,32,896]{2,1,0:T(8,128)(2,1)}, u32[]{:S(2)}) copy-start(bf16[3,32,896]{2,1,0:T(8,128)(2,1)} %param.9) | copy-start | bytes 516100
  288.1 2.4 copy-start.1
Sparse Core Ops, SparseCore 0:
  9.8 179.3 all-gather.4

commit v5 on v3

--- a/solution.py
+++ b/solution.py
@@ -47,17 +47,18 @@
     total_tokens = tok_rows * shards * replicas
     table_scale = math.sqrt(buckets / (shard_rows * total_tokens))
 
-    levels = jnp.arange(1, buckets + 1, dtype=jnp.float32)
     hash_float = hash_tiles.astype(jnp.float32)
-    code = jnp.sum(hash_float * levels[None, :, None], axis=1).astype(jnp.bfloat16)
-    all_code = lax.all_gather(code, "fsdp", axis=0, tiled=False).astype(jnp.float32)
-    magnitude = jnp.abs(all_code)
-    sign = jnp.where(all_code > 0, 1.0, -1.0)
-    all_hash = jnp.where(
-        magnitude[:, :, None, :] == levels[None, None, :, None], sign[:, :, None, :], 0.0
-    ).astype(jnp.bfloat16)
 
-    gathered = lax.all_gather(grad_out, "fsdp", axis=0, tiled=False)
+    outgoing = jnp.concatenate(
+        [
+            jnp.broadcast_to(grad_out[None], (shards, tok_rows, model_width)),
+            hidden.reshape(tok_rows, shards, shard_rows).transpose(1, 0, 2),
+        ],
+        axis=2,
+    )
+    arrived = lax.all_to_all(outgoing, "fsdp", split_axis=0, concat_axis=0, tiled=True)
+    gathered = arrived[:, :, :model_width]
+    hidden_cols = arrived[:, :, model_width:]
     partial_grads = jnp.einsum(
         "ptd,hd->pth", gathered, down_weight, preferred_element_type=jnp.float32
     ).astype(jnp.bfloat16)
@@ -67,13 +68,12 @@
     )
 
     projected = jnp.einsum(
-        "fki,tfi->fkt",
-        all_hash.reshape(shards, sketch_rows, shard_rows),
-        hidden.reshape(tok_rows, shards, shard_rows),
+        "ki,pti->kpt",
+        hash_tiles.reshape(sketch_rows, shard_rows),
+        hidden_cols,
         preferred_element_type=jnp.float32,
-    )
-    received = lax.all_to_all(projected, "fsdp", split_axis=0, concat_axis=0, tiled=True)
-    pieces = split3(received).transpose(0, 2, 1, 3).reshape(3 * sketch_rows, shards * tok_rows)
+    ).reshape(sketch_rows, shards * tok_rows)
+    pieces = split3(projected).reshape(3 * sketch_rows, shards * tok_rows)
     products = jnp.dot(
         pieces, gathered.reshape(shards * tok_rows, model_width), preferred_element_type=jnp.float32
     ).reshape(3, sketch_rows, replicas, columns)

time: 275 us -> 249 us (0.905)
  blocking collectives: 32.3 us -> 0 us
  local copies, waits for them, and re-layouts: 9.81 us -> 25.7 us
  between operations: 14.2 us -> 0.85 us
  other arithmetic: 2.27 us -> 7.64 us
  waiting for transfers between devices: 169 us -> 166 us
    all_gather x1 -> x0, waiting for transfers between devices: 134 us -> none  [on_device(): gathered = lax.all_gather(grad_out, 'fsdp', axis=0, tiled=False)]
    all_to_all x1, waiting for transfers between devices: 6.37 us -> 139 us  [on_device(): lax.all_to_all(outgoing, 'fsdp', split_axis=0, concat_axis=0, tiled=True)]
    all_gather x1 -> x0, blocking collectives: 32.3 us -> none  [on_device(): lax.all_gather(code, 'fsdp', axis=0, tiled=False).astype(jnp.float32)]
    slice x0 -> x1, local copies, waits for them, and re-layouts: none -> 7.83 us  [on_device(): gathered = arrived[:, :, :model_width]]
    concatenate x0 -> x1, other arithmetic: none -> 6.83 us  [on_device(): jnp.concatenate([jnp.broadcast_to(grad_out[None], (shards, tok_rows, mode...]
    all_to_all x1, starting transfers between devices: 8.44 us -> 3.72 us  [on_device(): lax.all_to_all(partial_grads.reshape(shards * tok_rows, shard_rows), 'fsd...]
    ppermute x5, starting transfers between devices: 10.9 us -> 15.2 us  [halving_scatter(): data = keep + lax.ppermute(send, 'rep', pairs)]
    unnamed x14 -> x15, local copies, waits for them, and re-layouts: 5.4 us -> 9.37 us
  transfers between devices with their start and end apart: 8 -> 7, of which waited for: 7 -> 6; matrix products, arithmetic and copies ran while one was open for 7% -> 7% of each run, Pallas kernels for 0% -> 0%
where the time goes in v5:
time: 249 us; the launch traced here: 248 us
  waiting for transfers between devices  166 us (67%)
  local copies, waits for them, and re-layouts  25.7 us (10%)
  starting transfers between devices  24.8 us (10%)
  matrix products  23 us (9%)
  other arithmetic  7.64 us (3%)
    all_to_all x1, waiting for transfers between devices, on_device(): lax.all_to_all(outgoing, 'fsdp', split_axis=0, concat_axis=0, tiled=True)  139 us
    ppermute x5, waiting for transfers between devices, halving_scatter(): data = keep + lax.ppermute(send, 'rep', pairs)  22 us
    ppermute x5, starting transfers between devices, halving_scatter(): data = keep + lax.ppermute(send, 'rep', pairs)  15.2 us
    dot_general x1, matrix products, on_device(): jnp.einsum('ptd,hd->pth', gathered, down_weight, preferred_element_type=j...  14.4 us
    unnamed x15, local copies, waits for them, and re-layouts  9.37 us
    slice x1, local copies, waits for them, and re-layouts, on_device(): gathered = arrived[:, :, :model_width]  7.83 us
    concatenate x1, other arithmetic, on_device(): jnp.concatenate([jnp.broadcast_to(grad_out[None], (shards, tok_rows, mode...  6.83 us
    all_to_all x1, starting transfers between devices, on_device(): lax.all_to_all(outgoing, 'fsdp', split_axis=0, concat_axis=0, tiled=True)  5.86 us
  transfers between devices with their start and end apart: 7, of which 6 were waited for; matrix products, arithmetic and copies ran while one was open for 7% of the time, Pallas kernels for 0%

profile of v5, /device:TPU:1, one launch (start us, length us, event | category | flops | bytes accessed | tf_op | source)
XLA Modules:
  0.0 247.8 jit_solution(6708327427317936273)
XLA Ops:
  0.7 4.0 %copy.11 = bf16[128,7168]{0,1:T(8,128)(2,1)} copy(bf16[128,7168]{1,0:T(8,128)(2,1)} %param.6) | data formatting | bytes 3670016 | tf_op args[0]
  4.6 3.1 %copy.12 = bf16[128,8,896]{2,0,1:T(8,128)(2,1)S(1)} copy(bf16[128,8,896]{0,2,1:T(8,128)(2,1)} %bitcast.77) | data formatting | bytes 3670016 | tf_op jit(solution)/shard_map/reshape | solution.py:55
  7.7 1.0 broadcast_in_dim.4
  8.7 6.8 %pad_maximum_fusion = bf16[8,128,4992]{2,1,0:T(8,128)(2,1)} fusion(bf16[8,128,896]{2,1,0:T(8,128)(2,1)S(1)} %bitcast.74, bf16[8,128,4096]{2,1,0:T(8,128)(2,1)S(1)} %broadcast_in_dim.4), kind=kLoop, calls=%fused_computation | loop fusion | flops 20447232 | bytes 20447232 | tf_op jit(solution)/shard_map/concatenate | solution.py:52
  15.6 5.9 %all-to-all-start = ((bf16[8,128,4992]{2,1,0:T(8,128)(2,1)}), bf16[8,128,4992]{2,1,0:T(8,128)(2,1)}, u32[]{:S(2)}, u32[]{:S(2)}) async-start(bf16[8,128,4992]{2,1,0:T(8,128)(2,1)} %pad_maximum_fusion), calls=%async_computation | async-start | bytes 20447232 | tf_op jit(solution)/shard_map/all_to_all | solution.py:59
  21.4 139.0 %all-to-all-done = bf16[8,128,4992]{2,1,0:T(8,128)(2,1)} async-done(((bf16[8,128,4992]{2,1,0:T(8,128)(2,1)}), bf16[8,128,4992]{2,1,0:T(8,128)(2,1)}, u32[]{:S(2)}, u32[]{:S(2)}) %all-to-all-start) | async-done | bytes 10223648 | tf_op jit(solution)/shard_map/all_to_all | solution.py:59
  160.4 2.2 fusion.10
  162.6 0.2 copy.14
  163.1 7.8 %slice.23 = bf16[8,128,4096]{2,1,0:T(8,128)(2,1)} slice(bf16[8,128,4992]{2,1,0:T(8,128)(2,1)} %all-to-all-done), slice={[0:8], [0:128], [0:4096]} | slice | bytes 16777216 | tf_op jit(solution)/shard_map/slice | solution.py:60
  170.9 5.0 %fusion.20 = f32[288,4096]{1,0:T(8,128)S(1)} fusion(bf16[288,1024]{1,0:T(8,128)(2,1)S(1)} %bitcast.81, bf16[1024,4096]{1,0:T(8,128)(2,1)} %bitcast.73), kind=kOutput, calls=%fused_computation.40 | convolution fusion | flops 2415919104 | bytes 13697024 | tf_op jit(solution)/shard_map/dot_general | solution.py:77
  175.9 0.3 fusion.8
  176.2 0.3 copy.21
  176.4 1.6 constant_dynamic-slice_fusion.1
  178.1 0.3 copy.26
  178.3 2.4 collective-permute-start
  180.8 1.9 collective-permute-done
  182.7 0.3 fusion.14
  183.0 1.8 collective-permute-start.1
  184.8 9.1 %collective-permute-done.1 = f32[2,2,2,3,32,128]{5,4,3,2,1,0:T(8,128)S(1)} collective-permute-done((f32[2,2,2,3,32,128]{5,4,3,2,1,0:T(8,128)S(1)}, f32[2,2,2,3,32,128]{5,4,3,2,1,0:T(8,128)S(1)}, u32[]{:S(2)}, u32[]{:S(2)}) %collective-permute-start.1) | collective-permute-done | bytes 393248 | tf_op jit(solution)/shard_map/ppermute | solution.py:32
  194.0 3.2 %collective-permute-start.2 = (f32[2,2,3,32,128]{4,3,2,1,0:T(8,128)S(1)}, f32[2,2,3,32,128]{4,3,2,1,0:T(8,128)S(1)}, u32[]{:S(2)}, u32[]{:S(2)}) collective-permute-start(f32[2,2,3,32,128]{4,3,2,1,0:T(8,128)S(1)} %dynamic-slice_bitcast_fusion.1), channel_id=1, source_target_pairs={{0,64},{8,72},{16,80},{24,88},{32,96},{40,104},{48,112},{56,120},{... | collective-permute-start | bytes 589832 | tf_op jit(solution)/shard_map/ppermute | solution.py:32
  197.2 14.4 %fusion.4 = bf16[8,128,896]{2,1,0:T(8,128)(2,1)} fusion(bf16[896,4096]{1,0:T(8,128)(2,1)} %param.8, bf16[8,128,4992]{2,1,0:T(8,128)(2,1)} %all-to-all-done), kind=kOutput, calls=%fused_computation.5 | convolution fusion | flops 7517110272 | bytes 17563648 | tf_op jit(solution)/shard_map/ptd,hd->pth/dot_general | solution.py:62
  211.5 3.7 %all-to-all-start.1 = ((bf16[8,128,896]{2,1,0:T(8,128)(2,1)}), bf16[8,128,896]{2,1,0:T(8,128)(2,1)S(1)}, u32[]{:S(2)}, u32[]{:S(2)}) async-start(bf16[8,128,896]{2,1,0:T(8,128)(2,1)} %fusion.4), calls=%async_computation.1 | async-start | bytes 3670016 | tf_op jit(solution)/shard_map/all_to_all | solution.py:65
  215.4 4.8 %collective-permute-start.3 = (f32[2,3,32,128]{3,2,1,0:T(8,128)S(1)}, f32[2,3,32,128]{3,2,1,0:T(8,128)S(1)}, u32[]{:S(2)}, u32[]{:S(2)}) collective-permute-start(f32[2,3,32,128]{3,2,1,0:T(8,128)S(1)} %dynamic-slice_bitcast_fusion.2), channel_id=1, source_target_pairs={{0,128},{8,136},{16,144},{24,152},{32,160},{40,168},{48,176},{56,1... | collective-permute-start | bytes 294920 | tf_op jit(solution)/shard_map/ppermute | solution.py:32
  220.2 2.7 %collective-permute-done.3 = f32[2,3,32,128]{3,2,1,0:T(8,128)S(1)} collective-permute-done((f32[2,3,32,128]{3,2,1,0:T(8,128)S(1)}, f32[2,3,32,128]{3,2,1,0:T(8,128)S(1)}, u32[]{:S(2)}, u32[]{:S(2)}) %collective-permute-start.3) | collective-permute-done | bytes 98336 | tf_op jit(solution)/shard_map/ppermute | solution.py:32
  223.0 3.0 %collective-permute-start.4 = (f32[3,32,128]{2,1,0:T(8,128)S(1)}, f32[3,32,128]{2,1,0:T(8,128)S(1)}, u32[]{:S(2)}, u32[]{:S(2)}) collective-permute-start(f32[3,32,128]{2,1,0:T(8,128)S(1)} %dynamic-slice_bitcast_fusion.3), channel_id=1, source_target_pairs={{0,16},{8,24},{16,0},{24,8},{32,48},{40,56},{48,32},{56,40},{64,80... | collective-permute-start | bytes 147464 | tf_op jit(solution)/shard_map/ppermute | solution.py:32
  225.9 8.2 %collective-permute-done.4 = f32[3,32,128]{2,1,0:T(8,128)S(1)} collective-permute-done((f32[3,32,128]{2,1,0:T(8,128)S(1)}, f32[3,32,128]{2,1,0:T(8,128)S(1)}, u32[]{:S(2)}, u32[]{:S(2)}) %collective-permute-start.4) | collective-permute-done | bytes 49184 | tf_op jit(solution)/shard_map/ppermute | solution.py:32
  234.2 0.4 fusion.9
  234.6 1.0 copy.18
  235.6 1.0 fusion.13
  236.6 4.9 %all-to-all-done.1 = bf16[8,128,896]{2,1,0:T(8,128)(2,1)S(1)} async-done(((bf16[8,128,896]{2,1,0:T(8,128)(2,1)}), bf16[8,128,896]{2,1,0:T(8,128)(2,1)S(1)}, u32[]{:S(2)}, u32[]{:S(2)}) %all-to-all-start.1) | async-done | bytes 1835040 | tf_op jit(solution)/shard_map/all_to_all | solution.py:65
  241.5 2.4 copy.13
  244.0 3.9 %copy.17 = bf16[128,7168]{1,0:T(8,128)(2,1)} copy(bf16[128,7168]{0,1:T(8,128)(2,1)} %bitcast.76) | data formatting | bytes 3670016
  (22 shorter events, 0.5 us)
Async XLA Ops:
  0.6 159.8 %copy-start = (bf16[3,32,896]{2,1,0:T(8,128)(2,1)S(1)}, bf16[3,32,896]{2,1,0:T(8,128)(2,1)}, u32[]{:S(2)}) copy-start(bf16[3,32,896]{2,1,0:T(8,128)(2,1)} %param.9) | copy-start | bytes 516100
  0.6 7.0 %copy-start.1 = (bf16[128,4096]{1,0:T(8,128)(2,1)S(1)}, bf16[128,4096]{1,0:T(8,128)(2,1)}, u32[]{:S(2)}) copy-start(bf16[128,4096]{1,0:T(8,128)(2,1)} %param.7) | copy-start | bytes 3145732
  15.6 144.8 %all-to-all-start = ((bf16[8,128,4992]{2,1,0:T(8,128)(2,1)}), bf16[8,128,4992]{2,1,0:T(8,128)(2,1)}, u32[]{:S(2)}, u32[]{:S(2)}) async-start(bf16[8,128,4992]{2,1,0:T(8,128)(2,1)} %pad_maximum_fusion), calls=%async_computation | async-start | bytes 20447232 | tf_op jit(solution)/shard_map/all_to_all | solution.py:59
  178.3 4.4 %collective-permute-start = (f32[2,2,2,2,3,32,128]{6,5,4,3,1,0,2:T(8,128)S(1)}, f32[2,2,2,2,3,32,128]{6,5,4,3,1,0,2:T(8,128)S(1)}, u32[]{:S(2)}, u32[]{:S(2)}) collective-permute-start(f32[2,2,2,2,3,32,128]{6,5,4,3,1,0,2:T(8,128)S(1)} %bitcast.80), channel_id=1, source_target_pairs={{0,8},{8,0},{16,24},{24,16},{32,40},{40,32},{48,56},{56,48},{64,72... | collective-permute-start | bytes 2359304 | tf_op jit(solution)/shard_map/ppermute | solution.py:32
  183.0 10.9 %collective-permute-start.1 = (f32[2,2,2,3,32,128]{5,4,3,2,1,0:T(8,128)S(1)}, f32[2,2,2,3,32,128]{5,4,3,2,1,0:T(8,128)S(1)}, u32[]{:S(2)}, u32[]{:S(2)}) collective-permute-start(f32[2,2,2,3,32,128]{5,4,3,2,1,0:T(8,128)S(1)} %dynamic-slice_bitcast_fusion), channel_id=1, source_target_pairs={{0,32},{8,40},{16,48},{24,56},{32,0},{40,8},{48,16},{56,24},{64,96... | collective-permute-start | bytes 1179656 | tf_op jit(solution)/shard_map/ppermute | solution.py:32
  194.0 21.3 %collective-permute-start.2 = (f32[2,2,3,32,128]{4,3,2,1,0:T(8,128)S(1)}, f32[2,2,3,32,128]{4,3,2,1,0:T(8,128)S(1)}, u32[]{:S(2)}, u32[]{:S(2)}) collective-permute-start(f32[2,2,3,32,128]{4,3,2,1,0:T(8,128)S(1)} %dynamic-slice_bitcast_fusion.1), channel_id=1, source_target_pairs={{0,64},{8,72},{16,80},{24,88},{32,96},{40,104},{48,112},{56,120},{... | collective-permute-start | bytes 589832 | tf_op jit(solution)/shard_map/ppermute | solution.py:32
  211.5 22.6 %copy-start.4 = (f32[1,3,32,128]{3,2,1,0:T(8,128)S(1)}, f32[1,3,32,128]{3,2,1,0:T(8,128)}, u32[]{:S(2)}) copy-start(f32[1,3,32,128]{3,2,1,0:T(8,128)} %param.10) | copy-start | bytes 147460
  211.5 22.6 %copy-start.3 = (f32[1,3,32,128]{3,2,1,0:T(8,128)S(1)}, f32[1,3,32,128]{3,2,1,0:T(8,128)}, u32[]{:S(2)}) copy-start(f32[1,3,32,128]{3,2,1,0:T(8,128)} %param.11) | copy-start | bytes 147460
  211.5 30.0 %all-to-all-start.1 = ((bf16[8,128,896]{2,1,0:T(8,128)(2,1)}), bf16[8,128,896]{2,1,0:T(8,128)(2,1)S(1)}, u32[]{:S(2)}, u32[]{:S(2)}) async-start(bf16[8,128,896]{2,1,0:T(8,128)(2,1)} %fusion.4), calls=%async_computation.1 | async-start | bytes 3670016 | tf_op jit(solution)/shard_map/all_to_all | solution.py:65
  215.4 7.6 %collective-permute-start.3 = (f32[2,3,32,128]{3,2,1,0:T(8,128)S(1)}, f32[2,3,32,128]{3,2,1,0:T(8,128)S(1)}, u32[]{:S(2)}, u32[]{:S(2)}) collective-permute-start(f32[2,3,32,128]{3,2,1,0:T(8,128)S(1)} %dynamic-slice_bitcast_fusion.2), channel_id=1, source_target_pairs={{0,128},{8,136},{16,144},{24,152},{32,160},{40,168},{48,176},{56,1... | collective-permute-start | bytes 294920 | tf_op jit(solution)/shard_map/ppermute | solution.py:32
  223.0 11.2 %collective-permute-start.4 = (f32[3,32,128]{2,1,0:T(8,128)S(1)}, f32[3,32,128]{2,1,0:T(8,128)S(1)}, u32[]{:S(2)}, u32[]{:S(2)}) collective-permute-start(f32[3,32,128]{2,1,0:T(8,128)S(1)} %dynamic-slice_bitcast_fusion.3), channel_id=1, source_target_pairs={{0,16},{8,24},{16,0},{24,8},{32,48},{40,56},{48,32},{56,40},{64,80... | collective-permute-start | bytes 147464 | tf_op jit(solution)/shard_map/ppermute | solution.py:32
  234.2 13.7 %copy-start.2 = (f32[1,3,32,128]{3,2,1,0:T(8,128)}, f32[1,3,32,128]{3,2,1,0:T(8,128)S(1)}, u32[]{:S(2)}) copy-start(f32[1,3,32,128]{3,2,1,0:T(8,128)S(1)} %bitcast_add_fusion.3) | copy-start | bytes 147460

commit v6 on v5

--- a/solution.py
+++ b/solution.py
@@ -17,21 +17,24 @@
     return jnp.stack([hi, mid, lo]).astype(jnp.bfloat16)
 
 
-def halving_scatter(blocks, replicas):
+def grouped_scatter(blocks):
     me = lax.axis_index("rep")
-    nbits = replicas.bit_length() - 1
+    replicas = blocks.shape[0]
+    inner = 4
+    outer = replicas // inner
     rest = blocks.shape[1:]
-    data = blocks.reshape((2,) * nbits + rest)
-    remaining = list(range(nbits - 1, -1, -1))
-    for bit in (0, 2, 3, 4, 1)[:nbits] if nbits == 5 else range(nbits):
-        axis = remaining.index(bit)
-        mine = (me >> bit) & 1
-        keep = lax.dynamic_index_in_dim(data, mine, axis=axis, keepdims=False)
-        send = lax.dynamic_index_in_dim(data, 1 - mine, axis=axis, keepdims=False)
-        pairs = [(j, j ^ (1 << bit)) for j in range(replicas)]
-        data = keep + lax.ppermute(send, "rep", pairs)
-        remaining.pop(axis)
-    return data.reshape((1,) + rest)
+    data = blocks.reshape((outer, inner) + rest)
+    low = me % inner
+    kept = lax.dynamic_index_in_dim(data, low, axis=1, keepdims=False)
+    for mask in range(1, inner):
+        send = lax.dynamic_index_in_dim(data, low ^ mask, axis=1, keepdims=False)
+        kept = kept + lax.ppermute(send, "rep", [(j, j ^ mask) for j in range(replicas)])
+    high = me // inner
+    total = lax.dynamic_index_in_dim(kept, high, axis=0, keepdims=False)
+    for mask in range(1, outer):
+        send = lax.dynamic_index_in_dim(kept, high ^ mask, axis=0, keepdims=False)
+        total = total + lax.ppermute(send, "rep", [(j, j ^ (mask * inner)) for j in range(replicas)])
+    return total[None]
 
 
 def on_device(hidden, grad_out, down_weight, hash_tiles, momentum, error):
@@ -78,8 +81,8 @@
         pieces, gathered.reshape(shards * tok_rows, model_width), preferred_element_type=jnp.float32
     ).reshape(3, sketch_rows, replicas, columns)
     summed = (products[0] + products[1] + products[2]).transpose(1, 0, 2)
-    sketch_table = halving_scatter(
-        (summed * table_scale).reshape(replicas, rows_count, buckets, columns), replicas
+    sketch_table = grouped_scatter(
+        (summed * table_scale).reshape(replicas, rows_count, buckets, columns)
     )
     new_momentum = momentum_decay * momentum + sketch_table
     accumulated = error + step_size * new_momentum

time: 249 us -> 236 us (0.948)
  waiting for transfers between devices: 166 us -> 148 us
  starting transfers between devices: 24.8 us -> 30.4 us
    ppermute x5 -> x10, waiting for transfers between devices: 22 us -> 6.16 us  [the longest x7 5.62 us: grouped_scatter(): lax.ppermute(send, 'rep', [(j, j ^ mask * inner) for j in range(replicas)])]
    ppermute x5 -> x10, starting transfers between devices: 15.2 us -> 20.8 us  [the longest x7 15.1 us: grouped_scatter(): lax.ppermute(send, 'rep', [(j, j ^ mask * inner) for j in range(replicas)])]
    unnamed x15 -> x18, local copies, waits for them, and re-layouts: 9.37 us -> 9.13 us
  transfers between devices with their start and end apart: 7 -> 12, of which waited for: 6 -> 5; matrix products, arithmetic and copies ran while one was open for 7% -> 7% of each run, Pallas kernels for 0% -> 0%
where the time goes in v6:
time: 236 us; the launch traced here: 235 us
  waiting for transfers between devices  148 us (63%)
  starting transfers between devices  30.4 us (13%)
  local copies, waits for them, and re-layouts  26.5 us (11%)
  matrix products  20.8 us (9%)
  other arithmetic  8.65 us (4%)
    all_to_all x1, waiting for transfers between devices, on_device(): lax.all_to_all(outgoing, 'fsdp', split_axis=0, concat_axis=0, tiled=True)  139 us
    ppermute x7, starting transfers between devices, grouped_scatter(): lax.ppermute(send, 'rep', [(j, j ^ mask * inner) for j in range(replicas)])  15.1 us
    dot_general x1, matrix products, on_device(): jnp.einsum('ptd,hd->pth', gathered, down_weight, preferred_element_type=j...  12.2 us
    unnamed x18, local copies, waits for them, and re-layouts  9.13 us
    slice x1, local copies, waits for them, and re-layouts, on_device(): gathered = arrived[:, :, :model_width]  7.83 us
    concatenate x1, other arithmetic, on_device(): jnp.concatenate([jnp.broadcast_to(grad_out[None], (shards, tok_rows, mode...  6.79 us
    all_to_all x1, starting transfers between devices, on_device(): lax.all_to_all(outgoing, 'fsdp', split_axis=0, concat_axis=0, tiled=True)  5.86 us
    ppermute x3, starting transfers between devices, grouped_scatter(): lax.ppermute(send, 'rep', [(j, j ^ mask) for j in range(replicas)])  5.77 us
  transfers between devices with their start and end apart: 12, of which 5 were waited for; matrix products, arithmetic and copies ran while one was open for 7% of the time, Pallas kernels for 0%

profile of v6, /device:TPU:1, one launch (start us, length us, event | category | flops | bytes accessed | tf_op | source)
XLA Modules:
  0.0 235.0 jit_solution(9050226875798304066)
XLA Ops:
  0.7 4.0 %copy.15 = bf16[128,7168]{0,1:T(8,128)(2,1)} copy(bf16[128,7168]{1,0:T(8,128)(2,1)} %param.6) | data formatting | bytes 3670016 | tf_op args[0]
  4.6 3.1 %copy.16 = bf16[128,8,896]{2,0,1:T(8,128)(2,1)S(1)} copy(bf16[128,8,896]{0,2,1:T(8,128)(2,1)} %bitcast.97) | data formatting | bytes 3670016 | tf_op jit(solution)/shard_map/reshape | solution.py:58
  7.7 1.0 broadcast_in_dim.12
  8.7 6.8 %pad_maximum_fusion = bf16[8,128,4992]{2,1,0:T(8,128)(2,1)} fusion(bf16[8,128,896]{2,1,0:T(8,128)(2,1)S(1)} %bitcast.94, bf16[8,128,4096]{2,1,0:T(8,128)(2,1)S(1)} %broadcast_in_dim.12), kind=kLoop, calls=%fused_computation | loop fusion | flops 20447232 | bytes 20447232 | tf_op jit(solution)/shard_map/concatenate | solution.py:55
  15.5 5.9 %all-to-all-start = ((bf16[8,128,4992]{2,1,0:T(8,128)(2,1)}), bf16[8,128,4992]{2,1,0:T(8,128)(2,1)}, u32[]{:S(2)}, u32[]{:S(2)}) async-start(bf16[8,128,4992]{2,1,0:T(8,128)(2,1)} %pad_maximum_fusion), calls=%async_computation | async-start | bytes 20447232 | tf_op jit(solution)/shard_map/all_to_all | solution.py:62
  21.4 139.0 %all-to-all-done = bf16[8,128,4992]{2,1,0:T(8,128)(2,1)} async-done(((bf16[8,128,4992]{2,1,0:T(8,128)(2,1)}), bf16[8,128,4992]{2,1,0:T(8,128)(2,1)}, u32[]{:S(2)}, u32[]{:S(2)}) %all-to-all-start) | async-done | bytes 10223648 | tf_op jit(solution)/shard_map/all_to_all | solution.py:62
  160.4 2.2 fusion.10
  163.0 7.8 %slice.23 = bf16[8,128,4096]{2,1,0:T(8,128)(2,1)} slice(bf16[8,128,4992]{2,1,0:T(8,128)(2,1)} %all-to-all-done), slice={[0:8], [0:128], [0:4096]} | slice | bytes 16777216 | tf_op jit(solution)/shard_map/slice | solution.py:63
  170.9 5.0 %fusion.27 = f32[288,4096]{1,0:T(8,128)S(1)} fusion(bf16[288,1024]{1,0:T(8,128)(2,1)S(1)} %bitcast.100, bf16[1024,4096]{1,0:T(8,128)(2,1)} %bitcast.93), kind=kOutput, calls=%fused_computation.51 | convolution fusion | flops 2415919104 | bytes 13697024 | tf_op jit(solution)/shard_map/dot_general | solution.py:80
  176.2 0.3 copy.25
  176.4 1.8 constant_dynamic-slice_fusion.3
  178.3 5.3 %collective-permute-start.2 = (f32[8,3,32,128]{3,2,1,0:T(8,128)S(1)}, f32[8,3,32,128]{3,2,1,0:T(8,128)}, u32[]{:S(2)}, u32[]{:S(2)}) collective-permute-start(f32[8,3,32,128]{3,2,1,0:T(8,128)S(1)} %bitcast.101), channel_id=1, source_target_pairs={{0,24},{8,16},{16,8},{24,0},{32,56},{40,48},{48,40},{56,32},{64,88... | collective-permute-start | bytes 1179656 | tf_op jit(solution)/shard_map/ppermute | solution.py:31
  183.8 0.8 copy.32
  184.6 0.4 collective-permute-start
  185.0 12.2 %fusion.4 = bf16[8,128,896]{2,1,0:T(8,128)(2,1)} fusion(bf16[896,4096]{1,0:T(8,128)(2,1)S(1)} %bitcast.104, bf16[8,128,4992]{2,1,0:T(8,128)(2,1)} %all-to-all-done), kind=kOutput, calls=%fused_computation.5 | convolution fusion | flops 7517110272 | bytes 17563648 | tf_op jit(solution)/shard_map/ptd,hd->pth/dot_general | solution.py:65
  197.2 3.7 %all-to-all-start.1 = ((bf16[8,128,896]{2,1,0:T(8,128)(2,1)}), bf16[8,128,896]{2,1,0:T(8,128)(2,1)S(1)}, u32[]{:S(2)}, u32[]{:S(2)}) async-start(bf16[8,128,896]{2,1,0:T(8,128)(2,1)} %fusion.4), calls=%async_computation.1 | async-start | bytes 3670016 | tf_op jit(solution)/shard_map/all_to_all | solution.py:68
  201.0 0.5 collective-permute-done.1
  201.5 1.4 fusion.17
  203.0 5.7 %collective-permute-start.9 = (f32[3,32,128]{2,1,0:T(8,128)S(1)}, f32[3,32,128]{2,1,0:T(8,128)S(1)}, u32[]{:S(2)}, u32[]{:S(2)}) collective-permute-start(f32[3,32,128]{2,1,0:T(8,128)S(1)} %get-tuple-element.17), channel_id=1, source_target_pairs={{0,224},{8,232},{16,240},{24,248},{32,192},{40,200},{48,208},{56,2... | collective-permute-start | bytes 147464 | tf_op jit(solution)/shard_map/ppermute | solution.py:36
  208.7 0.6 collective-permute-start.8
  209.2 3.5 %collective-permute-start.7 = (f32[3,32,128]{2,1,0:T(8,128)S(1)}, f32[3,32,128]{2,1,0:T(8,128)S(1)}, u32[]{:S(2)}, u32[]{:S(2)}) collective-permute-start(f32[3,32,128]{2,1,0:T(8,128)S(1)} %get-tuple-element.19), channel_id=1, source_target_pairs={{0,160},{8,168},{16,176},{24,184},{32,128},{40,136},{48,144},{56,1... | collective-permute-start | bytes 147464 | tf_op jit(solution)/shard_map/ppermute | solution.py:36
  212.7 1.8 collective-permute-start.6
  214.5 1.6 collective-permute-start.5
  216.2 1.9 collective-permute-start.3
  218.1 2.0 collective-permute-done.6
  220.1 3.6 %collective-permute-done.4 = f32[3,32,128]{2,1,0:T(8,128)S(1)} collective-permute-done((f32[3,32,128]{2,1,0:T(8,128)S(1)}, f32[3,32,128]{2,1,0:T(8,128)S(1)}, u32[]{:S(2)}, u32[]{:S(2)}) %collective-permute-start.4) | collective-permute-done | bytes 49184 | tf_op jit(solution)/shard_map/ppermute | solution.py:36
  223.8 0.4 fusion.9
  224.2 1.0 copy.24
  225.1 1.0 fusion.13
  226.2 2.6 %all-to-all-done.1 = bf16[8,128,896]{2,1,0:T(8,128)(2,1)S(1)} async-done(((bf16[8,128,896]{2,1,0:T(8,128)(2,1)}), bf16[8,128,896]{2,1,0:T(8,128)(2,1)S(1)}, u32[]{:S(2)}, u32[]{:S(2)}) %all-to-all-start.1) | async-done | bytes 1835040 | tf_op jit(solution)/shard_map/all_to_all | solution.py:68
  228.8 2.4 %copy.17 = bf16[128,8,896]{0,2,1:T(8,128)(2,1)} copy(bf16[128,8,896]{2,0,1:T(8,128)(2,1)S(1)} %bitcast.95) | data formatting | bytes 3670016 | tf_op jit(solution)/shard_map/all_to_all | solution.py:68
  231.2 3.9 %copy.23 = bf16[128,7168]{1,0:T(8,128)(2,1)} copy(bf16[128,7168]{0,1:T(8,128)(2,1)} %bitcast.96) | data formatting | bytes 3670016
  (33 shorter events, 1.2 us)
Async XLA Ops:
  0.6 159.7 %copy-start = (bf16[3,32,896]{2,1,0:T(8,128)(2,1)S(1)}, bf16[3,32,896]{2,1,0:T(8,128)(2,1)}, u32[]{:S(2)}) copy-start(bf16[3,32,896]{2,1,0:T(8,128)(2,1)} %param.9) | copy-start | bytes 516100
  0.6 7.0 %copy-start.1 = (bf16[128,4096]{1,0:T(8,128)(2,1)S(1)}, bf16[128,4096]{1,0:T(8,128)(2,1)}, u32[]{:S(2)}) copy-start(bf16[128,4096]{1,0:T(8,128)(2,1)} %param.7) | copy-start | bytes 3145732
  15.5 144.8 %all-to-all-start = ((bf16[8,128,4992]{2,1,0:T(8,128)(2,1)}), bf16[8,128,4992]{2,1,0:T(8,128)(2,1)}, u32[]{:S(2)}, u32[]{:S(2)}) async-start(bf16[8,128,4992]{2,1,0:T(8,128)(2,1)} %pad_maximum_fusion), calls=%async_computation | async-start | bytes 20447232 | tf_op jit(solution)/shard_map/all_to_all | solution.py:62
  175.9 9.1 %slice-start = ((s8[7340032]{0:T(1024)(128)(4,1)}), s8[4194304]{0:T(1024)(128)(4,1)S(1)}, s32[]{:S(2)}) async-start(s8[7340032]{0:T(1024)(128)(4,1)} %bitcast.103), calls=%async_computation.2 | async-start | bytes 8388608
  176.1 8.8 %slice-start.1 = ((s8[7340032]{0:T(1024)(128)(4,1)}), s8[3145728]{0:T(1024)(128)(4,1)S(1)}, s32[]{:S(2)}) async-start(s8[7340032]{0:T(1024)(128)(4,1)} %bitcast.103), calls=%async_computation.3 | async-start | bytes 6291456
  178.3 22.7 %collective-permute-start.2 = (f32[8,3,32,128]{3,2,1,0:T(8,128)S(1)}, f32[8,3,32,128]{3,2,1,0:T(8,128)}, u32[]{:S(2)}, u32[]{:S(2)}) collective-permute-start(f32[8,3,32,128]{3,2,1,0:T(8,128)S(1)} %bitcast.101), channel_id=1, source_target_pairs={{0,24},{8,16},{16,8},{24,0},{32,56},{40,48},{48,40},{56,32},{64,88... | collective-permute-start | bytes 1179656 | tf_op jit(solution)/shard_map/ppermute | solution.py:31
  183.6 17.9 %collective-permute-start.1 = (f32[8,3,32,128]{3,2,1,0:T(8,128)S(1)}, f32[8,3,32,128]{3,2,1,0:T(8,128)}, u32[]{:S(2)}, u32[]{:S(2)}) collective-permute-start(f32[8,3,32,128]{3,2,1,0:T(8,128)S(1)} %bitcast.102), channel_id=1, source_target_pairs={{0,16},{8,24},{16,0},{24,8},{32,48},{40,56},{48,32},{56,40},{64,80... | collective-permute-start | bytes 1179656 | tf_op jit(solution)/shard_map/ppermute | solution.py:31
  184.6 16.9 %collective-permute-start = (f32[8,3,32,128]{3,2,1,0:T(8,128)}, f32[8,3,32,128]{3,2,1,0:T(8,128)}, u32[]{:S(2)}, u32[]{:S(2)}) collective-permute-start(f32[8,3,32,128]{3,2,1,0:T(8,128)} %bitcast.91), channel_id=1, source_target_pairs={{0,8},{8,0},{16,24},{24,16},{32,40},{40,32},{48,56},{56,48},{64,72... | collective-permute-start | bytes 1179656 | tf_op jit(solution)/shard_map/ppermute | solution.py:31
  197.2 26.5 %copy-start.4 = (f32[1,3,32,128]{3,2,1,0:T(8,128)S(1)}, f32[1,3,32,128]{3,2,1,0:T(8,128)}, u32[]{:S(2)}) copy-start(f32[1,3,32,128]{3,2,1,0:T(8,128)} %param.10) | copy-start | bytes 147460
  197.2 26.6 %copy-start.3 = (f32[1,3,32,128]{3,2,1,0:T(8,128)S(1)}, f32[1,3,32,128]{3,2,1,0:T(8,128)}, u32[]{:S(2)}) copy-start(f32[1,3,32,128]{3,2,1,0:T(8,128)} %param.11) | copy-start | bytes 147460
  197.2 31.6 %all-to-all-start.1 = ((bf16[8,128,896]{2,1,0:T(8,128)(2,1)}), bf16[8,128,896]{2,1,0:T(8,128)(2,1)S(1)}, u32[]{:S(2)}, u32[]{:S(2)}) async-start(bf16[8,128,896]{2,1,0:T(8,128)(2,1)} %fusion.4), calls=%async_computation.1 | async-start | bytes 3670016 | tf_op jit(solution)/shard_map/all_to_all | solution.py:68
  203.0 13.2 %collective-permute-start.9 = (f32[3,32,128]{2,1,0:T(8,128)S(1)}, f32[3,32,128]{2,1,0:T(8,128)S(1)}, u32[]{:S(2)}, u32[]{:S(2)}) collective-permute-start(f32[3,32,128]{2,1,0:T(8,128)S(1)} %get-tuple-element.17), channel_id=1, source_target_pairs={{0,224},{8,232},{16,240},{24,248},{32,192},{40,200},{48,208},{56,2... | collective-permute-start | bytes 147464 | tf_op jit(solution)/shard_map/ppermute | solution.py:36
  208.7 7.5 %collective-permute-start.8 = (f32[3,32,128]{2,1,0:T(8,128)S(1)}, f32[3,32,128]{2,1,0:T(8,128)S(1)}, u32[]{:S(2)}, u32[]{:S(2)}) collective-permute-start(f32[3,32,128]{2,1,0:T(8,128)S(1)} %get-tuple-element.18), channel_id=1, source_target_pairs={{0,192},{8,200},{16,208},{24,216},{32,224},{40,232},{48,240},{56,2... | collective-permute-start | bytes 147464 | tf_op jit(solution)/shard_map/ppermute | solution.py:36
  209.2 8.8 %collective-permute-start.7 = (f32[3,32,128]{2,1,0:T(8,128)S(1)}, f32[3,32,128]{2,1,0:T(8,128)S(1)}, u32[]{:S(2)}, u32[]{:S(2)}) collective-permute-start(f32[3,32,128]{2,1,0:T(8,128)S(1)} %get-tuple-element.19), channel_id=1, source_target_pairs={{0,160},{8,168},{16,176},{24,184},{32,128},{40,136},{48,144},{56,1... | collective-permute-start | bytes 147464 | tf_op jit(solution)/shard_map/ppermute | solution.py:36
  212.7 7.4 %collective-permute-start.6 = (f32[3,32,128]{2,1,0:T(8,128)S(1)}, f32[3,32,128]{2,1,0:T(8,128)S(1)}, u32[]{:S(2)}, u32[]{:S(2)}) collective-permute-start(f32[3,32,128]{2,1,0:T(8,128)S(1)} %get-tuple-element.20), channel_id=1, source_target_pairs={{0,128},{8,136},{16,144},{24,152},{32,160},{40,168},{48,176},{56,1... | collective-permute-start | bytes 147464 | tf_op jit(solution)/shard_map/ppermute | solution.py:36
  214.5 5.6 %collective-permute-start.5 = (f32[3,32,128]{2,1,0:T(8,128)S(1)}, f32[3,32,128]{2,1,0:T(8,128)S(1)}, u32[]{:S(2)}, u32[]{:S(2)}) collective-permute-start(f32[3,32,128]{2,1,0:T(8,128)S(1)} %get-tuple-element.21), channel_id=1, source_target_pairs={{0,96},{8,104},{16,112},{24,120},{32,64},{40,72},{48,80},{56,88},{... | collective-permute-start | bytes 147464 | tf_op jit(solution)/shard_map/ppermute | solution.py:36
  216.1 7.5 %collective-permute-start.4 = (f32[3,32,128]{2,1,0:T(8,128)S(1)}, f32[3,32,128]{2,1,0:T(8,128)S(1)}, u32[]{:S(2)}, u32[]{:S(2)}) collective-permute-start(f32[3,32,128]{2,1,0:T(8,128)S(1)} %get-tuple-element.22), channel_id=1, source_target_pairs={{0,64},{8,72},{16,80},{24,88},{32,96},{40,104},{48,112},{56,120},{... | collective-permute-start | bytes 147464 | tf_op jit(solution)/shard_map/ppermute | solution.py:36
  216.2 7.5 %collective-permute-start.3 = (f32[3,32,128]{2,1,0:T(8,128)S(1)}, f32[3,32,128]{2,1,0:T(8,128)S(1)}, u32[]{:S(2)}, u32[]{:S(2)}) collective-permute-start(f32[3,32,128]{2,1,0:T(8,128)S(1)} %get-tuple-element.16), channel_id=1, source_target_pairs={{0,32},{8,40},{16,48},{24,56},{32,0},{40,8},{48,16},{56,24},{64,96... | collective-permute-start | bytes 147464 | tf_op jit(solution)/shard_map/ppermute | solution.py:36
  223.7 11.3 %copy-start.2 = (f32[1,3,32,128]{3,2,1,0:T(8,128)}, f32[1,3,32,128]{3,2,1,0:T(8,128)S(1)}, u32[]{:S(2)}) copy-start(f32[1,3,32,128]{3,2,1,0:T(8,128)S(1)} %bitcast_add_fusion.1) | copy-start | bytes 147460

commit v7 on v6

--- a/solution.py
+++ b/solution.py
@@ -52,16 +52,18 @@
 
     hash_float = hash_tiles.astype(jnp.float32)
 
+    hidden_rows = tok_rows * shard_rows // model_width
     outgoing = jnp.concatenate(
         [
             jnp.broadcast_to(grad_out[None], (shards, tok_rows, model_width)),
-            hidden.reshape(tok_rows, shards, shard_rows).transpose(1, 0, 2),
+            hidden.reshape(tok_rows, shards, shard_rows).transpose(1, 0, 2)
+            .reshape(shards, hidden_rows, model_width),
         ],
-        axis=2,
+        axis=1,
     )
     arrived = lax.all_to_all(outgoing, "fsdp", split_axis=0, concat_axis=0, tiled=True)
-    gathered = arrived[:, :, :model_width]
-    hidden_cols = arrived[:, :, model_width:]
+    gathered = arrived[:, :tok_rows]
+    hidden_cols = arrived[:, tok_rows:].reshape(shards, tok_rows, shard_rows)
     partial_grads = jnp.einsum(
         "ptd,hd->pth", gathered, down_weight, preferred_element_type=jnp.float32
     ).astype(jnp.bfloat16)
@@ -77,8 +79,11 @@
         preferred_element_type=jnp.float32,
     ).reshape(sketch_rows, shards * tok_rows)
     pieces = split3(projected).reshape(3 * sketch_rows, shards * tok_rows)
-    products = jnp.dot(
-        pieces, gathered.reshape(shards * tok_rows, model_width), preferred_element_type=jnp.float32
+    products = jnp.einsum(
+        "mpt,ptd->md",
+        pieces.reshape(3 * sketch_rows, shards, tok_rows),
+        gathered,
+        preferred_element_type=jnp.float32,
     ).reshape(3, sketch_rows, replicas, columns)
     summed = (products[0] + products[1] + products[2]).transpose(1, 0, 2)
     sketch_table = grouped_scatter(

time: 236 us -> 236 us (level)
  local copies, waits for them, and re-layouts: 26.5 us -> 23.1 us
  waiting for transfers between devices: 148 us -> 151 us
    reshape x0 -> x2, local copies, waits for them, and re-layouts: none -> 6.54 us  [the longest x1 3.48 us: on_device(): outgoing = jnp.concatenate([jnp.broadcast_to(grad_out[None], (shards, tok...]
    slice x1, local copies, waits for them, and re-layouts: 7.83 us -> 1.73 us  [on_device(): hidden_cols = arrived[:, tok_rows:].reshape(shards, tok_rows, shard_rows)]
    unnamed x18, local copies, waits for them, and re-layouts: 9.13 us -> 5.26 us
    all_to_all x1, waiting for transfers between devices: 139 us -> 142 us  [on_device(): lax.all_to_all(outgoing, 'fsdp', split_axis=0, concat_axis=0, tiled=True)]
where the time goes in v7:
time: 236 us
  waiting for transfers between devices  151 us (64%)
  starting transfers between devices  30.5 us (13%)
  local copies, waits for them, and re-layouts  23.1 us (10%)
  matrix products  20.9 us (9%)
  other arithmetic  9.29 us (4%)
    all_to_all x1, waiting for transfers between devices, on_device(): lax.all_to_all(outgoing, 'fsdp', split_axis=0, concat_axis=0, tiled=True)  142 us
    ppermute x7, starting transfers between devices, grouped_scatter(): lax.ppermute(send, 'rep', [(j, j ^ mask * inner) for j in range(replicas)])  15.1 us
    dot_general x1, matrix products, on_device(): jnp.einsum('ptd,hd->pth', gathered, down_weight, preferred_element_type=j...  12.2 us
    concatenate x1, other arithmetic, on_device(): jnp.concatenate([jnp.broadcast_to(grad_out[None], (shards, tok_rows, mode...  7.41 us
    all_to_all x1, starting transfers between devices, on_device(): lax.all_to_all(outgoing, 'fsdp', split_axis=0, concat_axis=0, tiled=True)  5.86 us
    ppermute x3, starting transfers between devices, grouped_scatter(): lax.ppermute(send, 'rep', [(j, j ^ mask) for j in range(replicas)])  5.81 us
    ppermute x7, waiting for transfers between devices, grouped_scatter(): lax.ppermute(send, 'rep', [(j, j ^ mask * inner) for j in range(replicas)])  5.62 us
    unnamed x18, local copies, waits for them, and re-layouts  5.26 us
  transfers between devices with their start and end apart: 12, of which 5 were waited for; matrix products, arithmetic and copies ran while one was open for 7% of the time, Pallas kernels for 0%

profile of v7, /device:TPU:1, one launch (start us, length us, event | category | flops | bytes accessed | tf_op | source)
XLA Modules:
  0.0 235.9 jit_solution(5903041457045671536)
XLA Ops:
  0.7 3.1 %copy.36 = bf16[16,8,8,896]{3,2,0,1:T(8,128)(2,1)} copy(bf16[16,8,8,896]{3,2,1,0:T(8,128)(2,1)} %bitcast.106) | data formatting | bytes 3670016 | tf_op jit(solution)/shard_map/reshape | solution.py:59
  3.7 3.5 %reshape.79 = bf16[8,28,4096]{2,1,0:T(8,128)(2,1)S(1)} reshape(bf16[8,128,896]{2,1,0:T(8,128)(2,1)} %bitcast.102) | data formatting | bytes 3670016 | tf_op jit(solution)/shard_map/reshape | solution.py:60
  7.2 1.0 broadcast_in_dim.12
  8.3 7.4 %pad_maximum_fusion = bf16[8,156,4096]{2,1,0:T(8,128)(2,1)} fusion(bf16[8,28,4096]{2,1,0:T(8,128)(2,1)S(1)} %reshape.79, bf16[8,128,4096]{2,1,0:T(8,128)(2,1)S(1)} %broadcast_in_dim.12), kind=kLoop, calls=%fused_computation | loop fusion | flops 20447232 | bytes 20447232 | tf_op jit(solution)/shard_map/concatenate | solution.py:56
  15.7 5.9 %all-to-all-start = ((bf16[8,156,4096]{2,1,0:T(8,128)(2,1)}), bf16[8,156,4096]{2,1,0:T(8,128)(2,1)}, u32[]{:S(2)}, u32[]{:S(2)}) async-start(bf16[8,156,4096]{2,1,0:T(8,128)(2,1)} %pad_maximum_fusion), calls=%async_computation | async-start | bytes 20971520 | tf_op jit(solution)/shard_map/all_to_all | solution.py:64
  21.5 142.5 %all-to-all-done = bf16[8,156,4096]{2,1,0:T(8,128)(2,1)} async-done(((bf16[8,156,4096]{2,1,0:T(8,128)(2,1)}), bf16[8,156,4096]{2,1,0:T(8,128)(2,1)}, u32[]{:S(2)}, u32[]{:S(2)}) %all-to-all-start) | async-done | bytes 10223648 | tf_op jit(solution)/shard_map/all_to_all | solution.py:64
  164.0 1.7 slice.24
  165.7 3.1 %reshape.80 = bf16[8,128,896]{2,1,0:T(8,128)(2,1)} reshape(bf16[8,28,4096]{2,1,0:T(8,128)(2,1)S(1)} %slice.24) | data formatting | bytes 3670016 | tf_op jit(solution)/shard_map/reshape | solution.py:66
  168.8 2.2 convolution_bitcast_fusion.1
  171.6 5.0 %fusion.5 = f32[288,4096]{1,0:T(8,128)S(1)} fusion(bf16[8,156,4096]{2,1,0:T(8,128)(2,1)} %all-to-all-done, bf16[288,8,128]{2,1,0:T(8,128)(2,1)S(1)} %bitcast.107), kind=kOutput, calls=%fused_computation.6 | convolution fusion | flops 2415919104 | bytes 13697024 | tf_op jit(solution)/shard_map/mpt,ptd->md/dot_general | solution.py:82
  177.2 1.8 constant_dynamic-slice_fusion.3
  179.1 5.3 %collective-permute-start.2 = (f32[8,3,32,128]{3,2,1,0:T(8,128)S(1)}, f32[8,3,32,128]{3,2,1,0:T(8,128)}, u32[]{:S(2)}, u32[]{:S(2)}) collective-permute-start(f32[8,3,32,128]{3,2,1,0:T(8,128)S(1)} %bitcast.108), channel_id=1, source_target_pairs={{0,24},{8,16},{16,8},{24,0},{32,56},{40,48},{48,40},{56,32},{64,88... | collective-permute-start | bytes 1179656 | tf_op jit(solution)/shard_map/ppermute | solution.py:31
  184.5 0.8 copy.39
  185.4 0.4 collective-permute-start
  185.8 12.2 %fusion.8 = bf16[8,128,896]{2,1,0:T(8,128)(2,1)} fusion(bf16[896,4096]{1,0:T(8,128)(2,1)S(1)} %bitcast.111, bf16[8,156,4096]{2,1,0:T(8,128)(2,1)} %all-to-all-done), kind=kOutput, calls=%fused_computation.8 | convolution fusion | flops 7517110272 | bytes 17563648 | tf_op jit(solution)/shard_map/ptd,hd->pth/dot_general | solution.py:67
  198.0 3.7 %all-to-all-start.1 = ((bf16[8,128,896]{2,1,0:T(8,128)(2,1)}), bf16[8,128,896]{2,1,0:T(8,128)(2,1)S(1)}, u32[]{:S(2)}, u32[]{:S(2)}) async-start(bf16[8,128,896]{2,1,0:T(8,128)(2,1)} %fusion.8), calls=%async_computation.1 | async-start | bytes 3670016 | tf_op jit(solution)/shard_map/all_to_all | solution.py:70
  201.8 0.5 collective-permute-done.1
  202.3 1.4 fusion.21
  203.7 5.8 %collective-permute-start.9 = (f32[3,32,128]{2,1,0:T(8,128)S(1)}, f32[3,32,128]{2,1,0:T(8,128)S(1)}, u32[]{:S(2)}, u32[]{:S(2)}) collective-permute-start(f32[3,32,128]{2,1,0:T(8,128)S(1)} %get-tuple-element.17), channel_id=1, source_target_pairs={{0,224},{8,232},{16,240},{24,248},{32,192},{40,200},{48,208},{56,2... | collective-permute-start | bytes 147464 | tf_op jit(solution)/shard_map/ppermute | solution.py:36
  209.5 0.6 collective-permute-start.8
  210.0 3.5 %collective-permute-start.7 = (f32[3,32,128]{2,1,0:T(8,128)S(1)}, f32[3,32,128]{2,1,0:T(8,128)S(1)}, u32[]{:S(2)}, u32[]{:S(2)}) collective-permute-start(f32[3,32,128]{2,1,0:T(8,128)S(1)} %get-tuple-element.19), channel_id=1, source_target_pairs={{0,160},{8,168},{16,176},{24,184},{32,128},{40,136},{48,144},{56,1... | collective-permute-start | bytes 147464 | tf_op jit(solution)/shard_map/ppermute | solution.py:36
  213.5 1.8 collective-permute-start.6
  215.3 1.6 collective-permute-start.5
  217.0 1.9 collective-permute-start.3
  218.9 2.0 collective-permute-done.6
  220.9 3.6 %collective-permute-done.4 = f32[3,32,128]{2,1,0:T(8,128)S(1)} collective-permute-done((f32[3,32,128]{2,1,0:T(8,128)S(1)}, f32[3,32,128]{2,1,0:T(8,128)S(1)}, u32[]{:S(2)}, u32[]{:S(2)}) %collective-permute-start.4) | collective-permute-done | bytes 49184 | tf_op jit(solution)/shard_map/ppermute | solution.py:36
  224.6 0.4 fusion.15
  225.0 1.0 copy.25
  225.9 1.0 fusion.16
  227.0 2.7 %all-to-all-done.1 = bf16[8,128,896]{2,1,0:T(8,128)(2,1)S(1)} async-done(((bf16[8,128,896]{2,1,0:T(8,128)(2,1)}), bf16[8,128,896]{2,1,0:T(8,128)(2,1)S(1)}, u32[]{:S(2)}, u32[]{:S(2)}) %all-to-all-start.1) | async-done | bytes 1835040 | tf_op jit(solution)/shard_map/all_to_all | solution.py:70
  229.7 2.4 %copy.17 = bf16[128,8,896]{0,2,1:T(8,128)(2,1)} copy(bf16[128,8,896]{2,0,1:T(8,128)(2,1)S(1)} %bitcast.100) | data formatting | bytes 3670016 | tf_op jit(solution)/shard_map/all_to_all | solution.py:70
  232.1 3.9 %copy.24 = bf16[128,7168]{1,0:T(8,128)(2,1)} copy(bf16[128,7168]{0,1:T(8,128)(2,1)} %bitcast.101) | data formatting | bytes 3670016
  (35 shorter events, 1.5 us)
Async XLA Ops:
  0.6 168.2 %copy-start = (bf16[3,32,896]{2,1,0:T(8,128)(2,1)S(1)}, bf16[3,32,896]{2,1,0:T(8,128)(2,1)}, u32[]{:S(2)}) copy-start(bf16[3,32,896]{2,1,0:T(8,128)(2,1)} %param.9) | copy-start | bytes 516100
  0.6 6.6 %copy-start.1 = (bf16[128,4096]{1,0:T(8,128)(2,1)S(1)}, bf16[128,4096]{1,0:T(8,128)(2,1)}, u32[]{:S(2)}) copy-start(bf16[128,4096]{1,0:T(8,128)(2,1)} %param.7) | copy-start | bytes 3145732
  15.7 148.3 %all-to-all-start = ((bf16[8,156,4096]{2,1,0:T(8,128)(2,1)}), bf16[8,156,4096]{2,1,0:T(8,128)(2,1)}, u32[]{:S(2)}, u32[]{:S(2)}) async-start(bf16[8,156,4096]{2,1,0:T(8,128)(2,1)} %pad_maximum_fusion), calls=%async_computation | async-start | bytes 20971520 | tf_op jit(solution)/shard_map/all_to_all | solution.py:64
  176.6 9.2 %slice-start = ((s8[7340032]{0:T(1024)(128)(4,1)}), s8[4194304]{0:T(1024)(128)(4,1)S(1)}, s32[]{:S(2)}) async-start(s8[7340032]{0:T(1024)(128)(4,1)} %bitcast.110), calls=%async_computation.2 | async-start | bytes 8388608
  176.9 8.9 %slice-start.1 = ((s8[7340032]{0:T(1024)(128)(4,1)}), s8[3145728]{0:T(1024)(128)(4,1)S(1)}, s32[]{:S(2)}) async-start(s8[7340032]{0:T(1024)(128)(4,1)} %bitcast.110), calls=%async_computation.3 | async-start | bytes 6291456
  179.1 22.7 %collective-permute-start.2 = (f32[8,3,32,128]{3,2,1,0:T(8,128)S(1)}, f32[8,3,32,128]{3,2,1,0:T(8,128)}, u32[]{:S(2)}, u32[]{:S(2)}) collective-permute-start(f32[8,3,32,128]{3,2,1,0:T(8,128)S(1)} %bitcast.108), channel_id=1, source_target_pairs={{0,24},{8,16},{16,8},{24,0},{32,56},{40,48},{48,40},{56,32},{64,88... | collective-permute-start | bytes 1179656 | tf_op jit(solution)/shard_map/ppermute | solution.py:31
  184.4 17.8 %collective-permute-start.1 = (f32[8,3,32,128]{3,2,1,0:T(8,128)S(1)}, f32[8,3,32,128]{3,2,1,0:T(8,128)}, u32[]{:S(2)}, u32[]{:S(2)}) collective-permute-start(f32[8,3,32,128]{3,2,1,0:T(8,128)S(1)} %bitcast.109), channel_id=1, source_target_pairs={{0,16},{8,24},{16,0},{24,8},{32,48},{40,56},{48,32},{56,40},{64,80... | collective-permute-start | bytes 1179656 | tf_op jit(solution)/shard_map/ppermute | solution.py:31
  185.4 16.9 %collective-permute-start = (f32[8,3,32,128]{3,2,1,0:T(8,128)}, f32[8,3,32,128]{3,2,1,0:T(8,128)}, u32[]{:S(2)}, u32[]{:S(2)}) collective-permute-start(f32[8,3,32,128]{3,2,1,0:T(8,128)} %bitcast.98), channel_id=1, source_target_pairs={{0,8},{8,0},{16,24},{24,16},{32,40},{40,32},{48,56},{56,48},{64,72... | collective-permute-start | bytes 1179656 | tf_op jit(solution)/shard_map/ppermute | solution.py:31
  198.0 26.5 %copy-start.4 = (f32[1,3,32,128]{3,2,1,0:T(8,128)S(1)}, f32[1,3,32,128]{3,2,1,0:T(8,128)}, u32[]{:S(2)}) copy-start(f32[1,3,32,128]{3,2,1,0:T(8,128)} %param.10) | copy-start | bytes 147460
  198.0 26.5 %copy-start.3 = (f32[1,3,32,128]{3,2,1,0:T(8,128)S(1)}, f32[1,3,32,128]{3,2,1,0:T(8,128)}, u32[]{:S(2)}) copy-start(f32[1,3,32,128]{3,2,1,0:T(8,128)} %param.11) | copy-start | bytes 147460
  198.0 31.7 %all-to-all-start.1 = ((bf16[8,128,896]{2,1,0:T(8,128)(2,1)}), bf16[8,128,896]{2,1,0:T(8,128)(2,1)S(1)}, u32[]{:S(2)}, u32[]{:S(2)}) async-start(bf16[8,128,896]{2,1,0:T(8,128)(2,1)} %fusion.8), calls=%async_computation.1 | async-start | bytes 3670016 | tf_op jit(solution)/shard_map/all_to_all | solution.py:70
  203.7 13.2 %collective-permute-start.9 = (f32[3,32,128]{2,1,0:T(8,128)S(1)}, f32[3,32,128]{2,1,0:T(8,128)S(1)}, u32[]{:S(2)}, u32[]{:S(2)}) collective-permute-start(f32[3,32,128]{2,1,0:T(8,128)S(1)} %get-tuple-element.17), channel_id=1, source_target_pairs={{0,224},{8,232},{16,240},{24,248},{32,192},{40,200},{48,208},{56,2... | collective-permute-start | bytes 147464 | tf_op jit(solution)/shard_map/ppermute | solution.py:36
  209.5 7.5 %collective-permute-start.8 = (f32[3,32,128]{2,1,0:T(8,128)S(1)}, f32[3,32,128]{2,1,0:T(8,128)S(1)}, u32[]{:S(2)}, u32[]{:S(2)}) collective-permute-start(f32[3,32,128]{2,1,0:T(8,128)S(1)} %get-tuple-element.18), channel_id=1, source_target_pairs={{0,192},{8,200},{16,208},{24,216},{32,224},{40,232},{48,240},{56,2... | collective-permute-start | bytes 147464 | tf_op jit(solution)/shard_map/ppermute | solution.py:36
  210.0 8.8 %collective-permute-start.7 = (f32[3,32,128]{2,1,0:T(8,128)S(1)}, f32[3,32,128]{2,1,0:T(8,128)S(1)}, u32[]{:S(2)}, u32[]{:S(2)}) collective-permute-start(f32[3,32,128]{2,1,0:T(8,128)S(1)} %get-tuple-element.19), channel_id=1, source_target_pairs={{0,160},{8,168},{16,176},{24,184},{32,128},{40,136},{48,144},{56,1... | collective-permute-start | bytes 147464 | tf_op jit(solution)/shard_map/ppermute | solution.py:36
  213.5 7.4 %collective-permute-start.6 = (f32[3,32,128]{2,1,0:T(8,128)S(1)}, f32[3,32,128]{2,1,0:T(8,128)S(1)}, u32[]{:S(2)}, u32[]{:S(2)}) collective-permute-start(f32[3,32,128]{2,1,0:T(8,128)S(1)} %get-tuple-element.20), channel_id=1, source_target_pairs={{0,128},{8,136},{16,144},{24,152},{32,160},{40,168},{48,176},{56,1... | collective-permute-start | bytes 147464 | tf_op jit(solution)/shard_map/ppermute | solution.py:36
  215.3 5.6 %collective-permute-start.5 = (f32[3,32,128]{2,1,0:T(8,128)S(1)}, f32[3,32,128]{2,1,0:T(8,128)S(1)}, u32[]{:S(2)}, u32[]{:S(2)}) collective-permute-start(f32[3,32,128]{2,1,0:T(8,128)S(1)} %get-tuple-element.21), channel_id=1, source_target_pairs={{0,96},{8,104},{16,112},{24,120},{32,64},{40,72},{48,80},{56,88},{... | collective-permute-start | bytes 147464 | tf_op jit(solution)/shard_map/ppermute | solution.py:36
  216.9 7.5 %collective-permute-start.4 = (f32[3,32,128]{2,1,0:T(8,128)S(1)}, f32[3,32,128]{2,1,0:T(8,128)S(1)}, u32[]{:S(2)}, u32[]{:S(2)}) collective-permute-start(f32[3,32,128]{2,1,0:T(8,128)S(1)} %get-tuple-element.22), channel_id=1, source_target_pairs={{0,64},{8,72},{16,80},{24,88},{32,96},{40,104},{48,112},{56,120},{... | collective-permute-start | bytes 147464 | tf_op jit(solution)/shard_map/ppermute | solution.py:36
  217.0 7.5 %collective-permute-start.3 = (f32[3,32,128]{2,1,0:T(8,128)S(1)}, f32[3,32,128]{2,1,0:T(8,128)S(1)}, u32[]{:S(2)}, u32[]{:S(2)}) collective-permute-start(f32[3,32,128]{2,1,0:T(8,128)S(1)} %get-tuple-element.16), channel_id=1, source_target_pairs={{0,32},{8,40},{16,48},{24,56},{32,0},{40,8},{48,16},{56,24},{64,96... | collective-permute-start | bytes 147464 | tf_op jit(solution)/shard_map/ppermute | solution.py:36
  224.5 11.4 %copy-start.2 = (f32[1,3,32,128]{3,2,1,0:T(8,128)}, f32[1,3,32,128]{3,2,1,0:T(8,128)S(1)}, u32[]{:S(2)}) copy-start(f32[1,3,32,128]{3,2,1,0:T(8,128)S(1)} %bitcast_add_fusion.1) | copy-start | bytes 147460

commit v8 on v6

--- a/solution.py
+++ b/solution.py
@@ -63,12 +63,11 @@
     gathered = arrived[:, :, :model_width]
     hidden_cols = arrived[:, :, model_width:]
     partial_grads = jnp.einsum(
-        "ptd,hd->pth", gathered, down_weight, preferred_element_type=jnp.float32
+        "ptd,hd->tph", gathered, down_weight, preferred_element_type=jnp.float32
     ).astype(jnp.bfloat16)
     grad_hidden = lax.all_to_all(
-        partial_grads.reshape(shards * tok_rows, shard_rows), "fsdp",
-        split_axis=0, concat_axis=1, tiled=True,
-    )
+        partial_grads, "fsdp", split_axis=1, concat_axis=1, tiled=True
+    ).reshape(tok_rows, shards * shard_rows)
 
     projected = jnp.einsum(
         "ki,pti->kpt",
@@ -77,8 +76,11 @@
         preferred_element_type=jnp.float32,
     ).reshape(sketch_rows, shards * tok_rows)
     pieces = split3(projected).reshape(3 * sketch_rows, shards * tok_rows)
-    products = jnp.dot(
-        pieces, gathered.reshape(shards * tok_rows, model_width), preferred_element_type=jnp.float32
+    products = jnp.einsum(
+        "mpt,ptd->md",
+        pieces.reshape(3 * sketch_rows, shards, tok_rows),
+        gathered,
+        preferred_element_type=jnp.float32,
     ).reshape(3, sketch_rows, replicas, columns)
     summed = (products[0] + products[1] + products[2]).transpose(1, 0, 2)
     sketch_table = grouped_scatter(

time: 236 us -> 228 us (0.966)
  local copies, waits for them, and re-layouts: 26.5 us -> 18.8 us
    slice x1 -> x0, local copies, waits for them, and re-layouts: 7.83 us -> none  [on_device(): gathered = arrived[:, :, :model_width]]
    unnamed x18 -> x19, local copies, waits for them, and re-layouts: 9.13 us -> 9.23 us
where the time goes in v8:
time: 228 us; the launch traced here: 227 us
  waiting for transfers between devices  148 us (65%)
  starting transfers between devices  30.4 us (13%)
  matrix products  20.8 us (9%)
  local copies, waits for them, and re-layouts  18.8 us (8%)
  other arithmetic  8.67 us (4%)
    all_to_all x1, waiting for transfers between devices, on_device(): lax.all_to_all(outgoing, 'fsdp', split_axis=0, concat_axis=0, tiled=True)  139 us
    ppermute x7, starting transfers between devices, grouped_scatter(): lax.ppermute(send, 'rep', [(j, j ^ mask * inner) for j in range(replicas)])  15.1 us
    dot_general x1, matrix products, on_device(): jnp.einsum('ptd,hd->tph', gathered, down_weight, preferred_element_type=j...  12.2 us
    unnamed x19, local copies, waits for them, and re-layouts  9.23 us
    concatenate x1, other arithmetic, on_device(): jnp.concatenate([jnp.broadcast_to(grad_out[None], (shards, tok_rows, mode...  6.79 us
    all_to_all x1, starting transfers between devices, on_device(): lax.all_to_all(outgoing, 'fsdp', split_axis=0, concat_axis=0, tiled=True)  5.86 us
    ppermute x3, starting transfers between devices, grouped_scatter(): lax.ppermute(send, 'rep', [(j, j ^ mask) for j in range(replicas)])  5.76 us
    ppermute x7, waiting for transfers between devices, grouped_scatter(): lax.ppermute(send, 'rep', [(j, j ^ mask * inner) for j in range(replicas)])  5.62 us
  transfers between devices with their start and end apart: 12, of which 5 were waited for; matrix products, arithmetic and copies ran while one was open for 7% of the time, Pallas kernels for 0%

profile of v8, /device:TPU:1, one launch (start us, length us, event | category | flops | bytes accessed | tf_op | source)
XLA Modules:
  0.0 227.3 jit_solution(13042546810772492705)
XLA Ops:
  0.7 4.0 %copy.15 = bf16[128,7168]{0,1:T(8,128)(2,1)} copy(bf16[128,7168]{1,0:T(8,128)(2,1)} %param.6) | data formatting | bytes 3670016 | tf_op args[0]
  4.6 3.1 %copy.16 = bf16[128,8,896]{2,0,1:T(8,128)(2,1)S(1)} copy(bf16[128,8,896]{0,2,1:T(8,128)(2,1)} %bitcast.97) | data formatting | bytes 3670016 | tf_op jit(solution)/shard_map/reshape | solution.py:58
  7.7 1.0 broadcast_in_dim.12
  8.7 6.8 %pad_maximum_fusion = bf16[8,128,4992]{2,1,0:T(8,128)(2,1)} fusion(bf16[8,128,896]{2,1,0:T(8,128)(2,1)S(1)} %bitcast.95, bf16[8,128,4096]{2,1,0:T(8,128)(2,1)S(1)} %broadcast_in_dim.12), kind=kLoop, calls=%fused_computation | loop fusion | flops 20447232 | bytes 20447232 | tf_op jit(solution)/shard_map/concatenate | solution.py:55
  15.5 5.9 %all-to-all-start = ((bf16[8,128,4992]{2,1,0:T(8,128)(2,1)}), bf16[8,128,4992]{2,1,0:T(8,128)(2,1)}, u32[]{:S(2)}, u32[]{:S(2)}) async-start(bf16[8,128,4992]{2,1,0:T(8,128)(2,1)} %pad_maximum_fusion), calls=%async_computation | async-start | bytes 20447232 | tf_op jit(solution)/shard_map/all_to_all | solution.py:62
  21.4 139.0 %all-to-all-done = bf16[8,128,4992]{2,1,0:T(8,128)(2,1)} async-done(((bf16[8,128,4992]{2,1,0:T(8,128)(2,1)}), bf16[8,128,4992]{2,1,0:T(8,128)(2,1)}, u32[]{:S(2)}, u32[]{:S(2)}) %all-to-all-start) | async-done | bytes 10223648 | tf_op jit(solution)/shard_map/all_to_all | solution.py:62
  160.4 2.2 fusion.17
  163.1 5.0 %fusion.5 = f32[288,4096]{1,0:T(8,128)S(1)} fusion(bf16[8,128,4992]{2,1,0:T(8,128)(2,1)} %all-to-all-done, bf16[288,8,128]{2,1,0:T(8,128)(2,1)S(1)} %bitcast.101), kind=kOutput, calls=%fused_computation.6 | convolution fusion | flops 2415919104 | bytes 13697024 | tf_op jit(solution)/shard_map/mpt,ptd->md/dot_general | solution.py:79
  168.2 0.3 fusion.15
  168.5 0.3 copy.27
  168.7 1.8 constant_dynamic-slice_fusion.3
  170.6 5.3 %collective-permute-start.2 = (f32[8,3,32,128]{3,2,1,0:T(8,128)S(1)}, f32[8,3,32,128]{3,2,1,0:T(8,128)}, u32[]{:S(2)}, u32[]{:S(2)}) collective-permute-start(f32[8,3,32,128]{3,2,1,0:T(8,128)S(1)} %bitcast.102), channel_id=1, source_target_pairs={{0,24},{8,16},{16,8},{24,0},{32,56},{40,48},{48,40},{56,32},{64,88... | collective-permute-start | bytes 1179656 | tf_op jit(solution)/shard_map/ppermute | solution.py:31
  176.1 0.8 copy.36
  176.9 0.4 collective-permute-start
  177.3 12.2 %convert_bitcast_fusion = bf16[128,8,896]{2,0,1:T(8,128)(2,1)} fusion(bf16[896,4096]{1,0:T(8,128)(2,1)S(1)} %bitcast.105, bf16[8,128,4992]{2,1,0:T(8,128)(2,1)} %all-to-all-done), kind=kOutput, calls=%fused_computation.9 | convolution fusion | flops 7517110272 | bytes 17563648 | tf_op jit(solution)/shard_map/ptd,hd->tph/dot_general | solution.py:65
  189.5 3.7 %all-to-all-start.1 = ((bf16[128,8,896]{2,0,1:T(8,128)(2,1)}), bf16[128,8,896]{2,0,1:T(8,128)(2,1)S(1)}, u32[]{:S(2)}, u32[]{:S(2)}) async-start(bf16[128,8,896]{2,0,1:T(8,128)(2,1)} %convert_bitcast_fusion), calls=%async_computation.1 | async-start | bytes 3670016 | tf_op jit(solution)/shard_map/all_to_all | solution.py:68
  193.3 0.5 collective-permute-done.1
  193.8 1.4 fusion.25
  195.3 5.7 %collective-permute-start.9 = (f32[3,32,128]{2,1,0:T(8,128)S(1)}, f32[3,32,128]{2,1,0:T(8,128)S(1)}, u32[]{:S(2)}, u32[]{:S(2)}) collective-permute-start(f32[3,32,128]{2,1,0:T(8,128)S(1)} %get-tuple-element.17), channel_id=1, source_target_pairs={{0,224},{8,232},{16,240},{24,248},{32,192},{40,200},{48,208},{56,2... | collective-permute-start | bytes 147464 | tf_op jit(solution)/shard_map/ppermute | solution.py:36
  201.0 0.6 collective-permute-start.8
  201.5 3.5 %collective-permute-start.7 = (f32[3,32,128]{2,1,0:T(8,128)S(1)}, f32[3,32,128]{2,1,0:T(8,128)S(1)}, u32[]{:S(2)}, u32[]{:S(2)}) collective-permute-start(f32[3,32,128]{2,1,0:T(8,128)S(1)} %get-tuple-element.19), channel_id=1, source_target_pairs={{0,160},{8,168},{16,176},{24,184},{32,128},{40,136},{48,144},{56,1... | collective-permute-start | bytes 147464 | tf_op jit(solution)/shard_map/ppermute | solution.py:36
  205.0 1.8 collective-permute-start.6
  206.8 1.6 collective-permute-start.5
  208.5 1.9 collective-permute-start.3
  210.4 2.0 collective-permute-done.6
  212.4 3.6 %collective-permute-done.4 = f32[3,32,128]{2,1,0:T(8,128)S(1)} collective-permute-done((f32[3,32,128]{2,1,0:T(8,128)S(1)}, f32[3,32,128]{2,1,0:T(8,128)S(1)}, u32[]{:S(2)}, u32[]{:S(2)}) %collective-permute-start.4) | collective-permute-done | bytes 49184 | tf_op jit(solution)/shard_map/ppermute | solution.py:36
  216.1 0.4 fusion.16
  216.5 1.0 copy.25
  217.4 1.0 fusion.20
  218.5 2.6 %all-to-all-done.1 = bf16[128,8,896]{2,0,1:T(8,128)(2,1)S(1)} async-done(((bf16[128,8,896]{2,0,1:T(8,128)(2,1)}), bf16[128,8,896]{2,0,1:T(8,128)(2,1)S(1)}, u32[]{:S(2)}, u32[]{:S(2)}) %all-to-all-start.1) | async-done | bytes 1835040 | tf_op jit(solution)/shard_map/all_to_all | solution.py:68
  221.1 2.4 %copy.17 = bf16[128,8,896]{0,2,1:T(8,128)(2,1)} copy(bf16[128,8,896]{2,0,1:T(8,128)(2,1)S(1)} %all-to-all-done.1) | data formatting | bytes 3670016 | tf_op jit(solution)/shard_map/all_to_all | solution.py:68
  223.5 3.9 %copy.24 = bf16[128,7168]{1,0:T(8,128)(2,1)} copy(bf16[128,7168]{0,1:T(8,128)(2,1)} %bitcast.96) | data formatting | bytes 3670016
  (33 shorter events, 1.0 us)
Async XLA Ops:
  0.6 159.7 %copy-start = (bf16[3,32,896]{2,1,0:T(8,128)(2,1)S(1)}, bf16[3,32,896]{2,1,0:T(8,128)(2,1)}, u32[]{:S(2)}) copy-start(bf16[3,32,896]{2,1,0:T(8,128)(2,1)} %param.9) | copy-start | bytes 516100
  0.6 7.0 %copy-start.1 = (bf16[128,4096]{1,0:T(8,128)(2,1)S(1)}, bf16[128,4096]{1,0:T(8,128)(2,1)}, u32[]{:S(2)}) copy-start(bf16[128,4096]{1,0:T(8,128)(2,1)} %param.7) | copy-start | bytes 3145732
  15.5 144.8 %all-to-all-start = ((bf16[8,128,4992]{2,1,0:T(8,128)(2,1)}), bf16[8,128,4992]{2,1,0:T(8,128)(2,1)}, u32[]{:S(2)}, u32[]{:S(2)}) async-start(bf16[8,128,4992]{2,1,0:T(8,128)(2,1)} %pad_maximum_fusion), calls=%async_computation | async-start | bytes 20447232 | tf_op jit(solution)/shard_map/all_to_all | solution.py:62
  168.2 9.1 %slice-start = ((s8[7340032]{0:T(1024)(128)(4,1)}), s8[4194304]{0:T(1024)(128)(4,1)S(1)}, s32[]{:S(2)}) async-start(s8[7340032]{0:T(1024)(128)(4,1)} %bitcast.104), calls=%async_computation.2 | async-start | bytes 8388608
  168.5 8.8 %slice-start.1 = ((s8[7340032]{0:T(1024)(128)(4,1)}), s8[3145728]{0:T(1024)(128)(4,1)S(1)}, s32[]{:S(2)}) async-start(s8[7340032]{0:T(1024)(128)(4,1)} %bitcast.104), calls=%async_computation.3 | async-start | bytes 6291456
  170.6 22.7 %collective-permute-start.2 = (f32[8,3,32,128]{3,2,1,0:T(8,128)S(1)}, f32[8,3,32,128]{3,2,1,0:T(8,128)}, u32[]{:S(2)}, u32[]{:S(2)}) collective-permute-start(f32[8,3,32,128]{3,2,1,0:T(8,128)S(1)} %bitcast.102), channel_id=1, source_target_pairs={{0,24},{8,16},{16,8},{24,0},{32,56},{40,48},{48,40},{56,32},{64,88... | collective-permute-start | bytes 1179656 | tf_op jit(solution)/shard_map/ppermute | solution.py:31
  175.9 17.9 %collective-permute-start.1 = (f32[8,3,32,128]{3,2,1,0:T(8,128)S(1)}, f32[8,3,32,128]{3,2,1,0:T(8,128)}, u32[]{:S(2)}, u32[]{:S(2)}) collective-permute-start(f32[8,3,32,128]{3,2,1,0:T(8,128)S(1)} %bitcast.103), channel_id=1, source_target_pairs={{0,16},{8,24},{16,0},{24,8},{32,48},{40,56},{48,32},{56,40},{64,80... | collective-permute-start | bytes 1179656 | tf_op jit(solution)/shard_map/ppermute | solution.py:31
  176.9 16.9 %collective-permute-start = (f32[8,3,32,128]{3,2,1,0:T(8,128)}, f32[8,3,32,128]{3,2,1,0:T(8,128)}, u32[]{:S(2)}, u32[]{:S(2)}) collective-permute-start(f32[8,3,32,128]{3,2,1,0:T(8,128)} %bitcast.93), channel_id=1, source_target_pairs={{0,8},{8,0},{16,24},{24,16},{32,40},{40,32},{48,56},{56,48},{64,72... | collective-permute-start | bytes 1179656 | tf_op jit(solution)/shard_map/ppermute | solution.py:31
  189.5 26.5 %copy-start.4 = (f32[1,3,32,128]{3,2,1,0:T(8,128)S(1)}, f32[1,3,32,128]{3,2,1,0:T(8,128)}, u32[]{:S(2)}) copy-start(f32[1,3,32,128]{3,2,1,0:T(8,128)} %param.10) | copy-start | bytes 147460
  189.5 26.6 %copy-start.3 = (f32[1,3,32,128]{3,2,1,0:T(8,128)S(1)}, f32[1,3,32,128]{3,2,1,0:T(8,128)}, u32[]{:S(2)}) copy-start(f32[1,3,32,128]{3,2,1,0:T(8,128)} %param.11) | copy-start | bytes 147460
  189.5 31.6 %all-to-all-start.1 = ((bf16[128,8,896]{2,0,1:T(8,128)(2,1)}), bf16[128,8,896]{2,0,1:T(8,128)(2,1)S(1)}, u32[]{:S(2)}, u32[]{:S(2)}) async-start(bf16[128,8,896]{2,0,1:T(8,128)(2,1)} %convert_bitcast_fusion), calls=%async_computation.1 | async-start | bytes 3670016 | tf_op jit(solution)/shard_map/all_to_all | solution.py:68
  195.3 13.2 %collective-permute-start.9 = (f32[3,32,128]{2,1,0:T(8,128)S(1)}, f32[3,32,128]{2,1,0:T(8,128)S(1)}, u32[]{:S(2)}, u32[]{:S(2)}) collective-permute-start(f32[3,32,128]{2,1,0:T(8,128)S(1)} %get-tuple-element.17), channel_id=1, source_target_pairs={{0,224},{8,232},{16,240},{24,248},{32,192},{40,200},{48,208},{56,2... | collective-permute-start | bytes 147464 | tf_op jit(solution)/shard_map/ppermute | solution.py:36
  201.0 7.5 %collective-permute-start.8 = (f32[3,32,128]{2,1,0:T(8,128)S(1)}, f32[3,32,128]{2,1,0:T(8,128)S(1)}, u32[]{:S(2)}, u32[]{:S(2)}) collective-permute-start(f32[3,32,128]{2,1,0:T(8,128)S(1)} %get-tuple-element.18), channel_id=1, source_target_pairs={{0,192},{8,200},{16,208},{24,216},{32,224},{40,232},{48,240},{56,2... | collective-permute-start | bytes 147464 | tf_op jit(solution)/shard_map/ppermute | solution.py:36
  201.5 8.8 %collective-permute-start.7 = (f32[3,32,128]{2,1,0:T(8,128)S(1)}, f32[3,32,128]{2,1,0:T(8,128)S(1)}, u32[]{:S(2)}, u32[]{:S(2)}) collective-permute-start(f32[3,32,128]{2,1,0:T(8,128)S(1)} %get-tuple-element.19), channel_id=1, source_target_pairs={{0,160},{8,168},{16,176},{24,184},{32,128},{40,136},{48,144},{56,1... | collective-permute-start | bytes 147464 | tf_op jit(solution)/shard_map/ppermute | solution.py:36
  205.0 7.4 %collective-permute-start.6 = (f32[3,32,128]{2,1,0:T(8,128)S(1)}, f32[3,32,128]{2,1,0:T(8,128)S(1)}, u32[]{:S(2)}, u32[]{:S(2)}) collective-permute-start(f32[3,32,128]{2,1,0:T(8,128)S(1)} %get-tuple-element.20), channel_id=1, source_target_pairs={{0,128},{8,136},{16,144},{24,152},{32,160},{40,168},{48,176},{56,1... | collective-permute-start | bytes 147464 | tf_op jit(solution)/shard_map/ppermute | solution.py:36
  206.8 5.6 %collective-permute-start.5 = (f32[3,32,128]{2,1,0:T(8,128)S(1)}, f32[3,32,128]{2,1,0:T(8,128)S(1)}, u32[]{:S(2)}, u32[]{:S(2)}) collective-permute-start(f32[3,32,128]{2,1,0:T(8,128)S(1)} %get-tuple-element.21), channel_id=1, source_target_pairs={{0,96},{8,104},{16,112},{24,120},{32,64},{40,72},{48,80},{56,88},{... | collective-permute-start | bytes 147464 | tf_op jit(solution)/shard_map/ppermute | solution.py:36
  208.4 7.5 %collective-permute-start.4 = (f32[3,32,128]{2,1,0:T(8,128)S(1)}, f32[3,32,128]{2,1,0:T(8,128)S(1)}, u32[]{:S(2)}, u32[]{:S(2)}) collective-permute-start(f32[3,32,128]{2,1,0:T(8,128)S(1)} %get-tuple-element.22), channel_id=1, source_target_pairs={{0,64},{8,72},{16,80},{24,88},{32,96},{40,104},{48,112},{56,120},{... | collective-permute-start | bytes 147464 | tf_op jit(solution)/shard_map/ppermute | solution.py:36
  208.5 7.5 %collective-permute-start.3 = (f32[3,32,128]{2,1,0:T(8,128)S(1)}, f32[3,32,128]{2,1,0:T(8,128)S(1)}, u32[]{:S(2)}, u32[]{:S(2)}) collective-permute-start(f32[3,32,128]{2,1,0:T(8,128)S(1)} %get-tuple-element.16), channel_id=1, source_target_pairs={{0,32},{8,40},{16,48},{24,56},{32,0},{40,8},{48,16},{56,24},{64,96... | collective-permute-start | bytes 147464 | tf_op jit(solution)/shard_map/ppermute | solution.py:36
  216.0 11.3 %copy-start.2 = (f32[1,3,32,128]{3,2,1,0:T(8,128)}, f32[1,3,32,128]{3,2,1,0:T(8,128)S(1)}, u32[]{:S(2)}) copy-start(f32[1,3,32,128]{3,2,1,0:T(8,128)S(1)} %bitcast_add_fusion.1) | copy-start | bytes 147460

commit v9 on v8

--- a/solution.py
+++ b/solution.py
@@ -69,6 +69,9 @@
         partial_grads, "fsdp", split_axis=1, concat_axis=1, tiled=True
     ).reshape(tok_rows, shards * shard_rows)
 
+    partial_grads, arrived = lax.optimization_barrier((partial_grads, arrived))
+    gathered = arrived[:, :, :model_width]
+    hidden_cols = arrived[:, :, model_width:]
     projected = jnp.einsum(
         "ki,pti->kpt",
         hash_tiles.reshape(sketch_rows, shard_rows),

time: 228 us -> 254 us (1.11)
  waiting for transfers between devices: 148 us -> 172 us
    ppermute x3, waiting for transfers between devices: 0.54 us -> 27.6 us  [grouped_scatter(): lax.ppermute(send, 'rep', [(j, j ^ mask) for j in range(replicas)])]
    all_to_all x1, waiting for transfers between devices: 2.58 us -> 0.01 us  [on_device(): lax.all_to_all(partial_grads, 'fsdp', split_axis=1, concat_axis=1, tiled=...]
    unnamed x19 -> x15, local copies, waits for them, and re-layouts: 9.23 us -> 9.22 us
  transfers between devices with their start and end apart: 12 -> 12, of which waited for: 5 -> 5; matrix products, arithmetic and copies ran while one was open for 7% -> 2% of each run, Pallas kernels for 0% -> 0%
where the time goes in v9:
time: 254 us; the launch traced here: 253 us
  waiting for transfers between devices  172 us (68%)
  starting transfers between devices  30.4 us (12%)
  matrix products  23 us (9%)
  local copies, waits for them, and re-layouts  18.7 us (7%)
  other arithmetic  8.81 us (3%)
    all_to_all x1, waiting for transfers between devices, on_device(): lax.all_to_all(outgoing, 'fsdp', split_axis=0, concat_axis=0, tiled=True)  139 us
    ppermute x3, waiting for transfers between devices, grouped_scatter(): lax.ppermute(send, 'rep', [(j, j ^ mask) for j in range(replicas)])  27.6 us
    ppermute x7, starting transfers between devices, grouped_scatter(): lax.ppermute(send, 'rep', [(j, j ^ mask * inner) for j in range(replicas)])  15.1 us
    dot_general x1, matrix products, on_device(): jnp.einsum('ptd,hd->tph', gathered, down_weight, preferred_element_type=j...  14.3 us
    unnamed x15, local copies, waits for them, and re-layouts  9.22 us
    concatenate x1, other arithmetic, on_device(): jnp.concatenate([jnp.broadcast_to(grad_out[None], (shards, tok_rows, mode...  6.93 us
    all_to_all x1, starting transfers between devices, on_device(): lax.all_to_all(outgoing, 'fsdp', split_axis=0, concat_axis=0, tiled=True)  5.86 us
    ppermute x3, starting transfers between devices, grouped_scatter(): lax.ppermute(send, 'rep', [(j, j ^ mask) for j in range(replicas)])  5.82 us
  transfers between devices with their start and end apart: 12, of which 5 were waited for; matrix products, arithmetic and copies ran while one was open for 2% of the time, Pallas kernels for 0%

profile of v9, /device:TPU:1, one launch (start us, length us, event | category | flops | bytes accessed | tf_op | source)
XLA Modules:
  0.0 253.4 jit_solution(3017054490179555562)
XLA Ops:
  0.7 4.0 %copy.15 = bf16[128,7168]{0,1:T(8,128)(2,1)} copy(bf16[128,7168]{1,0:T(8,128)(2,1)} %param.6) | data formatting | bytes 3670016 | tf_op args[0]
  4.6 3.1 %copy.16 = bf16[128,8,896]{2,0,1:T(8,128)(2,1)S(1)} copy(bf16[128,8,896]{0,2,1:T(8,128)(2,1)} %bitcast.97) | data formatting | bytes 3670016 | tf_op jit(solution)/shard_map/reshape | solution.py:58
  7.7 1.0 broadcast_in_dim.12
  8.7 6.9 %pad_maximum_fusion = bf16[8,128,4992]{2,1,0:T(8,128)(2,1)} fusion(bf16[8,128,896]{2,1,0:T(8,128)(2,1)S(1)} %bitcast.95, bf16[8,128,4096]{2,1,0:T(8,128)(2,1)S(1)} %broadcast_in_dim.12), kind=kLoop, calls=%fused_computation | loop fusion | flops 20447232 | bytes 20447232 | tf_op jit(solution)/shard_map/concatenate | solution.py:55
  15.7 5.9 %all-to-all-start = ((bf16[8,128,4992]{2,1,0:T(8,128)(2,1)}), bf16[8,128,4992]{2,1,0:T(8,128)(2,1)}, u32[]{:S(2)}, u32[]{:S(2)}) async-start(bf16[8,128,4992]{2,1,0:T(8,128)(2,1)} %pad_maximum_fusion), calls=%async_computation | async-start | bytes 20447232 | tf_op jit(solution)/shard_map/all_to_all | solution.py:62
  21.5 139.0 %all-to-all-done = bf16[8,128,4992]{2,1,0:T(8,128)(2,1)} async-done(((bf16[8,128,4992]{2,1,0:T(8,128)(2,1)}), bf16[8,128,4992]{2,1,0:T(8,128)(2,1)}, u32[]{:S(2)}, u32[]{:S(2)}) %all-to-all-start) | async-done | bytes 10223648 | tf_op jit(solution)/shard_map/all_to_all | solution.py:62
  160.5 14.3 %convert_bitcast_fusion = bf16[128,8,896]{2,0,1:T(8,128)(2,1)} fusion(bf16[896,4096]{1,0:T(8,128)(2,1)} %param.8, bf16[8,128,4992]{2,1,0:T(8,128)(2,1)} %all-to-all-done), kind=kOutput, calls=%fused_computation.9 | convolution fusion | flops 7517110272 | bytes 17563648 | tf_op jit(solution)/shard_map/ptd,hd->tph/dot_general | solution.py:65
  174.8 2.2 fusion.17
  177.6 5.0 %fusion.5 = f32[288,4096]{1,0:T(8,128)S(1)} fusion(bf16[8,128,4992]{2,1,0:T(8,128)(2,1)} %all-to-all-done, bf16[288,8,128]{2,1,0:T(8,128)(2,1)S(1)} %bitcast.101), kind=kOutput, calls=%fused_computation.6 | convolution fusion | flops 2415919104 | bytes 13697024 | tf_op jit(solution)/shard_map/mpt,ptd->md/dot_general | solution.py:82
  182.6 0.3 fusion.15
  182.9 0.3 copy.27
  183.2 1.7 constant_dynamic-slice_fusion.3
  185.0 5.3 %collective-permute-start.2 = (f32[8,3,32,128]{3,2,1,0:T(8,128)S(1)}, f32[8,3,32,128]{3,2,1,0:T(8,128)}, u32[]{:S(2)}, u32[]{:S(2)}) collective-permute-start(f32[8,3,32,128]{3,2,1,0:T(8,128)S(1)} %bitcast.102), channel_id=1, source_target_pairs={{0,24},{8,16},{16,8},{24,0},{32,56},{40,48},{48,40},{56,32},{64,88... | collective-permute-start | bytes 1179656 | tf_op jit(solution)/shard_map/ppermute | solution.py:31
  190.5 0.8 copy.36
  191.3 0.4 collective-permute-start
  191.7 3.6 %all-to-all-start.1 = ((bf16[128,8,896]{2,0,1:T(8,128)(2,1)}), bf16[128,8,896]{2,0,1:T(8,128)(2,1)S(1)}, u32[]{:S(2)}, u32[]{:S(2)}) async-start(bf16[128,8,896]{2,0,1:T(8,128)(2,1)} %convert_bitcast_fusion), calls=%async_computation.1 | async-start | bytes 3670016 | tf_op jit(solution)/shard_map/all_to_all | solution.py:68
  195.4 13.6 %collective-permute-done.2 = f32[8,3,32,128]{3,2,1,0:T(8,128)} collective-permute-done((f32[8,3,32,128]{3,2,1,0:T(8,128)S(1)}, f32[8,3,32,128]{3,2,1,0:T(8,128)}, u32[]{:S(2)}, u32[]{:S(2)}) %collective-permute-start.2) | collective-permute-done | bytes 393248 | tf_op jit(solution)/shard_map/ppermute | solution.py:31
  209.0 14.0 %collective-permute-done.1 = f32[8,3,32,128]{3,2,1,0:T(8,128)} collective-permute-done((f32[8,3,32,128]{3,2,1,0:T(8,128)S(1)}, f32[8,3,32,128]{3,2,1,0:T(8,128)}, u32[]{:S(2)}, u32[]{:S(2)}) %collective-permute-start.1) | collective-permute-done | bytes 393248 | tf_op jit(solution)/shard_map/ppermute | solution.py:31
  222.9 1.4 fusion.25
  224.4 5.7 %collective-permute-start.9 = (f32[3,32,128]{2,1,0:T(8,128)S(1)}, f32[3,32,128]{2,1,0:T(8,128)S(1)}, u32[]{:S(2)}, u32[]{:S(2)}) collective-permute-start(f32[3,32,128]{2,1,0:T(8,128)S(1)} %get-tuple-element.19), channel_id=1, source_target_pairs={{0,224},{8,232},{16,240},{24,248},{32,192},{40,200},{48,208},{56,2... | collective-permute-start | bytes 147464 | tf_op jit(solution)/shard_map/ppermute | solution.py:36
  230.2 0.5 collective-permute-start.8
  230.7 3.5 %collective-permute-start.7 = (f32[3,32,128]{2,1,0:T(8,128)S(1)}, f32[3,32,128]{2,1,0:T(8,128)S(1)}, u32[]{:S(2)}, u32[]{:S(2)}) collective-permute-start(f32[3,32,128]{2,1,0:T(8,128)S(1)} %get-tuple-element.21), channel_id=1, source_target_pairs={{0,160},{8,168},{16,176},{24,184},{32,128},{40,136},{48,144},{56,1... | collective-permute-start | bytes 147464 | tf_op jit(solution)/shard_map/ppermute | solution.py:36
  234.2 1.8 collective-permute-start.6
  236.0 1.6 collective-permute-start.5
  237.6 1.9 collective-permute-start.3
  239.5 1.8 collective-permute-done.6
  241.3 3.3 %collective-permute-done.4 = f32[3,32,128]{2,1,0:T(8,128)S(1)} collective-permute-done((f32[3,32,128]{2,1,0:T(8,128)S(1)}, f32[3,32,128]{2,1,0:T(8,128)S(1)}, u32[]{:S(2)}, u32[]{:S(2)}) %collective-permute-start.4) | collective-permute-done | bytes 49184 | tf_op jit(solution)/shard_map/ppermute | solution.py:36
  244.7 0.4 fusion.16
  245.1 1.0 copy.25
  246.0 1.0 fusion.20
  247.1 2.4 copy.17
  249.5 3.9 %copy.24 = bf16[128,7168]{1,0:T(8,128)(2,1)} copy(bf16[128,7168]{0,1:T(8,128)(2,1)} %bitcast.96) | data formatting | bytes 3670016
  (28 shorter events, 1.0 us)
Async XLA Ops:
  0.6 174.2 %copy-start = (bf16[3,32,896]{2,1,0:T(8,128)(2,1)S(1)}, bf16[3,32,896]{2,1,0:T(8,128)(2,1)}, u32[]{:S(2)}) copy-start(bf16[3,32,896]{2,1,0:T(8,128)(2,1)} %param.9) | copy-start | bytes 516100
  0.6 7.0 %copy-start.1 = (bf16[128,4096]{1,0:T(8,128)(2,1)S(1)}, bf16[128,4096]{1,0:T(8,128)(2,1)}, u32[]{:S(2)}) copy-start(bf16[128,4096]{1,0:T(8,128)(2,1)} %param.7) | copy-start | bytes 3145732
  15.7 144.8 %all-to-all-start = ((bf16[8,128,4992]{2,1,0:T(8,128)(2,1)}), bf16[8,128,4992]{2,1,0:T(8,128)(2,1)}, u32[]{:S(2)}, u32[]{:S(2)}) async-start(bf16[8,128,4992]{2,1,0:T(8,128)(2,1)} %pad_maximum_fusion), calls=%async_computation | async-start | bytes 20447232 | tf_op jit(solution)/shard_map/all_to_all | solution.py:62
  184.9 59.7 %copy-start.4 = (f32[1,3,32,128]{3,2,1,0:T(8,128)S(1)}, f32[1,3,32,128]{3,2,1,0:T(8,128)}, u32[]{:S(2)}) copy-start(f32[1,3,32,128]{3,2,1,0:T(8,128)} %param.10) | copy-start | bytes 147460
  184.9 59.8 %copy-start.3 = (f32[1,3,32,128]{3,2,1,0:T(8,128)S(1)}, f32[1,3,32,128]{3,2,1,0:T(8,128)}, u32[]{:S(2)}) copy-start(f32[1,3,32,128]{3,2,1,0:T(8,128)} %param.11) | copy-start | bytes 147460
  185.0 24.0 %collective-permute-start.2 = (f32[8,3,32,128]{3,2,1,0:T(8,128)S(1)}, f32[8,3,32,128]{3,2,1,0:T(8,128)}, u32[]{:S(2)}, u32[]{:S(2)}) collective-permute-start(f32[8,3,32,128]{3,2,1,0:T(8,128)S(1)} %bitcast.102), channel_id=1, source_target_pairs={{0,24},{8,16},{16,8},{24,0},{32,56},{40,48},{48,40},{56,32},{64,88... | collective-permute-start | bytes 1179656 | tf_op jit(solution)/shard_map/ppermute | solution.py:31
  190.3 32.6 %collective-permute-start.1 = (f32[8,3,32,128]{3,2,1,0:T(8,128)S(1)}, f32[8,3,32,128]{3,2,1,0:T(8,128)}, u32[]{:S(2)}, u32[]{:S(2)}) collective-permute-start(f32[8,3,32,128]{3,2,1,0:T(8,128)S(1)} %bitcast.103), channel_id=1, source_target_pairs={{0,16},{8,24},{16,0},{24,8},{32,48},{40,56},{48,32},{56,40},{64,80... | collective-permute-start | bytes 1179656 | tf_op jit(solution)/shard_map/ppermute | solution.py:31
  191.3 31.7 %collective-permute-start = (f32[8,3,32,128]{3,2,1,0:T(8,128)}, f32[8,3,32,128]{3,2,1,0:T(8,128)}, u32[]{:S(2)}, u32[]{:S(2)}) collective-permute-start(f32[8,3,32,128]{3,2,1,0:T(8,128)} %bitcast.93), channel_id=1, source_target_pairs={{0,8},{8,0},{16,24},{24,16},{32,40},{40,32},{48,56},{56,48},{64,72... | collective-permute-start | bytes 1179656 | tf_op jit(solution)/shard_map/ppermute | solution.py:31
  191.7 55.4 %all-to-all-start.1 = ((bf16[128,8,896]{2,0,1:T(8,128)(2,1)}), bf16[128,8,896]{2,0,1:T(8,128)(2,1)S(1)}, u32[]{:S(2)}, u32[]{:S(2)}) async-start(bf16[128,8,896]{2,0,1:T(8,128)(2,1)} %convert_bitcast_fusion), calls=%async_computation.1 | async-start | bytes 3670016 | tf_op jit(solution)/shard_map/all_to_all | solution.py:68
  224.4 13.2 %collective-permute-start.9 = (f32[3,32,128]{2,1,0:T(8,128)S(1)}, f32[3,32,128]{2,1,0:T(8,128)S(1)}, u32[]{:S(2)}, u32[]{:S(2)}) collective-permute-start(f32[3,32,128]{2,1,0:T(8,128)S(1)} %get-tuple-element.19), channel_id=1, source_target_pairs={{0,224},{8,232},{16,240},{24,248},{32,192},{40,200},{48,208},{56,2... | collective-permute-start | bytes 147464 | tf_op jit(solution)/shard_map/ppermute | solution.py:36
  230.2 7.5 %collective-permute-start.8 = (f32[3,32,128]{2,1,0:T(8,128)S(1)}, f32[3,32,128]{2,1,0:T(8,128)S(1)}, u32[]{:S(2)}, u32[]{:S(2)}) collective-permute-start(f32[3,32,128]{2,1,0:T(8,128)S(1)} %get-tuple-element.20), channel_id=1, source_target_pairs={{0,192},{8,200},{16,208},{24,216},{32,224},{40,232},{48,240},{56,2... | collective-permute-start | bytes 147464 | tf_op jit(solution)/shard_map/ppermute | solution.py:36
  230.7 8.8 %collective-permute-start.7 = (f32[3,32,128]{2,1,0:T(8,128)S(1)}, f32[3,32,128]{2,1,0:T(8,128)S(1)}, u32[]{:S(2)}, u32[]{:S(2)}) collective-permute-start(f32[3,32,128]{2,1,0:T(8,128)S(1)} %get-tuple-element.21), channel_id=1, source_target_pairs={{0,160},{8,168},{16,176},{24,184},{32,128},{40,136},{48,144},{56,1... | collective-permute-start | bytes 147464 | tf_op jit(solution)/shard_map/ppermute | solution.py:36
  234.2 7.2 %collective-permute-start.6 = (f32[3,32,128]{2,1,0:T(8,128)S(1)}, f32[3,32,128]{2,1,0:T(8,128)S(1)}, u32[]{:S(2)}, u32[]{:S(2)}) collective-permute-start(f32[3,32,128]{2,1,0:T(8,128)S(1)} %get-tuple-element.22), channel_id=1, source_target_pairs={{0,128},{8,136},{16,144},{24,152},{32,160},{40,168},{48,176},{56,1... | collective-permute-start | bytes 147464 | tf_op jit(solution)/shard_map/ppermute | solution.py:36
  236.0 5.4 %collective-permute-start.5 = (f32[3,32,128]{2,1,0:T(8,128)S(1)}, f32[3,32,128]{2,1,0:T(8,128)S(1)}, u32[]{:S(2)}, u32[]{:S(2)}) collective-permute-start(f32[3,32,128]{2,1,0:T(8,128)S(1)} %get-tuple-element.23), channel_id=1, source_target_pairs={{0,96},{8,104},{16,112},{24,120},{32,64},{40,72},{48,80},{56,88},{... | collective-permute-start | bytes 147464 | tf_op jit(solution)/shard_map/ppermute | solution.py:36
  237.6 7.0 %collective-permute-start.4 = (f32[3,32,128]{2,1,0:T(8,128)S(1)}, f32[3,32,128]{2,1,0:T(8,128)S(1)}, u32[]{:S(2)}, u32[]{:S(2)}) collective-permute-start(f32[3,32,128]{2,1,0:T(8,128)S(1)} %get-tuple-element.24), channel_id=1, source_target_pairs={{0,64},{8,72},{16,80},{24,88},{32,96},{40,104},{48,112},{56,120},{... | collective-permute-start | bytes 147464 | tf_op jit(solution)/shard_map/ppermute | solution.py:36
  237.6 7.0 %collective-permute-start.3 = (f32[3,32,128]{2,1,0:T(8,128)S(1)}, f32[3,32,128]{2,1,0:T(8,128)S(1)}, u32[]{:S(2)}, u32[]{:S(2)}) collective-permute-start(f32[3,32,128]{2,1,0:T(8,128)S(1)} %get-tuple-element.18), channel_id=1, source_target_pairs={{0,32},{8,40},{16,48},{24,56},{32,0},{40,8},{48,16},{56,24},{64,96... | collective-permute-start | bytes 147464 | tf_op jit(solution)/shard_map/ppermute | solution.py:36
  244.6 8.7 %copy-start.2 = (f32[1,3,32,128]{3,2,1,0:T(8,128)}, f32[1,3,32,128]{3,2,1,0:T(8,128)S(1)}, u32[]{:S(2)}) copy-start(f32[1,3,32,128]{3,2,1,0:T(8,128)S(1)} %bitcast_add_fusion.1) | copy-start | bytes 147460

commit v10 on v8

--- a/solution.py
+++ b/solution.py
@@ -24,16 +24,16 @@
     outer = replicas // inner
     rest = blocks.shape[1:]
     data = blocks.reshape((outer, inner) + rest)
+    high = me // inner
+    kept = lax.dynamic_index_in_dim(data, high, axis=0, keepdims=False)
+    for mask in range(1, outer):
+        send = lax.dynamic_index_in_dim(data, high ^ mask, axis=0, keepdims=False)
+        kept = kept + lax.ppermute(send, "rep", [(j, j ^ (mask * inner)) for j in range(replicas)])
     low = me % inner
-    kept = lax.dynamic_index_in_dim(data, low, axis=1, keepdims=False)
+    total = lax.dynamic_index_in_dim(kept, low, axis=0, keepdims=False)
     for mask in range(1, inner):
-        send = lax.dynamic_index_in_dim(data, low ^ mask, axis=1, keepdims=False)
-        kept = kept + lax.ppermute(send, "rep", [(j, j ^ mask) for j in range(replicas)])
-    high = me // inner
-    total = lax.dynamic_index_in_dim(kept, high, axis=0, keepdims=False)
-    for mask in range(1, outer):
-        send = lax.dynamic_index_in_dim(kept, high ^ mask, axis=0, keepdims=False)
-        total = total + lax.ppermute(send, "rep", [(j, j ^ (mask * inner)) for j in range(replicas)])
+        send = lax.dynamic_index_in_dim(kept, low ^ mask, axis=0, keepdims=False)
+        total = total + lax.ppermute(send, "rep", [(j, j ^ mask) for j in range(replicas)])
     return total[None]
 
 

time: 228 us -> 255 us (1.12)
  waiting for transfers between devices: 148 us -> 169 us
    ppermute x7, waiting for transfers between devices: 5.62 us -> 26.2 us  [grouped_scatter(): lax.ppermute(send, 'rep', [(j, j ^ mask * inner) for j in range(replicas)])]
    ppermute x3, waiting for transfers between devices: 0.54 us -> 3.95 us  [grouped_scatter(): lax.ppermute(send, 'rep', [(j, j ^ mask) for j in range(replicas)])]
    all_to_all x1, waiting for transfers between devices: 2.58 us -> 0.01 us  [on_device(): lax.all_to_all(partial_grads, 'fsdp', split_axis=1, concat_axis=1, tiled=...]
    unnamed x19 -> x17, local copies, waits for them, and re-layouts: 9.23 us -> 9.22 us
  transfers between devices with their start and end apart: 12 -> 12, of which waited for: 5 -> 8; matrix products, arithmetic and copies ran while one was open for 7% -> 6% of each run, Pallas kernels for 0% -> 0%
where the time goes in v10:
time: 255 us; the launch traced here: 254 us
  waiting for transfers between devices  169 us (66%)
  starting transfers between devices  32.9 us (13%)
  matrix products  23 us (9%)
  local copies, waits for them, and re-layouts  20 us (8%)
  other arithmetic  8.5 us (3%)
    all_to_all x1, waiting for transfers between devices, on_device(): lax.all_to_all(outgoing, 'fsdp', split_axis=0, concat_axis=0, tiled=True)  139 us
    ppermute x7, waiting for transfers between devices, grouped_scatter(): lax.ppermute(send, 'rep', [(j, j ^ mask * inner) for j in range(replicas)])  26.2 us
    ppermute x7, starting transfers between devices, grouped_scatter(): lax.ppermute(send, 'rep', [(j, j ^ mask * inner) for j in range(replicas)])  17 us
    dot_general x1, matrix products, on_device(): jnp.einsum('ptd,hd->tph', gathered, down_weight, preferred_element_type=j...  14.3 us
    unnamed x17, local copies, waits for them, and re-layouts  9.22 us
    concatenate x1, other arithmetic, on_device(): jnp.concatenate([jnp.broadcast_to(grad_out[None], (shards, tok_rows, mode...  6.87 us
    ppermute x3, starting transfers between devices, grouped_scatter(): lax.ppermute(send, 'rep', [(j, j ^ mask) for j in range(replicas)])  6.52 us
    all_to_all x1, starting transfers between devices, on_device(): lax.all_to_all(outgoing, 'fsdp', split_axis=0, concat_axis=0, tiled=True)  5.86 us
  transfers between devices with their start and end apart: 12, of which 8 were waited for; matrix products, arithmetic and copies ran while one was open for 6% of the time, Pallas kernels for 0%

profile of v10, /device:TPU:1, one launch (start us, length us, event | category | flops | bytes accessed | tf_op | source)
XLA Modules:
  0.0 254.3 jit_solution(4324608364440699194)
XLA Ops:
  0.7 4.0 %copy.19 = bf16[128,7168]{0,1:T(8,128)(2,1)} copy(bf16[128,7168]{1,0:T(8,128)(2,1)} %param.6) | data formatting | bytes 3670016 | tf_op args[0]
  4.6 3.1 %copy.20 = bf16[128,8,896]{2,0,1:T(8,128)(2,1)S(1)} copy(bf16[128,8,896]{0,2,1:T(8,128)(2,1)} %bitcast.101) | data formatting | bytes 3670016 | tf_op jit(solution)/shard_map/reshape | solution.py:58
  7.7 1.0 broadcast_in_dim.12
  8.7 6.9 %pad_maximum_fusion = bf16[8,128,4992]{2,1,0:T(8,128)(2,1)} fusion(bf16[8,128,896]{2,1,0:T(8,128)(2,1)S(1)} %bitcast.99, bf16[8,128,4096]{2,1,0:T(8,128)(2,1)S(1)} %broadcast_in_dim.12), kind=kLoop, calls=%fused_computation | loop fusion | flops 20447232 | bytes 20447232 | tf_op jit(solution)/shard_map/concatenate | solution.py:55
  15.6 5.9 %all-to-all-start = ((bf16[8,128,4992]{2,1,0:T(8,128)(2,1)}), bf16[8,128,4992]{2,1,0:T(8,128)(2,1)}, u32[]{:S(2)}, u32[]{:S(2)}) async-start(bf16[8,128,4992]{2,1,0:T(8,128)(2,1)} %pad_maximum_fusion), calls=%async_computation | async-start | bytes 20447232 | tf_op jit(solution)/shard_map/all_to_all | solution.py:62
  21.5 139.0 %all-to-all-done = bf16[8,128,4992]{2,1,0:T(8,128)(2,1)} async-done(((bf16[8,128,4992]{2,1,0:T(8,128)(2,1)}), bf16[8,128,4992]{2,1,0:T(8,128)(2,1)}, u32[]{:S(2)}, u32[]{:S(2)}) %all-to-all-start) | async-done | bytes 10223648 | tf_op jit(solution)/shard_map/all_to_all | solution.py:62
  160.4 14.3 %convert_bitcast_fusion = bf16[128,8,896]{2,0,1:T(8,128)(2,1)} fusion(bf16[896,4096]{1,0:T(8,128)(2,1)} %param.8, bf16[8,128,4992]{2,1,0:T(8,128)(2,1)} %all-to-all-done), kind=kOutput, calls=%fused_computation.9 | convolution fusion | flops 7517110272 | bytes 17563648 | tf_op jit(solution)/shard_map/ptd,hd->tph/dot_general | solution.py:65
  174.8 3.6 %all-to-all-start.1 = ((bf16[128,8,896]{2,0,1:T(8,128)(2,1)}), bf16[128,8,896]{2,0,1:T(8,128)(2,1)S(1)}, u32[]{:S(2)}, u32[]{:S(2)}) async-start(bf16[128,8,896]{2,0,1:T(8,128)(2,1)} %convert_bitcast_fusion), calls=%async_computation.1 | async-start | bytes 3670016 | tf_op jit(solution)/shard_map/all_to_all | solution.py:68
  178.4 2.2 fusion.17
  181.2 5.0 %fusion.5 = f32[288,4096]{1,0:T(8,128)S(1)} fusion(bf16[8,128,4992]{2,1,0:T(8,128)(2,1)} %all-to-all-done, bf16[288,8,128]{2,1,0:T(8,128)(2,1)S(1)} %bitcast.105), kind=kOutput, calls=%fused_computation.6 | convolution fusion | flops 2415919104 | bytes 13697024 | tf_op jit(solution)/shard_map/mpt,ptd->md/dot_general | solution.py:79
  187.2 6.4 %collective-permute-start.6 = (f32[4,3,32,128]{3,2,1,0:T(8,128)S(1)}, f32[4,3,32,128]{3,2,1,0:T(8,128)S(1)}, u32[]{:S(2)}, u32[]{:S(2)}) collective-permute-start(f32[4,3,32,128]{3,2,1,0:T(8,128)S(1)} %bitcast.107), channel_id=1, source_target_pairs={{0,224},{8,232},{16,240},{24,248},{32,192},{40,200},{48,208},{56,2... | collective-permute-start | bytes 589832 | tf_op jit(solution)/shard_map/ppermute | solution.py:31
  194.2 0.7 copy.48
  194.9 3.5 %collective-permute-start.4 = (f32[4,3,32,128]{3,2,1,0:T(8,128)}, f32[4,3,32,128]{3,2,1,0:T(8,128)S(1)}, u32[]{:S(2)}, u32[]{:S(2)}) collective-permute-start(f32[4,3,32,128]{3,2,1,0:T(8,128)} %bitcast.93), channel_id=1, source_target_pairs={{0,160},{8,168},{16,176},{24,184},{32,128},{40,136},{48,144},{56,1... | collective-permute-start | bytes 589832 | tf_op jit(solution)/shard_map/ppermute | solution.py:31
  198.5 0.7 copy.49
  199.2 1.8 collective-permute-start.3
  201.0 0.7 copy.50
  201.7 1.6 collective-permute-start.2
  204.0 0.7 copy.52
  204.7 9.3 %collective-permute-done.6 = f32[4,3,32,128]{3,2,1,0:T(8,128)S(1)} collective-permute-done((f32[4,3,32,128]{3,2,1,0:T(8,128)S(1)}, f32[4,3,32,128]{3,2,1,0:T(8,128)S(1)}, u32[]{:S(2)}, u32[]{:S(2)}) %collective-permute-start.6) | collective-permute-done | bytes 196640 | tf_op jit(solution)/shard_map/ppermute | solution.py:31
  214.0 8.0 %collective-permute-done.5 = f32[4,3,32,128]{3,2,1,0:T(8,128)S(1)} collective-permute-done((f32[4,3,32,128]{3,2,1,0:T(8,128)S(1)}, f32[4,3,32,128]{3,2,1,0:T(8,128)S(1)}, u32[]{:S(2)}, u32[]{:S(2)}) %collective-permute-start.5) | collective-permute-done | bytes 196640 | tf_op jit(solution)/shard_map/ppermute | solution.py:31
  222.0 3.0 %collective-permute-start = (f32[4,3,32,128]{3,2,1,0:T(8,128)}, f32[4,3,32,128]{3,2,1,0:T(8,128)}, u32[]{:S(2)}, u32[]{:S(2)}) collective-permute-start(f32[4,3,32,128]{3,2,1,0:T(8,128)} %bitcast.97), channel_id=1, source_target_pairs={{0,32},{8,40},{16,48},{24,56},{32,0},{40,8},{48,16},{56,24},{64,96... | collective-permute-start | bytes 589832 | tf_op jit(solution)/shard_map/ppermute | solution.py:31
  225.0 1.5 collective-permute-done.4
  226.5 6.6 %collective-permute-done.1 = f32[4,3,32,128]{3,2,1,0:T(8,128)S(1)} collective-permute-done((f32[4,3,32,128]{3,2,1,0:T(8,128)}, f32[4,3,32,128]{3,2,1,0:T(8,128)S(1)}, u32[]{:S(2)}, u32[]{:S(2)}) %collective-permute-start.1) | collective-permute-done | bytes 196640 | tf_op jit(solution)/shard_map/ppermute | solution.py:31
  233.1 0.8 collective-permute-done
  233.9 1.2 fusion.29
  235.1 6.0 %collective-permute-start.9 = (f32[3,32,128]{2,1,0:T(8,128)S(1)}, f32[3,32,128]{2,1,0:T(8,128)S(1)}, u32[]{:S(2)}, u32[]{:S(2)}) collective-permute-start(f32[3,32,128]{2,1,0:T(8,128)S(1)} %get-tuple-element.24), channel_id=1, source_target_pairs={{0,24},{8,16},{16,8},{24,0},{32,56},{40,48},{48,40},{56,32},{64,88... | collective-permute-start | bytes 147464 | tf_op jit(solution)/shard_map/ppermute | solution.py:36
  241.6 1.4 collective-permute-done.9
  243.0 2.6 %collective-permute-done.8 = f32[3,32,128]{2,1,0:T(8,128)S(1)} collective-permute-done((f32[3,32,128]{2,1,0:T(8,128)S(1)}, f32[3,32,128]{2,1,0:T(8,128)S(1)}, u32[]{:S(2)}, u32[]{:S(2)}) %collective-permute-start.8) | collective-permute-done | bytes 49184 | tf_op jit(solution)/shard_map/ppermute | solution.py:36
  246.0 1.0 copy.33
  247.0 1.0 fusion.20
  248.0 2.4 copy.21
  250.4 3.9 %copy.32 = bf16[128,7168]{1,0:T(8,128)(2,1)} copy(bf16[128,7168]{0,1:T(8,128)(2,1)} %bitcast.100) | data formatting | bytes 3670016
  (34 shorter events, 3.8 us)
Async XLA Ops:
  0.6 177.7 %copy-start = (bf16[3,32,896]{2,1,0:T(8,128)(2,1)S(1)}, bf16[3,32,896]{2,1,0:T(8,128)(2,1)}, u32[]{:S(2)}) copy-start(bf16[3,32,896]{2,1,0:T(8,128)(2,1)} %param.9) | copy-start | bytes 516100
  0.6 7.0 %copy-start.1 = (bf16[128,4096]{1,0:T(8,128)(2,1)S(1)}, bf16[128,4096]{1,0:T(8,128)(2,1)}, u32[]{:S(2)}) copy-start(bf16[128,4096]{1,0:T(8,128)(2,1)} %param.7) | copy-start | bytes 3145732
  15.6 144.8 %all-to-all-start = ((bf16[8,128,4992]{2,1,0:T(8,128)(2,1)}), bf16[8,128,4992]{2,1,0:T(8,128)(2,1)}, u32[]{:S(2)}, u32[]{:S(2)}) async-start(bf16[8,128,4992]{2,1,0:T(8,128)(2,1)} %pad_maximum_fusion), calls=%async_computation | async-start | bytes 20447232 | tf_op jit(solution)/shard_map/all_to_all | solution.py:62
  174.8 73.2 %all-to-all-start.1 = ((bf16[128,8,896]{2,0,1:T(8,128)(2,1)}), bf16[128,8,896]{2,0,1:T(8,128)(2,1)S(1)}, u32[]{:S(2)}, u32[]{:S(2)}) async-start(bf16[128,8,896]{2,0,1:T(8,128)(2,1)} %convert_bitcast_fusion), calls=%async_computation.1 | async-start | bytes 3670016 | tf_op jit(solution)/shard_map/all_to_all | solution.py:68
  186.7 58.8 %copy-start.5 = (f32[1,3,32,128]{3,2,1,0:T(8,128)S(1)}, f32[1,3,32,128]{3,2,1,0:T(8,128)}, u32[]{:S(2)}) copy-start(f32[1,3,32,128]{3,2,1,0:T(8,128)} %param.10) | copy-start | bytes 147460
  186.8 58.8 %copy-start.4 = (f32[1,3,32,128]{3,2,1,0:T(8,128)S(1)}, f32[1,3,32,128]{3,2,1,0:T(8,128)}, u32[]{:S(2)}) copy-start(f32[1,3,32,128]{3,2,1,0:T(8,128)} %param.11) | copy-start | bytes 147460
  187.2 26.8 %collective-permute-start.6 = (f32[4,3,32,128]{3,2,1,0:T(8,128)S(1)}, f32[4,3,32,128]{3,2,1,0:T(8,128)S(1)}, u32[]{:S(2)}, u32[]{:S(2)}) collective-permute-start(f32[4,3,32,128]{3,2,1,0:T(8,128)S(1)} %bitcast.107), channel_id=1, source_target_pairs={{0,224},{8,232},{16,240},{24,248},{32,192},{40,200},{48,208},{56,2... | collective-permute-start | bytes 589832 | tf_op jit(solution)/shard_map/ppermute | solution.py:31
  193.7 28.3 %collective-permute-start.5 = (f32[4,3,32,128]{3,2,1,0:T(8,128)S(1)}, f32[4,3,32,128]{3,2,1,0:T(8,128)S(1)}, u32[]{:S(2)}, u32[]{:S(2)}) collective-permute-start(f32[4,3,32,128]{3,2,1,0:T(8,128)S(1)} %bitcast.106), channel_id=1, source_target_pairs={{0,192},{8,200},{16,208},{24,216},{32,224},{40,232},{48,240},{56,2... | collective-permute-start | bytes 589832 | tf_op jit(solution)/shard_map/ppermute | solution.py:31
  194.9 31.6 %collective-permute-start.4 = (f32[4,3,32,128]{3,2,1,0:T(8,128)}, f32[4,3,32,128]{3,2,1,0:T(8,128)S(1)}, u32[]{:S(2)}, u32[]{:S(2)}) collective-permute-start(f32[4,3,32,128]{3,2,1,0:T(8,128)} %bitcast.93), channel_id=1, source_target_pairs={{0,160},{8,168},{16,176},{24,184},{32,128},{40,136},{48,144},{56,1... | collective-permute-start | bytes 589832 | tf_op jit(solution)/shard_map/ppermute | solution.py:31
  199.2 27.4 %collective-permute-start.3 = (f32[4,3,32,128]{3,2,1,0:T(8,128)}, f32[4,3,32,128]{3,2,1,0:T(8,128)S(1)}, u32[]{:S(2)}, u32[]{:S(2)}) collective-permute-start(f32[4,3,32,128]{3,2,1,0:T(8,128)} %bitcast.94), channel_id=1, source_target_pairs={{0,128},{8,136},{16,144},{24,152},{32,160},{40,168},{48,176},{56,1... | collective-permute-start | bytes 589832 | tf_op jit(solution)/shard_map/ppermute | solution.py:31
  201.7 24.8 %collective-permute-start.2 = (f32[4,3,32,128]{3,2,1,0:T(8,128)}, f32[4,3,32,128]{3,2,1,0:T(8,128)S(1)}, u32[]{:S(2)}, u32[]{:S(2)}) collective-permute-start(f32[4,3,32,128]{3,2,1,0:T(8,128)} %bitcast.95), channel_id=1, source_target_pairs={{0,96},{8,104},{16,112},{24,120},{32,64},{40,72},{48,80},{56,88},{... | collective-permute-start | bytes 589832 | tf_op jit(solution)/shard_map/ppermute | solution.py:31
  214.0 19.1 %collective-permute-start.1 = (f32[4,3,32,128]{3,2,1,0:T(8,128)}, f32[4,3,32,128]{3,2,1,0:T(8,128)S(1)}, u32[]{:S(2)}, u32[]{:S(2)}) collective-permute-start(f32[4,3,32,128]{3,2,1,0:T(8,128)} %bitcast.96), channel_id=1, source_target_pairs={{0,64},{8,72},{16,80},{24,88},{32,96},{40,104},{48,112},{56,120},{... | collective-permute-start | bytes 589832 | tf_op jit(solution)/shard_map/ppermute | solution.py:31
  222.0 11.9 %collective-permute-start = (f32[4,3,32,128]{3,2,1,0:T(8,128)}, f32[4,3,32,128]{3,2,1,0:T(8,128)}, u32[]{:S(2)}, u32[]{:S(2)}) collective-permute-start(f32[4,3,32,128]{3,2,1,0:T(8,128)} %bitcast.97), channel_id=1, source_target_pairs={{0,32},{8,40},{16,48},{24,56},{32,0},{40,8},{48,16},{56,24},{64,96... | collective-permute-start | bytes 589832 | tf_op jit(solution)/shard_map/ppermute | solution.py:31
  233.1 0.8 copy-start.3
  235.1 7.9 %collective-permute-start.9 = (f32[3,32,128]{2,1,0:T(8,128)S(1)}, f32[3,32,128]{2,1,0:T(8,128)S(1)}, u32[]{:S(2)}, u32[]{:S(2)}) collective-permute-start(f32[3,32,128]{2,1,0:T(8,128)S(1)} %get-tuple-element.24), channel_id=1, source_target_pairs={{0,24},{8,16},{16,8},{24,0},{32,56},{40,48},{48,40},{56,32},{64,88... | collective-permute-start | bytes 147464 | tf_op jit(solution)/shard_map/ppermute | solution.py:36
  241.1 4.4 %collective-permute-start.8 = (f32[3,32,128]{2,1,0:T(8,128)S(1)}, f32[3,32,128]{2,1,0:T(8,128)S(1)}, u32[]{:S(2)}, u32[]{:S(2)}) collective-permute-start(f32[3,32,128]{2,1,0:T(8,128)S(1)} %get-tuple-element.25), channel_id=1, source_target_pairs={{0,16},{8,24},{16,0},{24,8},{32,48},{40,56},{48,32},{56,40},{64,80... | collective-permute-start | bytes 147464 | tf_op jit(solution)/shard_map/ppermute | solution.py:36
  241.1 4.4 %collective-permute-start.7 = (f32[3,32,128]{2,1,0:T(8,128)S(1)}, f32[3,32,128]{2,1,0:T(8,128)S(1)}, u32[]{:S(2)}, u32[]{:S(2)}) collective-permute-start(f32[3,32,128]{2,1,0:T(8,128)S(1)} %get-tuple-element.23), channel_id=1, source_target_pairs={{0,8},{8,0},{16,24},{24,16},{32,40},{40,32},{48,56},{56,48},{64,72... | collective-permute-start | bytes 147464 | tf_op jit(solution)/shard_map/ppermute | solution.py:36
  245.6 8.7 %copy-start.2 = (f32[1,3,32,128]{3,2,1,0:T(8,128)}, f32[1,3,32,128]{3,2,1,0:T(8,128)S(1)}, u32[]{:S(2)}) copy-start(f32[1,3,32,128]{3,2,1,0:T(8,128)S(1)} %bitcast_add_fusion.1) | copy-start | bytes 147460

commit v11 on v8

--- a/solution.py
+++ b/solution.py
@@ -55,7 +55,7 @@
     outgoing = jnp.concatenate(
         [
             jnp.broadcast_to(grad_out[None], (shards, tok_rows, model_width)),
-            hidden.reshape(tok_rows, shards, shard_rows).transpose(1, 0, 2),
+            jnp.stack([hidden[:, p * shard_rows:(p + 1) * shard_rows] for p in range(shards)]),
         ],
         axis=2,
     )

time: 228 us -> 229 us (level)
    reshape x1 -> x0, local copies, waits for them, and re-layouts: 3.05 us -> none  [on_device(): hidden.reshape(tok_rows, shards, shard_rows).transpose(1, 0, 2)]
    unnamed x19 -> x25, local copies, waits for them, and re-layouts: 9.23 us -> 12.1 us
where the time goes in v11:
time: 229 us; the launch traced here: 228 us
  waiting for transfers between devices  148 us (65%)
  starting transfers between devices  30.5 us (13%)
  matrix products  20.8 us (9%)
  local copies, waits for them, and re-layouts  19.6 us (9%)
  other arithmetic  8.62 us (4%)
    all_to_all x1, waiting for transfers between devices, on_device(): lax.all_to_all(outgoing, 'fsdp', split_axis=0, concat_axis=0, tiled=True)  139 us
    ppermute x7, starting transfers between devices, grouped_scatter(): lax.ppermute(send, 'rep', [(j, j ^ mask * inner) for j in range(replicas)])  15.1 us
    dot_general x1, matrix products, on_device(): jnp.einsum('ptd,hd->tph', gathered, down_weight, preferred_element_type=j...  12.2 us
    unnamed x25, local copies, waits for them, and re-layouts  12.1 us
    concatenate x1, other arithmetic, on_device(): jnp.concatenate([jnp.broadcast_to(grad_out[None], (shards, tok_rows, mode...  6.73 us
    all_to_all x1, starting transfers between devices, on_device(): lax.all_to_all(outgoing, 'fsdp', split_axis=0, concat_axis=0, tiled=True)  5.86 us
    ppermute x3, starting transfers between devices, grouped_scatter(): lax.ppermute(send, 'rep', [(j, j ^ mask) for j in range(replicas)])  5.76 us
    ppermute x7, waiting for transfers between devices, grouped_scatter(): lax.ppermute(send, 'rep', [(j, j ^ mask * inner) for j in range(replicas)])  5.65 us
  transfers between devices with their start and end apart: 12, of which 5 were waited for; matrix products, arithmetic and copies ran while one was open for 7% of the time, Pallas kernels for 0%

profile of v11, /device:TPU:1, one launch (start us, length us, event | category | flops | bytes accessed | tf_op | source)
XLA Modules:
  0.0 228.1 jit_solution(3069238191633987502)
XLA Ops:
  0.7 1.1 bitcast_dynamic-update-slice_fusion.7
  1.7 1.0 bitcast_dynamic-update-slice_fusion.6
  2.7 1.0 bitcast_dynamic-update-slice_fusion.5
  3.7 1.0 bitcast_dynamic-update-slice_fusion.4
  4.6 1.0 bitcast_dynamic-update-slice_fusion.3
  5.6 1.0 bitcast_dynamic-update-slice_fusion.2
  6.6 1.0 bitcast_dynamic-update-slice_fusion.1
  7.5 1.0 bitcast_dynamic-update-slice_fusion
  8.5 1.0 broadcast_in_dim.12
  9.6 6.7 %pad_maximum_fusion = bf16[8,128,4992]{2,1,0:T(8,128)(2,1)} fusion(bf16[8,128,896]{2,1,0:T(8,128)(2,1)S(1)} %bitcast_dynamic-update-slice_fusion, bf16[8,128,4096]{2,1,0:T(8,128)(2,1)S(1)} %broadcast_in_dim.12), kind=kLoop, calls=%fused_computation | loop fusion | flops 20447232 | bytes 20447232 | tf_op jit(solution)/shard_map/concatenate | solution.py:55
  16.3 5.9 %all-to-all-start = ((bf16[8,128,4992]{2,1,0:T(8,128)(2,1)}), bf16[8,128,4992]{2,1,0:T(8,128)(2,1)}, u32[]{:S(2)}, u32[]{:S(2)}) async-start(bf16[8,128,4992]{2,1,0:T(8,128)(2,1)} %pad_maximum_fusion), calls=%async_computation | async-start | bytes 20447232 | tf_op jit(solution)/shard_map/all_to_all | solution.py:62
  22.2 139.0 %all-to-all-done = bf16[8,128,4992]{2,1,0:T(8,128)(2,1)} async-done(((bf16[8,128,4992]{2,1,0:T(8,128)(2,1)}), bf16[8,128,4992]{2,1,0:T(8,128)(2,1)}, u32[]{:S(2)}, u32[]{:S(2)}) %all-to-all-start) | async-done | bytes 10223648 | tf_op jit(solution)/shard_map/all_to_all | solution.py:62
  161.1 2.2 fusion.17
  163.9 5.0 %fusion.5 = f32[288,4096]{1,0:T(8,128)S(1)} fusion(bf16[8,128,4992]{2,1,0:T(8,128)(2,1)} %all-to-all-done, bf16[288,8,128]{2,1,0:T(8,128)(2,1)S(1)} %bitcast.113), kind=kOutput, calls=%fused_computation.6 | convolution fusion | flops 2415919104 | bytes 13697024 | tf_op jit(solution)/shard_map/mpt,ptd->md/dot_general | solution.py:79
  169.5 1.8 constant_dynamic-slice_fusion.3
  171.4 5.3 %collective-permute-start.2 = (f32[8,3,32,128]{3,2,1,0:T(8,128)S(1)}, f32[8,3,32,128]{3,2,1,0:T(8,128)}, u32[]{:S(2)}, u32[]{:S(2)}) collective-permute-start(f32[8,3,32,128]{3,2,1,0:T(8,128)S(1)} %bitcast.114), channel_id=1, source_target_pairs={{0,24},{8,16},{16,8},{24,0},{32,56},{40,48},{48,40},{56,32},{64,88... | collective-permute-start | bytes 1179656 | tf_op jit(solution)/shard_map/ppermute | solution.py:31
  176.8 0.8 copy.34
  178.0 12.2 %convert_bitcast_fusion = bf16[128,8,896]{2,0,1:T(8,128)(2,1)} fusion(bf16[896,4096]{1,0:T(8,128)(2,1)S(1)} %bitcast.117, bf16[8,128,4992]{2,1,0:T(8,128)(2,1)} %all-to-all-done), kind=kOutput, calls=%fused_computation.9 | convolution fusion | flops 7517110272 | bytes 17563648 | tf_op jit(solution)/shard_map/ptd,hd->tph/dot_general | solution.py:65
  190.2 3.8 %all-to-all-start.1 = ((bf16[128,8,896]{2,0,1:T(8,128)(2,1)}), bf16[128,8,896]{2,0,1:T(8,128)(2,1)S(1)}, u32[]{:S(2)}, u32[]{:S(2)}) async-start(bf16[128,8,896]{2,0,1:T(8,128)(2,1)} %convert_bitcast_fusion), calls=%async_computation.1 | async-start | bytes 3670016 | tf_op jit(solution)/shard_map/all_to_all | solution.py:68
  194.6 1.4 fusion.25
  196.0 5.7 %collective-permute-start.9 = (f32[3,32,128]{2,1,0:T(8,128)S(1)}, f32[3,32,128]{2,1,0:T(8,128)S(1)}, u32[]{:S(2)}, u32[]{:S(2)}) collective-permute-start(f32[3,32,128]{2,1,0:T(8,128)S(1)} %get-tuple-element.17), channel_id=1, source_target_pairs={{0,224},{8,232},{16,240},{24,248},{32,192},{40,200},{48,208},{56,2... | collective-permute-start | bytes 147464 | tf_op jit(solution)/shard_map/ppermute | solution.py:36
  202.3 3.5 %collective-permute-start.7 = (f32[3,32,128]{2,1,0:T(8,128)S(1)}, f32[3,32,128]{2,1,0:T(8,128)S(1)}, u32[]{:S(2)}, u32[]{:S(2)}) collective-permute-start(f32[3,32,128]{2,1,0:T(8,128)S(1)} %get-tuple-element.19), channel_id=1, source_target_pairs={{0,160},{8,168},{16,176},{24,184},{32,128},{40,136},{48,144},{56,1... | collective-permute-start | bytes 147464 | tf_op jit(solution)/shard_map/ppermute | solution.py:36
  205.8 1.8 collective-permute-start.6
  207.6 1.6 collective-permute-start.5
  209.2 1.9 collective-permute-start.3
  211.1 2.0 collective-permute-done.6
  213.2 3.6 %collective-permute-done.4 = f32[3,32,128]{2,1,0:T(8,128)S(1)} collective-permute-done((f32[3,32,128]{2,1,0:T(8,128)S(1)}, f32[3,32,128]{2,1,0:T(8,128)S(1)}, u32[]{:S(2)}, u32[]{:S(2)}) %collective-permute-start.4) | collective-permute-done | bytes 49184 | tf_op jit(solution)/shard_map/ppermute | solution.py:36
  217.3 1.0 copy.23
  218.2 1.0 fusion.20
  219.3 2.6 %all-to-all-done.1 = bf16[128,8,896]{2,0,1:T(8,128)(2,1)S(1)} async-done(((bf16[128,8,896]{2,0,1:T(8,128)(2,1)}), bf16[128,8,896]{2,0,1:T(8,128)(2,1)S(1)}, u32[]{:S(2)}, u32[]{:S(2)}) %all-to-all-start.1) | async-done | bytes 1835040 | tf_op jit(solution)/shard_map/all_to_all | solution.py:68
  221.9 2.4 %copy.15 = bf16[128,8,896]{0,2,1:T(8,128)(2,1)} copy(bf16[128,8,896]{2,0,1:T(8,128)(2,1)S(1)} %all-to-all-done.1) | data formatting | bytes 3670016 | tf_op jit(solution)/shard_map/all_to_all | solution.py:68
  224.3 3.9 %copy.22 = bf16[128,7168]{1,0:T(8,128)(2,1)} copy(bf16[128,7168]{0,1:T(8,128)(2,1)} %bitcast.109) | data formatting | bytes 3670016
  (39 shorter events, 3.4 us)
Async XLA Ops:
  0.6 160.5 %copy-start = (bf16[3,32,896]{2,1,0:T(8,128)(2,1)S(1)}, bf16[3,32,896]{2,1,0:T(8,128)(2,1)}, u32[]{:S(2)}) copy-start(bf16[3,32,896]{2,1,0:T(8,128)(2,1)} %param.9) | copy-start | bytes 516100
  0.6 7.9 %copy-start.1 = (bf16[128,4096]{1,0:T(8,128)(2,1)S(1)}, bf16[128,4096]{1,0:T(8,128)(2,1)}, u32[]{:S(2)}) copy-start(bf16[128,4096]{1,0:T(8,128)(2,1)} %param.7) | copy-start | bytes 3145732
  16.3 144.8 %all-to-all-start = ((bf16[8,128,4992]{2,1,0:T(8,128)(2,1)}), bf16[8,128,4992]{2,1,0:T(8,128)(2,1)}, u32[]{:S(2)}, u32[]{:S(2)}) async-start(bf16[8,128,4992]{2,1,0:T(8,128)(2,1)} %pad_maximum_fusion), calls=%async_computation | async-start | bytes 20447232 | tf_op jit(solution)/shard_map/all_to_all | solution.py:62
  168.9 9.1 %slice-start = ((s8[7340032]{0:T(1024)(128)(4,1)}), s8[4194304]{0:T(1024)(128)(4,1)S(1)}, s32[]{:S(2)}) async-start(s8[7340032]{0:T(1024)(128)(4,1)} %bitcast.116), calls=%async_computation.2 | async-start | bytes 8388608
  169.2 8.8 %slice-start.1 = ((s8[7340032]{0:T(1024)(128)(4,1)}), s8[3145728]{0:T(1024)(128)(4,1)S(1)}, s32[]{:S(2)}) async-start(s8[7340032]{0:T(1024)(128)(4,1)} %bitcast.116), calls=%async_computation.3 | async-start | bytes 6291456
  171.4 22.7 %collective-permute-start.2 = (f32[8,3,32,128]{3,2,1,0:T(8,128)S(1)}, f32[8,3,32,128]{3,2,1,0:T(8,128)}, u32[]{:S(2)}, u32[]{:S(2)}) collective-permute-start(f32[8,3,32,128]{3,2,1,0:T(8,128)S(1)} %bitcast.114), channel_id=1, source_target_pairs={{0,24},{8,16},{16,8},{24,0},{32,56},{40,48},{48,40},{56,32},{64,88... | collective-permute-start | bytes 1179656 | tf_op jit(solution)/shard_map/ppermute | solution.py:31
  176.7 17.9 %collective-permute-start.1 = (f32[8,3,32,128]{3,2,1,0:T(8,128)S(1)}, f32[8,3,32,128]{3,2,1,0:T(8,128)}, u32[]{:S(2)}, u32[]{:S(2)}) collective-permute-start(f32[8,3,32,128]{3,2,1,0:T(8,128)S(1)} %bitcast.115), channel_id=1, source_target_pairs={{0,16},{8,24},{16,0},{24,8},{32,48},{40,56},{48,32},{56,40},{64,80... | collective-permute-start | bytes 1179656 | tf_op jit(solution)/shard_map/ppermute | solution.py:31
  177.7 16.9 %collective-permute-start = (f32[8,3,32,128]{3,2,1,0:T(8,128)}, f32[8,3,32,128]{3,2,1,0:T(8,128)}, u32[]{:S(2)}, u32[]{:S(2)}) collective-permute-start(f32[8,3,32,128]{3,2,1,0:T(8,128)} %bitcast.107), channel_id=1, source_target_pairs={{0,8},{8,0},{16,24},{24,16},{32,40},{40,32},{48,56},{56,48},{64,72... | collective-permute-start | bytes 1179656 | tf_op jit(solution)/shard_map/ppermute | solution.py:31
  190.2 31.6 %all-to-all-start.1 = ((bf16[128,8,896]{2,0,1:T(8,128)(2,1)}), bf16[128,8,896]{2,0,1:T(8,128)(2,1)S(1)}, u32[]{:S(2)}, u32[]{:S(2)}) async-start(bf16[128,8,896]{2,0,1:T(8,128)(2,1)} %convert_bitcast_fusion), calls=%async_computation.1 | async-start | bytes 3670016 | tf_op jit(solution)/shard_map/all_to_all | solution.py:68
  194.0 22.8 %copy-start.4 = (f32[1,3,32,128]{3,2,1,0:T(8,128)S(1)}, f32[1,3,32,128]{3,2,1,0:T(8,128)}, u32[]{:S(2)}) copy-start(f32[1,3,32,128]{3,2,1,0:T(8,128)} %param.10) | copy-start | bytes 147460
  194.0 22.8 %copy-start.3 = (f32[1,3,32,128]{3,2,1,0:T(8,128)S(1)}, f32[1,3,32,128]{3,2,1,0:T(8,128)}, u32[]{:S(2)}) copy-start(f32[1,3,32,128]{3,2,1,0:T(8,128)} %param.11) | copy-start | bytes 147460
  196.0 13.2 %collective-permute-start.9 = (f32[3,32,128]{2,1,0:T(8,128)S(1)}, f32[3,32,128]{2,1,0:T(8,128)S(1)}, u32[]{:S(2)}, u32[]{:S(2)}) collective-permute-start(f32[3,32,128]{2,1,0:T(8,128)S(1)} %get-tuple-element.17), channel_id=1, source_target_pairs={{0,224},{8,232},{16,240},{24,248},{32,192},{40,200},{48,208},{56,2... | collective-permute-start | bytes 147464 | tf_op jit(solution)/shard_map/ppermute | solution.py:36
  201.8 7.5 %collective-permute-start.8 = (f32[3,32,128]{2,1,0:T(8,128)S(1)}, f32[3,32,128]{2,1,0:T(8,128)S(1)}, u32[]{:S(2)}, u32[]{:S(2)}) collective-permute-start(f32[3,32,128]{2,1,0:T(8,128)S(1)} %get-tuple-element.18), channel_id=1, source_target_pairs={{0,192},{8,200},{16,208},{24,216},{32,224},{40,232},{48,240},{56,2... | collective-permute-start | bytes 147464 | tf_op jit(solution)/shard_map/ppermute | solution.py:36
  202.3 8.8 %collective-permute-start.7 = (f32[3,32,128]{2,1,0:T(8,128)S(1)}, f32[3,32,128]{2,1,0:T(8,128)S(1)}, u32[]{:S(2)}, u32[]{:S(2)}) collective-permute-start(f32[3,32,128]{2,1,0:T(8,128)S(1)} %get-tuple-element.19), channel_id=1, source_target_pairs={{0,160},{8,168},{16,176},{24,184},{32,128},{40,136},{48,144},{56,1... | collective-permute-start | bytes 147464 | tf_op jit(solution)/shard_map/ppermute | solution.py:36
  205.8 7.4 %collective-permute-start.6 = (f32[3,32,128]{2,1,0:T(8,128)S(1)}, f32[3,32,128]{2,1,0:T(8,128)S(1)}, u32[]{:S(2)}, u32[]{:S(2)}) collective-permute-start(f32[3,32,128]{2,1,0:T(8,128)S(1)} %get-tuple-element.20), channel_id=1, source_target_pairs={{0,128},{8,136},{16,144},{24,152},{32,160},{40,168},{48,176},{56,1... | collective-permute-start | bytes 147464 | tf_op jit(solution)/shard_map/ppermute | solution.py:36
  207.6 5.6 %collective-permute-start.5 = (f32[3,32,128]{2,1,0:T(8,128)S(1)}, f32[3,32,128]{2,1,0:T(8,128)S(1)}, u32[]{:S(2)}, u32[]{:S(2)}) collective-permute-start(f32[3,32,128]{2,1,0:T(8,128)S(1)} %get-tuple-element.21), channel_id=1, source_target_pairs={{0,96},{8,104},{16,112},{24,120},{32,64},{40,72},{48,80},{56,88},{... | collective-permute-start | bytes 147464 | tf_op jit(solution)/shard_map/ppermute | solution.py:36
  209.2 7.6 %collective-permute-start.4 = (f32[3,32,128]{2,1,0:T(8,128)S(1)}, f32[3,32,128]{2,1,0:T(8,128)S(1)}, u32[]{:S(2)}, u32[]{:S(2)}) collective-permute-start(f32[3,32,128]{2,1,0:T(8,128)S(1)} %get-tuple-element.22), channel_id=1, source_target_pairs={{0,64},{8,72},{16,80},{24,88},{32,96},{40,104},{48,112},{56,120},{... | collective-permute-start | bytes 147464 | tf_op jit(solution)/shard_map/ppermute | solution.py:36
  209.2 7.6 %collective-permute-start.3 = (f32[3,32,128]{2,1,0:T(8,128)S(1)}, f32[3,32,128]{2,1,0:T(8,128)S(1)}, u32[]{:S(2)}, u32[]{:S(2)}) collective-permute-start(f32[3,32,128]{2,1,0:T(8,128)S(1)} %get-tuple-element.16), channel_id=1, source_target_pairs={{0,32},{8,40},{16,48},{24,56},{32,0},{40,8},{48,16},{56,24},{64,96... | collective-permute-start | bytes 147464 | tf_op jit(solution)/shard_map/ppermute | solution.py:36
  216.8 7.4 %copy-start.2 = (f32[1,3,32,128]{3,2,1,0:T(8,128)}, f32[1,3,32,128]{3,2,1,0:T(8,128)S(1)}, u32[]{:S(2)}) copy-start(f32[1,3,32,128]{3,2,1,0:T(8,128)S(1)} %bitcast_add_fusion.1) | copy-start | bytes 147460

commit v12 on v8

--- a/solution.py
+++ b/solution.py
@@ -3,10 +3,26 @@
 import jax
 import jax.numpy as jnp
 from jax import lax
+from jax.experimental import pallas as pl
 from jax.sharding import PartitionSpec as P
 
 momentum_decay = 0.9
 step_size = 0.5
+
+
+def _place_block(block_ref, out_ref):
+    out_ref[...] = block_ref[0]
+
+
+def place_blocks(blocks):
+    count, rows, width = blocks.shape
+    return pl.pallas_call(
+        _place_block,
+        out_shape=jax.ShapeDtypeStruct((rows, count * width), blocks.dtype),
+        grid=(count,),
+        in_specs=[pl.BlockSpec((1, rows, width), lambda i: (i, 0, 0))],
+        out_specs=pl.BlockSpec((rows, width), lambda i: (0, i)),
+    )(blocks)
 
 
 def split3(x):
@@ -63,11 +79,11 @@
     gathered = arrived[:, :, :model_width]
     hidden_cols = arrived[:, :, model_width:]
     partial_grads = jnp.einsum(
-        "ptd,hd->tph", gathered, down_weight, preferred_element_type=jnp.float32
+        "ptd,hd->pth", gathered, down_weight, preferred_element_type=jnp.float32
     ).astype(jnp.bfloat16)
-    grad_hidden = lax.all_to_all(
-        partial_grads, "fsdp", split_axis=1, concat_axis=1, tiled=True
-    ).reshape(tok_rows, shards * shard_rows)
+    grad_hidden = place_blocks(
+        lax.all_to_all(partial_grads, "fsdp", split_axis=0, concat_axis=0, tiled=True)
+    )
 
     projected = jnp.einsum(
         "ki,pti->kpt",

time: 228 us -> 229 us (level)
  Pallas kernels: 0 us -> 5.54 us
  local copies, waits for them, and re-layouts: 18.8 us -> 13.8 us
    pallas_call x0 -> x1, Pallas kernels: none -> 5.54 us  [place_blocks(): pl.pallas_call(_place_block, out_shape=jax.ShapeDtypeStruct((rows, count...]
    unnamed x19 -> x20, local copies, waits for them, and re-layouts: 9.23 us -> 6.61 us
    all_to_all x1 -> x0, local copies, waits for them, and re-layouts: 2.4 us -> none  [on_device(): lax.all_to_all(partial_grads, 'fsdp', split_axis=1, concat_axis=1, tiled=...]
where the time goes in v12:
time: 229 us; the launch traced here: 228 us
  waiting for transfers between devices  148 us (65%)
  starting transfers between devices  30.3 us (13%)
  matrix products  20.8 us (9%)
  local copies, waits for them, and re-layouts  13.8 us (6%)
  other arithmetic  8.96 us (4%)
  Pallas kernels  5.54 us (2%)
    all_to_all x1, waiting for transfers between devices, on_device(): lax.all_to_all(outgoing, 'fsdp', split_axis=0, concat_axis=0, tiled=True)  139 us
    ppermute x7, starting transfers between devices, grouped_scatter(): lax.ppermute(send, 'rep', [(j, j ^ mask * inner) for j in range(replicas)])  15.1 us
    dot_general x1, matrix products, on_device(): jnp.einsum('ptd,hd->pth', gathered, down_weight, preferred_element_type=j...  12.2 us
    concatenate x1, other arithmetic, on_device(): jnp.concatenate([jnp.broadcast_to(grad_out[None], (shards, tok_rows, mode...  7.07 us
    unnamed x20, local copies, waits for them, and re-layouts  6.61 us
    all_to_all x1, starting transfers between devices, on_device(): lax.all_to_all(outgoing, 'fsdp', split_axis=0, concat_axis=0, tiled=True)  5.86 us
    ppermute x3, starting transfers between devices, grouped_scatter(): lax.ppermute(send, 'rep', [(j, j ^ mask) for j in range(replicas)])  5.76 us
    ppermute x7, waiting for transfers between devices, grouped_scatter(): lax.ppermute(send, 'rep', [(j, j ^ mask * inner) for j in range(replicas)])  5.62 us
  transfers between devices with their start and end apart: 12, of which 5 were waited for; matrix products, arithmetic and copies ran while one was open for 7% of the time, Pallas kernels for 0%

profile of v12, /device:TPU:1, one launch (start us, length us, event | category | flops | bytes accessed | tf_op | source)
XLA Modules:
  0.0 228.0 jit_solution(14454961489861455758)
XLA Ops:
  0.7 4.0 %copy.15 = bf16[128,7168]{0,1:T(8,128)(2,1)} copy(bf16[128,7168]{1,0:T(8,128)(2,1)} %param.6) | data formatting | bytes 3670016 | tf_op args[0]
  4.6 3.1 %copy.16 = bf16[128,8,896]{2,0,1:T(8,128)(2,1)S(1)} copy(bf16[128,8,896]{0,2,1:T(8,128)(2,1)} %bitcast.93) | data formatting | bytes 3670016 | tf_op jit(solution)/shard_map/reshape | solution.py:74
  7.7 1.0 broadcast_in_dim.12
  8.7 7.1 %pad_maximum_fusion = bf16[8,128,4992]{2,1,0:T(8,128)(2,1)} fusion(bf16[8,128,896]{2,1,0:T(8,128)(2,1)S(1)} %bitcast.92, bf16[8,128,4096]{2,1,0:T(8,128)(2,1)S(1)} %broadcast_in_dim.12), kind=kLoop, calls=%fused_computation | loop fusion | flops 20447232 | bytes 20447232 | tf_op jit(solution)/shard_map/concatenate | solution.py:71
  15.8 5.9 %all-to-all-start = ((bf16[8,128,4992]{2,1,0:T(8,128)(2,1)}), bf16[8,128,4992]{2,1,0:T(8,128)(2,1)}, u32[]{:S(2)}, u32[]{:S(2)}) async-start(bf16[8,128,4992]{2,1,0:T(8,128)(2,1)} %pad_maximum_fusion), calls=%async_computation | async-start | bytes 20447232 | tf_op jit(solution)/shard_map/all_to_all | solution.py:78
  21.7 139.0 %all-to-all-done = bf16[8,128,4992]{2,1,0:T(8,128)(2,1)} async-done(((bf16[8,128,4992]{2,1,0:T(8,128)(2,1)}), bf16[8,128,4992]{2,1,0:T(8,128)(2,1)}, u32[]{:S(2)}, u32[]{:S(2)}) %all-to-all-start) | async-done | bytes 10223648 | tf_op jit(solution)/shard_map/all_to_all | solution.py:78
  160.6 2.2 fusion.18
  163.4 5.0 %fusion.5 = f32[288,4096]{1,0:T(8,128)S(1)} fusion(bf16[8,128,4992]{2,1,0:T(8,128)(2,1)} %all-to-all-done, bf16[288,8,128]{2,1,0:T(8,128)(2,1)S(1)} %bitcast.97), kind=kOutput, calls=%fused_computation.6 | convolution fusion | flops 2415919104 | bytes 13697024 | tf_op jit(solution)/shard_map/mpt,ptd->md/dot_general | solution.py:95
  168.5 0.3 fusion.16
  168.8 0.3 copy.25
  169.0 1.8 constant_dynamic-slice_fusion.3
  170.9 5.3 %collective-permute-start.2 = (f32[8,3,32,128]{3,2,1,0:T(8,128)S(1)}, f32[8,3,32,128]{3,2,1,0:T(8,128)}, u32[]{:S(2)}, u32[]{:S(2)}) collective-permute-start(f32[8,3,32,128]{3,2,1,0:T(8,128)S(1)} %bitcast.98), channel_id=1, source_target_pairs={{0,24},{8,16},{16,8},{24,0},{32,56},{40,48},{48,40},{56,32},{64,88... | collective-permute-start | bytes 1179656 | tf_op jit(solution)/shard_map/ppermute | solution.py:47
  176.4 0.8 copy.34
  177.2 0.4 collective-permute-start
  177.6 12.2 %fusion.10 = bf16[8,128,896]{2,1,0:T(8,128)(2,1)} fusion(bf16[896,4096]{1,0:T(8,128)(2,1)S(1)} %bitcast.101, bf16[8,128,4992]{2,1,0:T(8,128)(2,1)} %all-to-all-done), kind=kOutput, calls=%fused_computation.9 | convolution fusion | flops 7517110272 | bytes 17563648 | tf_op jit(solution)/shard_map/ptd,hd->pth/dot_general | solution.py:81
  189.8 3.6 %all-to-all-start.1 = ((bf16[8,128,896]{2,1,0:T(8,128)(2,1)}), bf16[8,128,896]{2,1,0:T(8,128)(2,1)S(1)}, u32[]{:S(2)}, u32[]{:S(2)}) async-start(bf16[8,128,896]{2,1,0:T(8,128)(2,1)} %fusion.10), calls=%async_computation.1 | async-start | bytes 3670016 | tf_op jit(solution)/shard_map/all_to_all | solution.py:85
  193.4 0.7 collective-permute-done.1
  194.1 1.4 fusion.26
  195.6 5.7 %collective-permute-start.9 = (f32[3,32,128]{2,1,0:T(8,128)S(1)}, f32[3,32,128]{2,1,0:T(8,128)S(1)}, u32[]{:S(2)}, u32[]{:S(2)}) collective-permute-start(f32[3,32,128]{2,1,0:T(8,128)S(1)} %get-tuple-element.17), channel_id=1, source_target_pairs={{0,224},{8,232},{16,240},{24,248},{32,192},{40,200},{48,208},{56,2... | collective-permute-start | bytes 147464 | tf_op jit(solution)/shard_map/ppermute | solution.py:52
  201.3 0.6 collective-permute-start.8
  201.8 3.5 %collective-permute-start.7 = (f32[3,32,128]{2,1,0:T(8,128)S(1)}, f32[3,32,128]{2,1,0:T(8,128)S(1)}, u32[]{:S(2)}, u32[]{:S(2)}) collective-permute-start(f32[3,32,128]{2,1,0:T(8,128)S(1)} %get-tuple-element.19), channel_id=1, source_target_pairs={{0,160},{8,168},{16,176},{24,184},{32,128},{40,136},{48,144},{56,1... | collective-permute-start | bytes 147464 | tf_op jit(solution)/shard_map/ppermute | solution.py:52
  205.3 1.8 collective-permute-start.6
  207.1 1.6 collective-permute-start.5
  208.7 1.9 collective-permute-start.3
  210.7 2.0 collective-permute-done.6
  212.7 3.6 %collective-permute-done.4 = f32[3,32,128]{2,1,0:T(8,128)S(1)} collective-permute-done((f32[3,32,128]{2,1,0:T(8,128)S(1)}, f32[3,32,128]{2,1,0:T(8,128)S(1)}, u32[]{:S(2)}, u32[]{:S(2)}) %collective-permute-start.4) | collective-permute-done | bytes 49184 | tf_op jit(solution)/shard_map/ppermute | solution.py:52
  216.3 0.4 fusion.17
  216.7 1.0 copy.23
  217.7 1.0 fusion.21
  218.8 2.5 %all-to-all-done.1.block_ref = bf16[8,128,896]{2,1,0:T(8,128)(2,1)S(1)} async-done(((bf16[8,128,896]{2,1,0:T(8,128)(2,1)}), bf16[8,128,896]{2,1,0:T(8,128)(2,1)S(1)}, u32[]{:S(2)}, u32[]{:S(2)}) %all-to-all-start.1) | async-done | bytes 1835040 | tf_op jit(solution)/shard_map/all_to_all | solution.py:85
  221.2 1.3 copy-done.1
  222.5 5.5 %shard_map.93 = bf16[128,7168]{1,0:T(8,128)(2,1)} custom-call(bf16[8,128,896]{2,1,0:T(8,128)(2,1)} %copy-done.1), custom_call_target="tpu_custom_call" | custom-call | tf_op jit(solution)/shard_map/pallas_call | solution.py:19
  (34 shorter events, 1.0 us)
Async XLA Ops:
  0.6 160.0 %copy-start = (bf16[3,32,896]{2,1,0:T(8,128)(2,1)S(1)}, bf16[3,32,896]{2,1,0:T(8,128)(2,1)}, u32[]{:S(2)}) copy-start(bf16[3,32,896]{2,1,0:T(8,128)(2,1)} %param.9) | copy-start | bytes 516100
  0.6 7.0 %copy-start.2 = (bf16[128,4096]{1,0:T(8,128)(2,1)S(1)}, bf16[128,4096]{1,0:T(8,128)(2,1)}, u32[]{:S(2)}) copy-start(bf16[128,4096]{1,0:T(8,128)(2,1)} %param.7) | copy-start | bytes 3145732
  15.8 144.8 %all-to-all-start = ((bf16[8,128,4992]{2,1,0:T(8,128)(2,1)}), bf16[8,128,4992]{2,1,0:T(8,128)(2,1)}, u32[]{:S(2)}, u32[]{:S(2)}) async-start(bf16[8,128,4992]{2,1,0:T(8,128)(2,1)} %pad_maximum_fusion), calls=%async_computation | async-start | bytes 20447232 | tf_op jit(solution)/shard_map/all_to_all | solution.py:78
  168.4 9.1 %slice-start = ((s8[7340032]{0:T(1024)(128)(4,1)}), s8[4194304]{0:T(1024)(128)(4,1)S(1)}, s32[]{:S(2)}) async-start(s8[7340032]{0:T(1024)(128)(4,1)} %bitcast.100), calls=%async_computation.2 | async-start | bytes 8388608
  168.7 8.8 %slice-start.1 = ((s8[7340032]{0:T(1024)(128)(4,1)}), s8[3145728]{0:T(1024)(128)(4,1)S(1)}, s32[]{:S(2)}) async-start(s8[7340032]{0:T(1024)(128)(4,1)} %bitcast.100), calls=%async_computation.3 | async-start | bytes 6291456
  170.9 22.5 %collective-permute-start.2 = (f32[8,3,32,128]{3,2,1,0:T(8,128)S(1)}, f32[8,3,32,128]{3,2,1,0:T(8,128)}, u32[]{:S(2)}, u32[]{:S(2)}) collective-permute-start(f32[8,3,32,128]{3,2,1,0:T(8,128)S(1)} %bitcast.98), channel_id=1, source_target_pairs={{0,24},{8,16},{16,8},{24,0},{32,56},{40,48},{48,40},{56,32},{64,88... | collective-permute-start | bytes 1179656 | tf_op jit(solution)/shard_map/ppermute | solution.py:47
  176.2 17.9 %collective-permute-start.1 = (f32[8,3,32,128]{3,2,1,0:T(8,128)S(1)}, f32[8,3,32,128]{3,2,1,0:T(8,128)}, u32[]{:S(2)}, u32[]{:S(2)}) collective-permute-start(f32[8,3,32,128]{3,2,1,0:T(8,128)S(1)} %bitcast.99), channel_id=1, source_target_pairs={{0,16},{8,24},{16,0},{24,8},{32,48},{40,56},{48,32},{56,40},{64,80... | collective-permute-start | bytes 1179656 | tf_op jit(solution)/shard_map/ppermute | solution.py:47
  177.2 39.1 %copy-start.5 = (f32[1,3,32,128]{3,2,1,0:T(8,128)S(1)}, f32[1,3,32,128]{3,2,1,0:T(8,128)}, u32[]{:S(2)}) copy-start(f32[1,3,32,128]{3,2,1,0:T(8,128)} %param.10) | copy-start | bytes 147460
  177.2 39.1 %copy-start.4 = (f32[1,3,32,128]{3,2,1,0:T(8,128)S(1)}, f32[1,3,32,128]{3,2,1,0:T(8,128)}, u32[]{:S(2)}) copy-start(f32[1,3,32,128]{3,2,1,0:T(8,128)} %param.11) | copy-start | bytes 147460
  177.2 16.9 %collective-permute-start = (f32[8,3,32,128]{3,2,1,0:T(8,128)}, f32[8,3,32,128]{3,2,1,0:T(8,128)}, u32[]{:S(2)}, u32[]{:S(2)}) collective-permute-start(f32[8,3,32,128]{3,2,1,0:T(8,128)} %bitcast.90), channel_id=1, source_target_pairs={{0,8},{8,0},{16,24},{24,16},{32,40},{40,32},{48,56},{56,48},{64,72... | collective-permute-start | bytes 1179656 | tf_op jit(solution)/shard_map/ppermute | solution.py:47
  189.8 31.4 %all-to-all-start.1 = ((bf16[8,128,896]{2,1,0:T(8,128)(2,1)}), bf16[8,128,896]{2,1,0:T(8,128)(2,1)S(1)}, u32[]{:S(2)}, u32[]{:S(2)}) async-start(bf16[8,128,896]{2,1,0:T(8,128)(2,1)} %fusion.10), calls=%async_computation.1 | async-start | bytes 3670016 | tf_op jit(solution)/shard_map/all_to_all | solution.py:85
  195.6 13.1 %collective-permute-start.9 = (f32[3,32,128]{2,1,0:T(8,128)S(1)}, f32[3,32,128]{2,1,0:T(8,128)S(1)}, u32[]{:S(2)}, u32[]{:S(2)}) collective-permute-start(f32[3,32,128]{2,1,0:T(8,128)S(1)} %get-tuple-element.17), channel_id=1, source_target_pairs={{0,224},{8,232},{16,240},{24,248},{32,192},{40,200},{48,208},{56,2... | collective-permute-start | bytes 147464 | tf_op jit(solution)/shard_map/ppermute | solution.py:52
  201.3 7.5 %collective-permute-start.8 = (f32[3,32,128]{2,1,0:T(8,128)S(1)}, f32[3,32,128]{2,1,0:T(8,128)S(1)}, u32[]{:S(2)}, u32[]{:S(2)}) collective-permute-start(f32[3,32,128]{2,1,0:T(8,128)S(1)} %get-tuple-element.18), channel_id=1, source_target_pairs={{0,192},{8,200},{16,208},{24,216},{32,224},{40,232},{48,240},{56,2... | collective-permute-start | bytes 147464 | tf_op jit(solution)/shard_map/ppermute | solution.py:52
  201.8 8.8 %collective-permute-start.7 = (f32[3,32,128]{2,1,0:T(8,128)S(1)}, f32[3,32,128]{2,1,0:T(8,128)S(1)}, u32[]{:S(2)}, u32[]{:S(2)}) collective-permute-start(f32[3,32,128]{2,1,0:T(8,128)S(1)} %get-tuple-element.19), channel_id=1, source_target_pairs={{0,160},{8,168},{16,176},{24,184},{32,128},{40,136},{48,144},{56,1... | collective-permute-start | bytes 147464 | tf_op jit(solution)/shard_map/ppermute | solution.py:52
  205.3 7.4 %collective-permute-start.6 = (f32[3,32,128]{2,1,0:T(8,128)S(1)}, f32[3,32,128]{2,1,0:T(8,128)S(1)}, u32[]{:S(2)}, u32[]{:S(2)}) collective-permute-start(f32[3,32,128]{2,1,0:T(8,128)S(1)} %get-tuple-element.20), channel_id=1, source_target_pairs={{0,128},{8,136},{16,144},{24,152},{32,160},{40,168},{48,176},{56,1... | collective-permute-start | bytes 147464 | tf_op jit(solution)/shard_map/ppermute | solution.py:52
  207.1 5.6 %collective-permute-start.5 = (f32[3,32,128]{2,1,0:T(8,128)S(1)}, f32[3,32,128]{2,1,0:T(8,128)S(1)}, u32[]{:S(2)}, u32[]{:S(2)}) collective-permute-start(f32[3,32,128]{2,1,0:T(8,128)S(1)} %get-tuple-element.21), channel_id=1, source_target_pairs={{0,96},{8,104},{16,112},{24,120},{32,64},{40,72},{48,80},{56,88},{... | collective-permute-start | bytes 147464 | tf_op jit(solution)/shard_map/ppermute | solution.py:52
  208.7 7.5 %collective-permute-start.4 = (f32[3,32,128]{2,1,0:T(8,128)S(1)}, f32[3,32,128]{2,1,0:T(8,128)S(1)}, u32[]{:S(2)}, u32[]{:S(2)}) collective-permute-start(f32[3,32,128]{2,1,0:T(8,128)S(1)} %get-tuple-element.22), channel_id=1, source_target_pairs={{0,64},{8,72},{16,80},{24,88},{32,96},{40,104},{48,112},{56,120},{... | collective-permute-start | bytes 147464 | tf_op jit(solution)/shard_map/ppermute | solution.py:52
  208.7 7.5 %collective-permute-start.3 = (f32[3,32,128]{2,1,0:T(8,128)S(1)}, f32[3,32,128]{2,1,0:T(8,128)S(1)}, u32[]{:S(2)}, u32[]{:S(2)}) collective-permute-start(f32[3,32,128]{2,1,0:T(8,128)S(1)} %get-tuple-element.16), channel_id=1, source_target_pairs={{0,32},{8,40},{16,48},{24,56},{32,0},{40,8},{48,16},{56,24},{64,96... | collective-permute-start | bytes 147464 | tf_op jit(solution)/shard_map/ppermute | solution.py:52
  216.3 11.7 %copy-start.3 = (f32[1,3,32,128]{3,2,1,0:T(8,128)}, f32[1,3,32,128]{3,2,1,0:T(8,128)S(1)}, u32[]{:S(2)}) copy-start(f32[1,3,32,128]{3,2,1,0:T(8,128)S(1)} %bitcast_add_fusion.1) | copy-start | bytes 147460
  221.2 1.3 copy-start.1

commit v13 on v12

--- a/solution.py
+++ b/solution.py
@@ -4,24 +4,25 @@
 import jax.numpy as jnp
 from jax import lax
 from jax.experimental import pallas as pl
+from jax.experimental.pallas import tpu as pltpu
 from jax.sharding import PartitionSpec as P
 
 momentum_decay = 0.9
 step_size = 0.5
 
 
-def _place_block(block_ref, out_ref):
-    out_ref[...] = block_ref[0]
-
-
 def place_blocks(blocks):
     count, rows, width = blocks.shape
+
+    def body(block_ref, out_ref):
+        for p in range(count):
+            out_ref[:, p * width:(p + 1) * width] = block_ref[p]
+
     return pl.pallas_call(
-        _place_block,
+        body,
         out_shape=jax.ShapeDtypeStruct((rows, count * width), blocks.dtype),
-        grid=(count,),
-        in_specs=[pl.BlockSpec((1, rows, width), lambda i: (i, 0, 0))],
-        out_specs=pl.BlockSpec((rows, width), lambda i: (0, i)),
+        in_specs=[pl.BlockSpec(memory_space=pltpu.VMEM)],
+        out_specs=pl.BlockSpec(memory_space=pltpu.VMEM),
     )(blocks)
 
 

time: 229 us -> 226 us (0.987)
  Pallas kernels: 5.54 us -> 2.86 us
    pallas_call x1, Pallas kernels: 5.54 us -> 2.86 us  [place_blocks(): pl.pallas_call(body, out_shape=jax.ShapeDtypeStruct((rows, count * width)...]
  transfers between devices with their start and end apart: 12 -> 12, of which waited for: 5 -> 5; matrix products, arithmetic and copies ran while one was open for 7% -> 8% of each run, Pallas kernels for 0% -> 0%
where the time goes in v13:
time: 226 us; the launch traced here: 225 us
  waiting for transfers between devices  148 us (65%)
  starting transfers between devices  30.3 us (13%)
  matrix products  20.8 us (9%)
  local copies, waits for them, and re-layouts  13.8 us (6%)
  other arithmetic  8.96 us (4%)
  Pallas kernels  2.86 us (1%)
    all_to_all x1, waiting for transfers between devices, on_device(): lax.all_to_all(outgoing, 'fsdp', split_axis=0, concat_axis=0, tiled=True)  139 us
    ppermute x7, starting transfers between devices, grouped_scatter(): lax.ppermute(send, 'rep', [(j, j ^ mask * inner) for j in range(replicas)])  15.1 us
    dot_general x1, matrix products, on_device(): jnp.einsum('ptd,hd->pth', gathered, down_weight, preferred_element_type=j...  12.2 us
    concatenate x1, other arithmetic, on_device(): jnp.concatenate([jnp.broadcast_to(grad_out[None], (shards, tok_rows, mode...  7.07 us
    unnamed x20, local copies, waits for them, and re-layouts  6.61 us
    all_to_all x1, starting transfers between devices, on_device(): lax.all_to_all(outgoing, 'fsdp', split_axis=0, concat_axis=0, tiled=True)  5.86 us
    ppermute x3, starting transfers between devices, grouped_scatter(): lax.ppermute(send, 'rep', [(j, j ^ mask) for j in range(replicas)])  5.76 us
    ppermute x7, waiting for transfers between devices, grouped_scatter(): lax.ppermute(send, 'rep', [(j, j ^ mask * inner) for j in range(replicas)])  5.62 us
  transfers between devices with their start and end apart: 12, of which 5 were waited for; matrix products, arithmetic and copies ran while one was open for 8% of the time, Pallas kernels for 0%

profile of v13, /device:TPU:1, one launch (start us, length us, event | category | flops | bytes accessed | tf_op | source)
XLA Modules:
  0.0 225.3 jit_solution(8611946839398018508)
XLA Ops:
  0.7 4.0 %copy.15 = bf16[128,7168]{0,1:T(8,128)(2,1)} copy(bf16[128,7168]{1,0:T(8,128)(2,1)} %param.6) | data formatting | bytes 3670016 | tf_op args[0]
  4.6 3.1 %copy.16 = bf16[128,8,896]{2,0,1:T(8,128)(2,1)S(1)} copy(bf16[128,8,896]{0,2,1:T(8,128)(2,1)} %bitcast.93) | data formatting | bytes 3670016 | tf_op jit(solution)/shard_map/reshape | solution.py:75
  7.7 1.0 broadcast_in_dim.12
  8.7 7.1 %pad_maximum_fusion = bf16[8,128,4992]{2,1,0:T(8,128)(2,1)} fusion(bf16[8,128,896]{2,1,0:T(8,128)(2,1)S(1)} %bitcast.92, bf16[8,128,4096]{2,1,0:T(8,128)(2,1)S(1)} %broadcast_in_dim.12), kind=kLoop, calls=%fused_computation | loop fusion | flops 20447232 | bytes 20447232 | tf_op jit(solution)/shard_map/concatenate | solution.py:72
  15.8 5.9 %all-to-all-start = ((bf16[8,128,4992]{2,1,0:T(8,128)(2,1)}), bf16[8,128,4992]{2,1,0:T(8,128)(2,1)}, u32[]{:S(2)}, u32[]{:S(2)}) async-start(bf16[8,128,4992]{2,1,0:T(8,128)(2,1)} %pad_maximum_fusion), calls=%async_computation | async-start | bytes 20447232 | tf_op jit(solution)/shard_map/all_to_all | solution.py:79
  21.7 139.0 %all-to-all-done = bf16[8,128,4992]{2,1,0:T(8,128)(2,1)} async-done(((bf16[8,128,4992]{2,1,0:T(8,128)(2,1)}), bf16[8,128,4992]{2,1,0:T(8,128)(2,1)}, u32[]{:S(2)}, u32[]{:S(2)}) %all-to-all-start) | async-done | bytes 10223648 | tf_op jit(solution)/shard_map/all_to_all | solution.py:79
  160.6 2.2 fusion.18
  163.4 5.0 %fusion.5 = f32[288,4096]{1,0:T(8,128)S(1)} fusion(bf16[8,128,4992]{2,1,0:T(8,128)(2,1)} %all-to-all-done, bf16[288,8,128]{2,1,0:T(8,128)(2,1)S(1)} %bitcast.97), kind=kOutput, calls=%fused_computation.6 | convolution fusion | flops 2415919104 | bytes 13697024 | tf_op jit(solution)/shard_map/mpt,ptd->md/dot_general | solution.py:96
  168.5 0.3 fusion.16
  168.8 0.3 copy.25
  169.0 1.8 constant_dynamic-slice_fusion.3
  170.9 5.3 %collective-permute-start.2 = (f32[8,3,32,128]{3,2,1,0:T(8,128)S(1)}, f32[8,3,32,128]{3,2,1,0:T(8,128)}, u32[]{:S(2)}, u32[]{:S(2)}) collective-permute-start(f32[8,3,32,128]{3,2,1,0:T(8,128)S(1)} %bitcast.98), channel_id=1, source_target_pairs={{0,24},{8,16},{16,8},{24,0},{32,56},{40,48},{48,40},{56,32},{64,88... | collective-permute-start | bytes 1179656 | tf_op jit(solution)/shard_map/ppermute | solution.py:48
  176.4 0.8 copy.34
  177.2 0.4 collective-permute-start
  177.6 12.2 %fusion.10 = bf16[8,128,896]{2,1,0:T(8,128)(2,1)} fusion(bf16[896,4096]{1,0:T(8,128)(2,1)S(1)} %bitcast.101, bf16[8,128,4992]{2,1,0:T(8,128)(2,1)} %all-to-all-done), kind=kOutput, calls=%fused_computation.9 | convolution fusion | flops 7517110272 | bytes 17563648 | tf_op jit(solution)/shard_map/ptd,hd->pth/dot_general | solution.py:82
  189.8 3.6 %all-to-all-start.1 = ((bf16[8,128,896]{2,1,0:T(8,128)(2,1)}), bf16[8,128,896]{2,1,0:T(8,128)(2,1)S(1)}, u32[]{:S(2)}, u32[]{:S(2)}) async-start(bf16[8,128,896]{2,1,0:T(8,128)(2,1)} %fusion.10), calls=%async_computation.1 | async-start | bytes 3670016 | tf_op jit(solution)/shard_map/all_to_all | solution.py:86
  193.4 0.7 collective-permute-done.1
  194.1 1.4 fusion.26
  195.6 5.7 %collective-permute-start.9 = (f32[3,32,128]{2,1,0:T(8,128)S(1)}, f32[3,32,128]{2,1,0:T(8,128)S(1)}, u32[]{:S(2)}, u32[]{:S(2)}) collective-permute-start(f32[3,32,128]{2,1,0:T(8,128)S(1)} %get-tuple-element.17), channel_id=1, source_target_pairs={{0,224},{8,232},{16,240},{24,248},{32,192},{40,200},{48,208},{56,2... | collective-permute-start | bytes 147464 | tf_op jit(solution)/shard_map/ppermute | solution.py:53
  201.3 0.6 collective-permute-start.8
  201.8 3.5 %collective-permute-start.7 = (f32[3,32,128]{2,1,0:T(8,128)S(1)}, f32[3,32,128]{2,1,0:T(8,128)S(1)}, u32[]{:S(2)}, u32[]{:S(2)}) collective-permute-start(f32[3,32,128]{2,1,0:T(8,128)S(1)} %get-tuple-element.19), channel_id=1, source_target_pairs={{0,160},{8,168},{16,176},{24,184},{32,128},{40,136},{48,144},{56,1... | collective-permute-start | bytes 147464 | tf_op jit(solution)/shard_map/ppermute | solution.py:53
  205.3 1.8 collective-permute-start.6
  207.1 1.6 collective-permute-start.5
  208.7 1.9 collective-permute-start.3
  210.7 2.0 collective-permute-done.6
  212.7 3.6 %collective-permute-done.4 = f32[3,32,128]{2,1,0:T(8,128)S(1)} collective-permute-done((f32[3,32,128]{2,1,0:T(8,128)S(1)}, f32[3,32,128]{2,1,0:T(8,128)S(1)}, u32[]{:S(2)}, u32[]{:S(2)}) %collective-permute-start.4) | collective-permute-done | bytes 49184 | tf_op jit(solution)/shard_map/ppermute | solution.py:53
  216.3 0.4 fusion.17
  216.7 1.0 copy.23
  217.7 1.0 fusion.21
  218.8 2.5 %all-to-all-done.1.block_ref = bf16[8,128,896]{2,1,0:T(8,128)(2,1)S(1)} async-done(((bf16[8,128,896]{2,1,0:T(8,128)(2,1)}), bf16[8,128,896]{2,1,0:T(8,128)(2,1)S(1)}, u32[]{:S(2)}, u32[]{:S(2)}) %all-to-all-start.1) | async-done | bytes 1835040 | tf_op jit(solution)/shard_map/all_to_all | solution.py:86
  221.2 1.3 copy-done.1
  222.5 2.9 %shard_map.93 = bf16[128,7168]{1,0:T(8,128)(2,1)} custom-call(bf16[8,128,896]{2,1,0:T(8,128)(2,1)} %copy-done.1), custom_call_target="tpu_custom_call" | custom-call | tf_op jit(solution)/shard_map/pallas_call | solution.py:21
  (34 shorter events, 1.0 us)
Async XLA Ops:
  0.6 160.0 %copy-start = (bf16[3,32,896]{2,1,0:T(8,128)(2,1)S(1)}, bf16[3,32,896]{2,1,0:T(8,128)(2,1)}, u32[]{:S(2)}) copy-start(bf16[3,32,896]{2,1,0:T(8,128)(2,1)} %param.9) | copy-start | bytes 516100
  0.6 7.0 %copy-start.2 = (bf16[128,4096]{1,0:T(8,128)(2,1)S(1)}, bf16[128,4096]{1,0:T(8,128)(2,1)}, u32[]{:S(2)}) copy-start(bf16[128,4096]{1,0:T(8,128)(2,1)} %param.7) | copy-start | bytes 3145732
  15.8 144.8 %all-to-all-start = ((bf16[8,128,4992]{2,1,0:T(8,128)(2,1)}), bf16[8,128,4992]{2,1,0:T(8,128)(2,1)}, u32[]{:S(2)}, u32[]{:S(2)}) async-start(bf16[8,128,4992]{2,1,0:T(8,128)(2,1)} %pad_maximum_fusion), calls=%async_computation | async-start | bytes 20447232 | tf_op jit(solution)/shard_map/all_to_all | solution.py:79
  168.4 9.1 %slice-start = ((s8[7340032]{0:T(1024)(128)(4,1)}), s8[4194304]{0:T(1024)(128)(4,1)S(1)}, s32[]{:S(2)}) async-start(s8[7340032]{0:T(1024)(128)(4,1)} %bitcast.100), calls=%async_computation.2 | async-start | bytes 8388608
  168.7 8.8 %slice-start.1 = ((s8[7340032]{0:T(1024)(128)(4,1)}), s8[3145728]{0:T(1024)(128)(4,1)S(1)}, s32[]{:S(2)}) async-start(s8[7340032]{0:T(1024)(128)(4,1)} %bitcast.100), calls=%async_computation.3 | async-start | bytes 6291456
  170.9 22.5 %collective-permute-start.2 = (f32[8,3,32,128]{3,2,1,0:T(8,128)S(1)}, f32[8,3,32,128]{3,2,1,0:T(8,128)}, u32[]{:S(2)}, u32[]{:S(2)}) collective-permute-start(f32[8,3,32,128]{3,2,1,0:T(8,128)S(1)} %bitcast.98), channel_id=1, source_target_pairs={{0,24},{8,16},{16,8},{24,0},{32,56},{40,48},{48,40},{56,32},{64,88... | collective-permute-start | bytes 1179656 | tf_op jit(solution)/shard_map/ppermute | solution.py:48
  176.2 17.9 %collective-permute-start.1 = (f32[8,3,32,128]{3,2,1,0:T(8,128)S(1)}, f32[8,3,32,128]{3,2,1,0:T(8,128)}, u32[]{:S(2)}, u32[]{:S(2)}) collective-permute-start(f32[8,3,32,128]{3,2,1,0:T(8,128)S(1)} %bitcast.99), channel_id=1, source_target_pairs={{0,16},{8,24},{16,0},{24,8},{32,48},{40,56},{48,32},{56,40},{64,80... | collective-permute-start | bytes 1179656 | tf_op jit(solution)/shard_map/ppermute | solution.py:48
  177.2 39.1 %copy-start.5 = (f32[1,3,32,128]{3,2,1,0:T(8,128)S(1)}, f32[1,3,32,128]{3,2,1,0:T(8,128)}, u32[]{:S(2)}) copy-start(f32[1,3,32,128]{3,2,1,0:T(8,128)} %param.10) | copy-start | bytes 147460
  177.2 39.1 %copy-start.4 = (f32[1,3,32,128]{3,2,1,0:T(8,128)S(1)}, f32[1,3,32,128]{3,2,1,0:T(8,128)}, u32[]{:S(2)}) copy-start(f32[1,3,32,128]{3,2,1,0:T(8,128)} %param.11) | copy-start | bytes 147460
  177.2 16.9 %collective-permute-start = (f32[8,3,32,128]{3,2,1,0:T(8,128)}, f32[8,3,32,128]{3,2,1,0:T(8,128)}, u32[]{:S(2)}, u32[]{:S(2)}) collective-permute-start(f32[8,3,32,128]{3,2,1,0:T(8,128)} %bitcast.90), channel_id=1, source_target_pairs={{0,8},{8,0},{16,24},{24,16},{32,40},{40,32},{48,56},{56,48},{64,72... | collective-permute-start | bytes 1179656 | tf_op jit(solution)/shard_map/ppermute | solution.py:48
  189.8 31.4 %all-to-all-start.1 = ((bf16[8,128,896]{2,1,0:T(8,128)(2,1)}), bf16[8,128,896]{2,1,0:T(8,128)(2,1)S(1)}, u32[]{:S(2)}, u32[]{:S(2)}) async-start(bf16[8,128,896]{2,1,0:T(8,128)(2,1)} %fusion.10), calls=%async_computation.1 | async-start | bytes 3670016 | tf_op jit(solution)/shard_map/all_to_all | solution.py:86
  195.6 13.1 %collective-permute-start.9 = (f32[3,32,128]{2,1,0:T(8,128)S(1)}, f32[3,32,128]{2,1,0:T(8,128)S(1)}, u32[]{:S(2)}, u32[]{:S(2)}) collective-permute-start(f32[3,32,128]{2,1,0:T(8,128)S(1)} %get-tuple-element.17), channel_id=1, source_target_pairs={{0,224},{8,232},{16,240},{24,248},{32,192},{40,200},{48,208},{56,2... | collective-permute-start | bytes 147464 | tf_op jit(solution)/shard_map/ppermute | solution.py:53
  201.3 7.5 %collective-permute-start.8 = (f32[3,32,128]{2,1,0:T(8,128)S(1)}, f32[3,32,128]{2,1,0:T(8,128)S(1)}, u32[]{:S(2)}, u32[]{:S(2)}) collective-permute-start(f32[3,32,128]{2,1,0:T(8,128)S(1)} %get-tuple-element.18), channel_id=1, source_target_pairs={{0,192},{8,200},{16,208},{24,216},{32,224},{40,232},{48,240},{56,2... | collective-permute-start | bytes 147464 | tf_op jit(solution)/shard_map/ppermute | solution.py:53
  201.8 8.8 %collective-permute-start.7 = (f32[3,32,128]{2,1,0:T(8,128)S(1)}, f32[3,32,128]{2,1,0:T(8,128)S(1)}, u32[]{:S(2)}, u32[]{:S(2)}) collective-permute-start(f32[3,32,128]{2,1,0:T(8,128)S(1)} %get-tuple-element.19), channel_id=1, source_target_pairs={{0,160},{8,168},{16,176},{24,184},{32,128},{40,136},{48,144},{56,1... | collective-permute-start | bytes 147464 | tf_op jit(solution)/shard_map/ppermute | solution.py:53
  205.3 7.4 %collective-permute-start.6 = (f32[3,32,128]{2,1,0:T(8,128)S(1)}, f32[3,32,128]{2,1,0:T(8,128)S(1)}, u32[]{:S(2)}, u32[]{:S(2)}) collective-permute-start(f32[3,32,128]{2,1,0:T(8,128)S(1)} %get-tuple-element.20), channel_id=1, source_target_pairs={{0,128},{8,136},{16,144},{24,152},{32,160},{40,168},{48,176},{56,1... | collective-permute-start | bytes 147464 | tf_op jit(solution)/shard_map/ppermute | solution.py:53
  207.1 5.6 %collective-permute-start.5 = (f32[3,32,128]{2,1,0:T(8,128)S(1)}, f32[3,32,128]{2,1,0:T(8,128)S(1)}, u32[]{:S(2)}, u32[]{:S(2)}) collective-permute-start(f32[3,32,128]{2,1,0:T(8,128)S(1)} %get-tuple-element.21), channel_id=1, source_target_pairs={{0,96},{8,104},{16,112},{24,120},{32,64},{40,72},{48,80},{56,88},{... | collective-permute-start | bytes 147464 | tf_op jit(solution)/shard_map/ppermute | solution.py:53
  208.7 7.5 %collective-permute-start.4 = (f32[3,32,128]{2,1,0:T(8,128)S(1)}, f32[3,32,128]{2,1,0:T(8,128)S(1)}, u32[]{:S(2)}, u32[]{:S(2)}) collective-permute-start(f32[3,32,128]{2,1,0:T(8,128)S(1)} %get-tuple-element.22), channel_id=1, source_target_pairs={{0,64},{8,72},{16,80},{24,88},{32,96},{40,104},{48,112},{56,120},{... | collective-permute-start | bytes 147464 | tf_op jit(solution)/shard_map/ppermute | solution.py:53
  208.7 7.5 %collective-permute-start.3 = (f32[3,32,128]{2,1,0:T(8,128)S(1)}, f32[3,32,128]{2,1,0:T(8,128)S(1)}, u32[]{:S(2)}, u32[]{:S(2)}) collective-permute-start(f32[3,32,128]{2,1,0:T(8,128)S(1)} %get-tuple-element.16), channel_id=1, source_target_pairs={{0,32},{8,40},{16,48},{24,56},{32,0},{40,8},{48,16},{56,24},{64,96... | collective-permute-start | bytes 147464 | tf_op jit(solution)/shard_map/ppermute | solution.py:53
  216.3 9.0 %copy-start.3 = (f32[1,3,32,128]{3,2,1,0:T(8,128)}, f32[1,3,32,128]{3,2,1,0:T(8,128)S(1)}, u32[]{:S(2)}) copy-start(f32[1,3,32,128]{3,2,1,0:T(8,128)S(1)} %bitcast_add_fusion.1) | copy-start | bytes 147460
  221.2 1.3 copy-start.1

commit v14 on v13

--- a/solution.py
+++ b/solution.py
@@ -24,6 +24,23 @@
         in_specs=[pl.BlockSpec(memory_space=pltpu.VMEM)],
         out_specs=pl.BlockSpec(memory_space=pltpu.VMEM),
     )(blocks)
+
+
+def build_outgoing(grad_out, hidden, count):
+    rows, width = grad_out.shape
+    block = hidden.shape[1] // count
+
+    def body(grad_ref, hidden_ref, out_ref):
+        for p in range(count):
+            out_ref[p, :, :width] = grad_ref[...]
+            out_ref[p, :, width:] = hidden_ref[:, p * block:(p + 1) * block]
+
+    return pl.pallas_call(
+        body,
+        out_shape=jax.ShapeDtypeStruct((count, rows, width + block), grad_out.dtype),
+        in_specs=[pl.BlockSpec(memory_space=pltpu.VMEM)] * 2,
+        out_specs=pl.BlockSpec(memory_space=pltpu.VMEM),
+    )(grad_out, hidden)
 
 
 def split3(x):
@@ -69,13 +86,7 @@
 
     hash_float = hash_tiles.astype(jnp.float32)
 
-    outgoing = jnp.concatenate(
-        [
-            jnp.broadcast_to(grad_out[None], (shards, tok_rows, model_width)),
-            hidden.reshape(tok_rows, shards, shard_rows).transpose(1, 0, 2),
-        ],
-        axis=2,
-    )
+    outgoing = build_outgoing(grad_out, hidden, shards)
     arrived = lax.all_to_all(outgoing, "fsdp", split_axis=0, concat_axis=0, tiled=True)
     gathered = arrived[:, :, :model_width]
     hidden_cols = arrived[:, :, model_width:]

time: 226 us -> 217 us (0.960)
  local copies, waits for them, and re-layouts: 13.8 us -> 5.71 us
  other arithmetic: 8.96 us -> 1.88 us
  Pallas kernels: 2.86 us -> 9.15 us
    concatenate x1 -> x0, other arithmetic: 7.07 us -> none  [on_device(): jnp.concatenate([jnp.broadcast_to(grad_out[None], (shards, tok_rows, mode...]
    pallas_call x0 -> x1, Pallas kernels: none -> 6.29 us  [build_outgoing(): pl.pallas_call(body, out_shape=jax.ShapeDtypeStruct((count, rows, width +...]
    unnamed x20 -> x17, local copies, waits for them, and re-layouts: 6.61 us -> 2.64 us
    reshape x1 -> x0, local copies, waits for them, and re-layouts: 3.05 us -> none  [on_device(): hidden.reshape(tok_rows, shards, shard_rows).transpose(1, 0, 2)]
  transfers between devices with their start and end apart: 12 -> 12, of which waited for: 5 -> 6; matrix products, arithmetic and copies ran while one was open for 8% -> 8% of each run, Pallas kernels for 0% -> 0%
where the time goes in v14:
time: 217 us
  waiting for transfers between devices  148 us (68%)
  starting transfers between devices  30.4 us (14%)
  matrix products  20.8 us (10%)
  Pallas kernels  9.15 us (4%)
  local copies, waits for them, and re-layouts  5.71 us (3%)
    all_to_all x1, waiting for transfers between devices, on_device(): lax.all_to_all(outgoing, 'fsdp', split_axis=0, concat_axis=0, tiled=True)  139 us
    ppermute x7, starting transfers between devices, grouped_scatter(): lax.ppermute(send, 'rep', [(j, j ^ mask * inner) for j in range(replicas)])  15.1 us
    dot_general x1, matrix products, on_device(): jnp.einsum('ptd,hd->pth', gathered, down_weight, preferred_element_type=j...  12.2 us
    pallas_call x1, Pallas kernels, build_outgoing(): pl.pallas_call(body, out_shape=jax.ShapeDtypeStruct((count, rows, width +...  6.29 us
    all_to_all x1, starting transfers between devices, on_device(): lax.all_to_all(outgoing, 'fsdp', split_axis=0, concat_axis=0, tiled=True)  5.86 us
    ppermute x7, waiting for transfers between devices, grouped_scatter(): lax.ppermute(send, 'rep', [(j, j ^ mask * inner) for j in range(replicas)])  5.84 us
    ppermute x3, starting transfers between devices, grouped_scatter(): lax.ppermute(send, 'rep', [(j, j ^ mask) for j in range(replicas)])  5.76 us
    dot_general x1, matrix products, on_device(): jnp.einsum('mpt,ptd->md', pieces.reshape(3 * sketch_rows, shards, tok_row...  5 us
  transfers between devices with their start and end apart: 12, of which 6 were waited for; matrix products, arithmetic and copies ran while one was open for 8% of the time, Pallas kernels for 0%

profile of v14, /device:TPU:1, one launch (start us, length us, event | category | flops | bytes accessed | tf_op | source)
XLA Modules:
  0.0 216.6 jit_solution(18217909997148554536)
XLA Ops:
  0.6 6.3 %shard_map.93 = bf16[8,128,4992]{2,1,0:T(8,128)(2,1)} custom-call(bf16[128,4096]{1,0:T(8,128)(2,1)} %grad_ref.1, bf16[128,7168]{1,0:T(8,128)(2,1)} %hidden_ref.1), custom_call_target="tpu_custom_call" | custom-call | tf_op jit(solution)/shard_map/pallas_call | solution.py:38
  6.9 5.9 %all-to-all-start = ((bf16[8,128,4992]{2,1,0:T(8,128)(2,1)}), bf16[8,128,4992]{2,1,0:T(8,128)(2,1)}, u32[]{:S(2)}, u32[]{:S(2)}) async-start(bf16[8,128,4992]{2,1,0:T(8,128)(2,1)} %shard_map.93), calls=%async_computation | async-start | bytes 20447232 | tf_op jit(solution)/shard_map/all_to_all | solution.py:90
  12.8 139.0 %all-to-all-done = bf16[8,128,4992]{2,1,0:T(8,128)(2,1)} async-done(((bf16[8,128,4992]{2,1,0:T(8,128)(2,1)}), bf16[8,128,4992]{2,1,0:T(8,128)(2,1)}, u32[]{:S(2)}, u32[]{:S(2)}) %all-to-all-start) | async-done | bytes 10223648 | tf_op jit(solution)/shard_map/all_to_all | solution.py:90
  151.8 2.2 %fusion.18 = f32[96,8,128]{2,0,1:T(8,128)S(1)} fusion(bf16[96,896,1]{1,0,2:T(8,128)(2,1)S(1)} %bitcast.89, bf16[8,128,4992]{2,1,0:T(8,128)(2,1)} %all-to-all-done), kind=kOutput, calls=%fused_computation.15 | convolution fusion | flops 176160768 | bytes 2400256 | tf_op jit(solution)/shard_map/ki,pti->kpt/dot_general | solution.py:100
  154.0 0.2 copy.15
  154.5 5.0 %fusion.5 = f32[288,4096]{1,0:T(8,128)S(1)} fusion(bf16[8,128,4992]{2,1,0:T(8,128)(2,1)} %all-to-all-done, bf16[288,8,128]{2,1,0:T(8,128)(2,1)S(1)} %bitcast.93), kind=kOutput, calls=%fused_computation.5 | convolution fusion | flops 2415919104 | bytes 13697024 | tf_op jit(solution)/shard_map/mpt,ptd->md/dot_general | solution.py:107
  159.6 0.3 fusion.16
  159.9 0.3 copy.23
  160.2 1.8 constant_dynamic-slice_fusion.3
  162.0 5.3 %collective-permute-start.2 = (f32[8,3,32,128]{3,2,1,0:T(8,128)S(1)}, f32[8,3,32,128]{3,2,1,0:T(8,128)}, u32[]{:S(2)}, u32[]{:S(2)}) collective-permute-start(f32[8,3,32,128]{3,2,1,0:T(8,128)S(1)} %bitcast.94), channel_id=1, source_target_pairs={{0,24},{8,16},{16,8},{24,0},{32,56},{40,48},{48,40},{56,32},{64,88... | collective-permute-start | bytes 1179656 | tf_op jit(solution)/shard_map/ppermute | solution.py:65
  167.3 0.1 collective-permute-start.1
  167.5 0.8 copy.32
  168.3 0.4 collective-permute-start
  168.7 12.2 %fusion.10 = bf16[8,128,896]{2,1,0:T(8,128)(2,1)} fusion(bf16[896,4096]{1,0:T(8,128)(2,1)S(1)} %bitcast.97, bf16[8,128,4992]{2,1,0:T(8,128)(2,1)} %all-to-all-done), kind=kOutput, calls=%fused_computation.8 | convolution fusion | flops 7517110272 | bytes 17563648 | tf_op jit(solution)/shard_map/ptd,hd->pth/dot_general | solution.py:93
  180.9 3.7 %all-to-all-start.1 = ((bf16[8,128,896]{2,1,0:T(8,128)(2,1)}), bf16[8,128,896]{2,1,0:T(8,128)(2,1)S(1)}, u32[]{:S(2)}, u32[]{:S(2)}) async-start(bf16[8,128,896]{2,1,0:T(8,128)(2,1)} %fusion.10), calls=%async_computation.1 | async-start | bytes 3670016 | tf_op jit(solution)/shard_map/all_to_all | solution.py:97
  184.7 0.5 collective-permute-done.1
  185.2 1.4 fusion.26
  186.7 5.7 %collective-permute-start.9 = (f32[3,32,128]{2,1,0:T(8,128)S(1)}, f32[3,32,128]{2,1,0:T(8,128)S(1)}, u32[]{:S(2)}, u32[]{:S(2)}) collective-permute-start(f32[3,32,128]{2,1,0:T(8,128)S(1)} %get-tuple-element.17), channel_id=1, source_target_pairs={{0,224},{8,232},{16,240},{24,248},{32,192},{40,200},{48,208},{56,2... | collective-permute-start | bytes 147464 | tf_op jit(solution)/shard_map/ppermute | solution.py:70
  192.4 0.7 collective-permute-start.8
  193.1 3.3 %collective-permute-start.7 = (f32[3,32,128]{2,1,0:T(8,128)S(1)}, f32[3,32,128]{2,1,0:T(8,128)S(1)}, u32[]{:S(2)}, u32[]{:S(2)}) collective-permute-start(f32[3,32,128]{2,1,0:T(8,128)S(1)} %get-tuple-element.19), channel_id=1, source_target_pairs={{0,160},{8,168},{16,176},{24,184},{32,128},{40,136},{48,144},{56,1... | collective-permute-start | bytes 147464 | tf_op jit(solution)/shard_map/ppermute | solution.py:70
  196.4 1.8 collective-permute-start.6
  198.2 1.6 collective-permute-start.5
  199.9 0.1 collective-permute-start.4
  200.0 1.8 collective-permute-start.3
  201.8 2.0 collective-permute-done.6
  203.8 3.8 %collective-permute-done.4 = f32[3,32,128]{2,1,0:T(8,128)S(1)} collective-permute-done((f32[3,32,128]{2,1,0:T(8,128)S(1)}, f32[3,32,128]{2,1,0:T(8,128)S(1)}, u32[]{:S(2)}, u32[]{:S(2)}) %collective-permute-start.4) | collective-permute-done | bytes 49184 | tf_op jit(solution)/shard_map/ppermute | solution.py:70
  207.7 0.4 fusion.17
  208.1 1.0 copy.21
  209.1 1.0 fusion.21
  210.1 2.4 %all-to-all-done.1.block_ref = bf16[8,128,896]{2,1,0:T(8,128)(2,1)S(1)} async-done(((bf16[8,128,896]{2,1,0:T(8,128)(2,1)}), bf16[8,128,896]{2,1,0:T(8,128)(2,1)S(1)}, u32[]{:S(2)}, u32[]{:S(2)}) %all-to-all-start.1) | async-done | bytes 1835040 | tf_op jit(solution)/shard_map/all_to_all | solution.py:97
  212.5 1.3 copy-done.1
  213.7 2.9 %shard_map.94 = bf16[128,7168]{1,0:T(8,128)(2,1)} custom-call(bf16[8,128,896]{2,1,0:T(8,128)(2,1)} %copy-done.1), custom_call_target="tpu_custom_call" | custom-call | tf_op jit(solution)/shard_map/pallas_call | solution.py:21
  (29 shorter events, 0.7 us)
Async XLA Ops:
  0.6 151.1 %copy-start = (bf16[3,32,896]{2,1,0:T(8,128)(2,1)S(1)}, bf16[3,32,896]{2,1,0:T(8,128)(2,1)}, u32[]{:S(2)}) copy-start(bf16[3,32,896]{2,1,0:T(8,128)(2,1)} %param.9) | copy-start | bytes 516100
  6.9 144.8 %all-to-all-start = ((bf16[8,128,4992]{2,1,0:T(8,128)(2,1)}), bf16[8,128,4992]{2,1,0:T(8,128)(2,1)}, u32[]{:S(2)}, u32[]{:S(2)}) async-start(bf16[8,128,4992]{2,1,0:T(8,128)(2,1)} %shard_map.93), calls=%async_computation | async-start | bytes 20447232 | tf_op jit(solution)/shard_map/all_to_all | solution.py:90
  159.6 9.1 %slice-start = ((s8[7340032]{0:T(1024)(128)(4,1)}), s8[4194304]{0:T(1024)(128)(4,1)S(1)}, s32[]{:S(2)}) async-start(s8[7340032]{0:T(1024)(128)(4,1)} %bitcast.96), calls=%async_computation.2 | async-start | bytes 8388608
  159.9 8.8 %slice-start.1 = ((s8[7340032]{0:T(1024)(128)(4,1)}), s8[3145728]{0:T(1024)(128)(4,1)S(1)}, s32[]{:S(2)}) async-start(s8[7340032]{0:T(1024)(128)(4,1)} %bitcast.96), calls=%async_computation.3 | async-start | bytes 6291456
  162.0 22.7 %collective-permute-start.2 = (f32[8,3,32,128]{3,2,1,0:T(8,128)S(1)}, f32[8,3,32,128]{3,2,1,0:T(8,128)}, u32[]{:S(2)}, u32[]{:S(2)}) collective-permute-start(f32[8,3,32,128]{3,2,1,0:T(8,128)S(1)} %bitcast.94), channel_id=1, source_target_pairs={{0,24},{8,16},{16,8},{24,0},{32,56},{40,48},{48,40},{56,32},{64,88... | collective-permute-start | bytes 1179656 | tf_op jit(solution)/shard_map/ppermute | solution.py:65
  167.3 17.9 %collective-permute-start.1 = (f32[8,3,32,128]{3,2,1,0:T(8,128)S(1)}, f32[8,3,32,128]{3,2,1,0:T(8,128)}, u32[]{:S(2)}, u32[]{:S(2)}) collective-permute-start(f32[8,3,32,128]{3,2,1,0:T(8,128)S(1)} %bitcast.95), channel_id=1, source_target_pairs={{0,16},{8,24},{16,0},{24,8},{32,48},{40,56},{48,32},{56,40},{64,80... | collective-permute-start | bytes 1179656 | tf_op jit(solution)/shard_map/ppermute | solution.py:65
  168.3 16.9 %collective-permute-start = (f32[8,3,32,128]{3,2,1,0:T(8,128)}, f32[8,3,32,128]{3,2,1,0:T(8,128)}, u32[]{:S(2)}, u32[]{:S(2)}) collective-permute-start(f32[8,3,32,128]{3,2,1,0:T(8,128)} %bitcast.88), channel_id=1, source_target_pairs={{0,8},{8,0},{16,24},{24,16},{32,40},{40,32},{48,56},{56,48},{64,72... | collective-permute-start | bytes 1179656 | tf_op jit(solution)/shard_map/ppermute | solution.py:65
  180.9 26.7 %copy-start.4 = (f32[1,3,32,128]{3,2,1,0:T(8,128)S(1)}, f32[1,3,32,128]{3,2,1,0:T(8,128)}, u32[]{:S(2)}) copy-start(f32[1,3,32,128]{3,2,1,0:T(8,128)} %param.10) | copy-start | bytes 147460
  180.9 26.8 %copy-start.3 = (f32[1,3,32,128]{3,2,1,0:T(8,128)S(1)}, f32[1,3,32,128]{3,2,1,0:T(8,128)}, u32[]{:S(2)}) copy-start(f32[1,3,32,128]{3,2,1,0:T(8,128)} %param.11) | copy-start | bytes 147460
  180.9 31.6 %all-to-all-start.1 = ((bf16[8,128,896]{2,1,0:T(8,128)(2,1)}), bf16[8,128,896]{2,1,0:T(8,128)(2,1)S(1)}, u32[]{:S(2)}, u32[]{:S(2)}) async-start(bf16[8,128,896]{2,1,0:T(8,128)(2,1)} %fusion.10), calls=%async_computation.1 | async-start | bytes 3670016 | tf_op jit(solution)/shard_map/all_to_all | solution.py:97
  186.7 13.2 %collective-permute-start.9 = (f32[3,32,128]{2,1,0:T(8,128)S(1)}, f32[3,32,128]{2,1,0:T(8,128)S(1)}, u32[]{:S(2)}, u32[]{:S(2)}) collective-permute-start(f32[3,32,128]{2,1,0:T(8,128)S(1)} %get-tuple-element.17), channel_id=1, source_target_pairs={{0,224},{8,232},{16,240},{24,248},{32,192},{40,200},{48,208},{56,2... | collective-permute-start | bytes 147464 | tf_op jit(solution)/shard_map/ppermute | solution.py:70
  192.4 7.6 %collective-permute-start.8 = (f32[3,32,128]{2,1,0:T(8,128)S(1)}, f32[3,32,128]{2,1,0:T(8,128)S(1)}, u32[]{:S(2)}, u32[]{:S(2)}) collective-permute-start(f32[3,32,128]{2,1,0:T(8,128)S(1)} %get-tuple-element.18), channel_id=1, source_target_pairs={{0,192},{8,200},{16,208},{24,216},{32,224},{40,232},{48,240},{56,2... | collective-permute-start | bytes 147464 | tf_op jit(solution)/shard_map/ppermute | solution.py:70
  193.1 8.7 %collective-permute-start.7 = (f32[3,32,128]{2,1,0:T(8,128)S(1)}, f32[3,32,128]{2,1,0:T(8,128)S(1)}, u32[]{:S(2)}, u32[]{:S(2)}) collective-permute-start(f32[3,32,128]{2,1,0:T(8,128)S(1)} %get-tuple-element.19), channel_id=1, source_target_pairs={{0,160},{8,168},{16,176},{24,184},{32,128},{40,136},{48,144},{56,1... | collective-permute-start | bytes 147464 | tf_op jit(solution)/shard_map/ppermute | solution.py:70
  196.4 7.3 %collective-permute-start.6 = (f32[3,32,128]{2,1,0:T(8,128)S(1)}, f32[3,32,128]{2,1,0:T(8,128)S(1)}, u32[]{:S(2)}, u32[]{:S(2)}) collective-permute-start(f32[3,32,128]{2,1,0:T(8,128)S(1)} %get-tuple-element.20), channel_id=1, source_target_pairs={{0,128},{8,136},{16,144},{24,152},{32,160},{40,168},{48,176},{56,1... | collective-permute-start | bytes 147464 | tf_op jit(solution)/shard_map/ppermute | solution.py:70
  198.2 5.6 %collective-permute-start.5 = (f32[3,32,128]{2,1,0:T(8,128)S(1)}, f32[3,32,128]{2,1,0:T(8,128)S(1)}, u32[]{:S(2)}, u32[]{:S(2)}) collective-permute-start(f32[3,32,128]{2,1,0:T(8,128)S(1)} %get-tuple-element.21), channel_id=1, source_target_pairs={{0,96},{8,104},{16,112},{24,120},{32,64},{40,72},{48,80},{56,88},{... | collective-permute-start | bytes 147464 | tf_op jit(solution)/shard_map/ppermute | solution.py:70
  199.9 7.8 %collective-permute-start.4 = (f32[3,32,128]{2,1,0:T(8,128)S(1)}, f32[3,32,128]{2,1,0:T(8,128)S(1)}, u32[]{:S(2)}, u32[]{:S(2)}) collective-permute-start(f32[3,32,128]{2,1,0:T(8,128)S(1)} %get-tuple-element.22), channel_id=1, source_target_pairs={{0,64},{8,72},{16,80},{24,88},{32,96},{40,104},{48,112},{56,120},{... | collective-permute-start | bytes 147464 | tf_op jit(solution)/shard_map/ppermute | solution.py:70
  200.0 7.6 %collective-permute-start.3 = (f32[3,32,128]{2,1,0:T(8,128)S(1)}, f32[3,32,128]{2,1,0:T(8,128)S(1)}, u32[]{:S(2)}, u32[]{:S(2)}) collective-permute-start(f32[3,32,128]{2,1,0:T(8,128)S(1)} %get-tuple-element.16), channel_id=1, source_target_pairs={{0,32},{8,40},{16,48},{24,56},{32,0},{40,8},{48,16},{56,24},{64,96... | collective-permute-start | bytes 147464 | tf_op jit(solution)/shard_map/ppermute | solution.py:70
  207.7 8.9 %copy-start.2 = (f32[1,3,32,128]{3,2,1,0:T(8,128)}, f32[1,3,32,128]{3,2,1,0:T(8,128)S(1)}, u32[]{:S(2)}) copy-start(f32[1,3,32,128]{3,2,1,0:T(8,128)S(1)} %bitcast_add_fusion.1) | copy-start | bytes 147460
  212.5 1.3 copy-start.1

commit v15 on v14

--- a/solution.py
+++ b/solution.py
@@ -14,15 +14,24 @@
 def place_blocks(blocks):
     count, rows, width = blocks.shape
 
-    def body(block_ref, out_ref):
-        for p in range(count):
-            out_ref[:, p * width:(p + 1) * width] = block_ref[p]
+    def body(block_ref, out_ref, sems):
+        copies = [
+            pltpu.make_async_copy(
+                block_ref.at[p], out_ref.at[:, pl.ds(p * width, width)], sems.at[p]
+            )
+            for p in range(count)
+        ]
+        for c in copies:
+            c.start()
+        for c in copies:
+            c.wait()
 
     return pl.pallas_call(
         body,
         out_shape=jax.ShapeDtypeStruct((rows, count * width), blocks.dtype),
-        in_specs=[pl.BlockSpec(memory_space=pltpu.VMEM)],
-        out_specs=pl.BlockSpec(memory_space=pltpu.VMEM),
+        in_specs=[pl.BlockSpec(memory_space=pl.ANY)],
+        out_specs=pl.BlockSpec(memory_space=pl.ANY),
+        scratch_shapes=[pltpu.SemaphoreType.DMA((count,))],
     )(blocks)
 
 

time: 217 us -> 271 us (1.25)
  Pallas kernels: 9.15 us -> 63 us
    pallas_call x1, Pallas kernels: 2.86 us -> 56.8 us  [place_blocks(): pl.pallas_call(body, out_shape=jax.ShapeDtypeStruct((rows, count * width)...]
  transfers between devices with their start and end apart: 12 -> 12, of which waited for: 6 -> 6; matrix products, arithmetic and copies ran while one was open for 8% -> 6% of each run, Pallas kernels for 0% -> 0%
where the time goes in v15:
time: 271 us
  waiting for transfers between devices  148 us (55%)
  Pallas kernels  63 us (23%)
  starting transfers between devices  30.4 us (11%)
  matrix products  20.8 us (8%)
  local copies, waits for them, and re-layouts  5.71 us (2%)
    all_to_all x1, waiting for transfers between devices, on_device(): lax.all_to_all(outgoing, 'fsdp', split_axis=0, concat_axis=0, tiled=True)  139 us
    pallas_call x1, Pallas kernels, place_blocks(): pl.pallas_call(body, out_shape=jax.ShapeDtypeStruct((rows, count * width)...  56.8 us
    ppermute x7, starting transfers between devices, grouped_scatter(): lax.ppermute(send, 'rep', [(j, j ^ mask * inner) for j in range(replicas)])  15.1 us
    dot_general x1, matrix products, on_device(): jnp.einsum('ptd,hd->pth', gathered, down_weight, preferred_element_type=j...  12.2 us
    pallas_call x1, Pallas kernels, build_outgoing(): pl.pallas_call(body, out_shape=jax.ShapeDtypeStruct((count, rows, width +...  6.29 us
    all_to_all x1, starting transfers between devices, on_device(): lax.all_to_all(outgoing, 'fsdp', split_axis=0, concat_axis=0, tiled=True)  5.86 us
    ppermute x7, waiting for transfers between devices, grouped_scatter(): lax.ppermute(send, 'rep', [(j, j ^ mask * inner) for j in range(replicas)])  5.84 us
    ppermute x3, starting transfers between devices, grouped_scatter(): lax.ppermute(send, 'rep', [(j, j ^ mask) for j in range(replicas)])  5.76 us
  transfers between devices with their start and end apart: 12, of which 6 were waited for; matrix products, arithmetic and copies ran while one was open for 6% of the time, Pallas kernels for 0%

profile of v15, /device:TPU:1, one launch (start us, length us, event | category | flops | bytes accessed | tf_op | source)
XLA Modules:
  0.0 270.7 jit_solution(11926737684021640110)
XLA Ops:
  0.6 6.3 %shard_map.93 = bf16[8,128,4992]{2,1,0:T(8,128)(2,1)} custom-call(bf16[128,4096]{1,0:T(8,128)(2,1)} %grad_ref.1, bf16[128,7168]{1,0:T(8,128)(2,1)} %hidden_ref.1), custom_call_target="tpu_custom_call" | custom-call | tf_op jit(solution)/shard_map/pallas_call | solution.py:47
  6.9 5.9 %all-to-all-start = ((bf16[8,128,4992]{2,1,0:T(8,128)(2,1)}), bf16[8,128,4992]{2,1,0:T(8,128)(2,1)}, u32[]{:S(2)}, u32[]{:S(2)}) async-start(bf16[8,128,4992]{2,1,0:T(8,128)(2,1)} %shard_map.93), calls=%async_computation | async-start | bytes 20447232 | tf_op jit(solution)/shard_map/all_to_all | solution.py:99
  12.8 139.0 %all-to-all-done = bf16[8,128,4992]{2,1,0:T(8,128)(2,1)} async-done(((bf16[8,128,4992]{2,1,0:T(8,128)(2,1)}), bf16[8,128,4992]{2,1,0:T(8,128)(2,1)}, u32[]{:S(2)}, u32[]{:S(2)}) %all-to-all-start) | async-done | bytes 10223648 | tf_op jit(solution)/shard_map/all_to_all | solution.py:99
  151.8 2.2 fusion.18
  154.0 0.2 copy.15
  154.5 5.0 %fusion.5 = f32[288,4096]{1,0:T(8,128)S(1)} fusion(bf16[8,128,4992]{2,1,0:T(8,128)(2,1)} %all-to-all-done, bf16[288,8,128]{2,1,0:T(8,128)(2,1)S(1)} %bitcast.93), kind=kOutput, calls=%fused_computation.5 | convolution fusion | flops 2415919104 | bytes 13697024 | tf_op jit(solution)/shard_map/mpt,ptd->md/dot_general | solution.py:116
  159.6 0.3 fusion.16
  159.9 0.3 copy.23
  160.2 1.8 constant_dynamic-slice_fusion.3
  162.0 5.3 %collective-permute-start.2 = (f32[8,3,32,128]{3,2,1,0:T(8,128)S(1)}, f32[8,3,32,128]{3,2,1,0:T(8,128)}, u32[]{:S(2)}, u32[]{:S(2)}) collective-permute-start(f32[8,3,32,128]{3,2,1,0:T(8,128)S(1)} %bitcast.94), channel_id=1, source_target_pairs={{0,24},{8,16},{16,8},{24,0},{32,56},{40,48},{48,40},{56,32},{64,88... | collective-permute-start | bytes 1179656 | tf_op jit(solution)/shard_map/ppermute | solution.py:74
  167.3 0.1 collective-permute-start.1
  167.5 0.8 copy.32
  168.3 0.4 collective-permute-start
  168.7 12.2 %fusion.10 = bf16[8,128,896]{2,1,0:T(8,128)(2,1)} fusion(bf16[896,4096]{1,0:T(8,128)(2,1)S(1)} %bitcast.97, bf16[8,128,4992]{2,1,0:T(8,128)(2,1)} %all-to-all-done), kind=kOutput, calls=%fused_computation.8 | convolution fusion | flops 7517110272 | bytes 17563648 | tf_op jit(solution)/shard_map/ptd,hd->pth/dot_general | solution.py:102
  180.9 3.7 %all-to-all-start.1 = ((bf16[8,128,896]{2,1,0:T(8,128)(2,1)}), bf16[8,128,896]{2,1,0:T(8,128)(2,1)S(1)}, u32[]{:S(2)}, u32[]{:S(2)}) async-start(bf16[8,128,896]{2,1,0:T(8,128)(2,1)} %fusion.10), calls=%async_computation.1 | async-start | bytes 3670016 | tf_op jit(solution)/shard_map/all_to_all | solution.py:106
  184.7 0.5 collective-permute-done.1
  185.2 1.4 fusion.26
  186.7 5.7 %collective-permute-start.9 = (f32[3,32,128]{2,1,0:T(8,128)S(1)}, f32[3,32,128]{2,1,0:T(8,128)S(1)}, u32[]{:S(2)}, u32[]{:S(2)}) collective-permute-start(f32[3,32,128]{2,1,0:T(8,128)S(1)} %get-tuple-element.17), channel_id=1, source_target_pairs={{0,224},{8,232},{16,240},{24,248},{32,192},{40,200},{48,208},{56,2... | collective-permute-start | bytes 147464 | tf_op jit(solution)/shard_map/ppermute | solution.py:79
  192.4 0.7 collective-permute-start.8
  193.1 3.3 %collective-permute-start.7 = (f32[3,32,128]{2,1,0:T(8,128)S(1)}, f32[3,32,128]{2,1,0:T(8,128)S(1)}, u32[]{:S(2)}, u32[]{:S(2)}) collective-permute-start(f32[3,32,128]{2,1,0:T(8,128)S(1)} %get-tuple-element.19), channel_id=1, source_target_pairs={{0,160},{8,168},{16,176},{24,184},{32,128},{40,136},{48,144},{56,1... | collective-permute-start | bytes 147464 | tf_op jit(solution)/shard_map/ppermute | solution.py:79
  196.4 1.8 collective-permute-start.6
  198.2 1.6 collective-permute-start.5
  199.9 0.1 collective-permute-start.4
  200.0 1.8 collective-permute-start.3
  201.8 2.0 collective-permute-done.6
  203.8 3.8 %collective-permute-done.4 = f32[3,32,128]{2,1,0:T(8,128)S(1)} collective-permute-done((f32[3,32,128]{2,1,0:T(8,128)S(1)}, f32[3,32,128]{2,1,0:T(8,128)S(1)}, u32[]{:S(2)}, u32[]{:S(2)}) %collective-permute-start.4) | collective-permute-done | bytes 49184 | tf_op jit(solution)/shard_map/ppermute | solution.py:79
  207.7 0.4 fusion.17
  208.1 1.0 copy.21
  209.1 1.0 fusion.21
  210.1 2.4 all-to-all-done.1.block_ref
  212.5 1.3 copy-done.1
  213.7 56.8 %shard_map.94 = bf16[128,7168]{1,0:T(8,128)(2,1)} custom-call(bf16[8,128,896]{2,1,0:T(8,128)(2,1)} %copy-done.1), custom_call_target="tpu_custom_call" | custom-call | tf_op jit(solution)/shard_map/pallas_call | solution.py:29
  (29 shorter events, 0.7 us)
Async XLA Ops:
  0.6 151.1 %copy-start = (bf16[3,32,896]{2,1,0:T(8,128)(2,1)S(1)}, bf16[3,32,896]{2,1,0:T(8,128)(2,1)}, u32[]{:S(2)}) copy-start(bf16[3,32,896]{2,1,0:T(8,128)(2,1)} %param.9) | copy-start | bytes 516100
  6.9 144.8 %all-to-all-start = ((bf16[8,128,4992]{2,1,0:T(8,128)(2,1)}), bf16[8,128,4992]{2,1,0:T(8,128)(2,1)}, u32[]{:S(2)}, u32[]{:S(2)}) async-start(bf16[8,128,4992]{2,1,0:T(8,128)(2,1)} %shard_map.93), calls=%async_computation | async-start | bytes 20447232 | tf_op jit(solution)/shard_map/all_to_all | solution.py:99
  159.6 9.1 %slice-start = ((s8[7340032]{0:T(1024)(128)(4,1)}), s8[4194304]{0:T(1024)(128)(4,1)S(1)}, s32[]{:S(2)}) async-start(s8[7340032]{0:T(1024)(128)(4,1)} %bitcast.96), calls=%async_computation.2 | async-start | bytes 8388608
  159.9 8.8 %slice-start.1 = ((s8[7340032]{0:T(1024)(128)(4,1)}), s8[3145728]{0:T(1024)(128)(4,1)S(1)}, s32[]{:S(2)}) async-start(s8[7340032]{0:T(1024)(128)(4,1)} %bitcast.96), calls=%async_computation.3 | async-start | bytes 6291456
  162.0 22.7 %collective-permute-start.2 = (f32[8,3,32,128]{3,2,1,0:T(8,128)S(1)}, f32[8,3,32,128]{3,2,1,0:T(8,128)}, u32[]{:S(2)}, u32[]{:S(2)}) collective-permute-start(f32[8,3,32,128]{3,2,1,0:T(8,128)S(1)} %bitcast.94), channel_id=1, source_target_pairs={{0,24},{8,16},{16,8},{24,0},{32,56},{40,48},{48,40},{56,32},{64,88... | collective-permute-start | bytes 1179656 | tf_op jit(solution)/shard_map/ppermute | solution.py:74
  167.3 17.9 %collective-permute-start.1 = (f32[8,3,32,128]{3,2,1,0:T(8,128)S(1)}, f32[8,3,32,128]{3,2,1,0:T(8,128)}, u32[]{:S(2)}, u32[]{:S(2)}) collective-permute-start(f32[8,3,32,128]{3,2,1,0:T(8,128)S(1)} %bitcast.95), channel_id=1, source_target_pairs={{0,16},{8,24},{16,0},{24,8},{32,48},{40,56},{48,32},{56,40},{64,80... | collective-permute-start | bytes 1179656 | tf_op jit(solution)/shard_map/ppermute | solution.py:74
  168.3 16.9 %collective-permute-start = (f32[8,3,32,128]{3,2,1,0:T(8,128)}, f32[8,3,32,128]{3,2,1,0:T(8,128)}, u32[]{:S(2)}, u32[]{:S(2)}) collective-permute-start(f32[8,3,32,128]{3,2,1,0:T(8,128)} %bitcast.88), channel_id=1, source_target_pairs={{0,8},{8,0},{16,24},{24,16},{32,40},{40,32},{48,56},{56,48},{64,72... | collective-permute-start | bytes 1179656 | tf_op jit(solution)/shard_map/ppermute | solution.py:74
  180.9 26.7 %copy-start.4 = (f32[1,3,32,128]{3,2,1,0:T(8,128)S(1)}, f32[1,3,32,128]{3,2,1,0:T(8,128)}, u32[]{:S(2)}) copy-start(f32[1,3,32,128]{3,2,1,0:T(8,128)} %param.10) | copy-start | bytes 147460
  180.9 26.8 %copy-start.3 = (f32[1,3,32,128]{3,2,1,0:T(8,128)S(1)}, f32[1,3,32,128]{3,2,1,0:T(8,128)}, u32[]{:S(2)}) copy-start(f32[1,3,32,128]{3,2,1,0:T(8,128)} %param.11) | copy-start | bytes 147460
  180.9 31.6 %all-to-all-start.1 = ((bf16[8,128,896]{2,1,0:T(8,128)(2,1)}), bf16[8,128,896]{2,1,0:T(8,128)(2,1)S(1)}, u32[]{:S(2)}, u32[]{:S(2)}) async-start(bf16[8,128,896]{2,1,0:T(8,128)(2,1)} %fusion.10), calls=%async_computation.1 | async-start | bytes 3670016 | tf_op jit(solution)/shard_map/all_to_all | solution.py:106
  186.7 13.2 %collective-permute-start.9 = (f32[3,32,128]{2,1,0:T(8,128)S(1)}, f32[3,32,128]{2,1,0:T(8,128)S(1)}, u32[]{:S(2)}, u32[]{:S(2)}) collective-permute-start(f32[3,32,128]{2,1,0:T(8,128)S(1)} %get-tuple-element.17), channel_id=1, source_target_pairs={{0,224},{8,232},{16,240},{24,248},{32,192},{40,200},{48,208},{56,2... | collective-permute-start | bytes 147464 | tf_op jit(solution)/shard_map/ppermute | solution.py:79
  192.4 7.6 %collective-permute-start.8 = (f32[3,32,128]{2,1,0:T(8,128)S(1)}, f32[3,32,128]{2,1,0:T(8,128)S(1)}, u32[]{:S(2)}, u32[]{:S(2)}) collective-permute-start(f32[3,32,128]{2,1,0:T(8,128)S(1)} %get-tuple-element.18), channel_id=1, source_target_pairs={{0,192},{8,200},{16,208},{24,216},{32,224},{40,232},{48,240},{56,2... | collective-permute-start | bytes 147464 | tf_op jit(solution)/shard_map/ppermute | solution.py:79
  193.1 8.7 %collective-permute-start.7 = (f32[3,32,128]{2,1,0:T(8,128)S(1)}, f32[3,32,128]{2,1,0:T(8,128)S(1)}, u32[]{:S(2)}, u32[]{:S(2)}) collective-permute-start(f32[3,32,128]{2,1,0:T(8,128)S(1)} %get-tuple-element.19), channel_id=1, source_target_pairs={{0,160},{8,168},{16,176},{24,184},{32,128},{40,136},{48,144},{56,1... | collective-permute-start | bytes 147464 | tf_op jit(solution)/shard_map/ppermute | solution.py:79
  196.4 7.3 %collective-permute-start.6 = (f32[3,32,128]{2,1,0:T(8,128)S(1)}, f32[3,32,128]{2,1,0:T(8,128)S(1)}, u32[]{:S(2)}, u32[]{:S(2)}) collective-permute-start(f32[3,32,128]{2,1,0:T(8,128)S(1)} %get-tuple-element.20), channel_id=1, source_target_pairs={{0,128},{8,136},{16,144},{24,152},{32,160},{40,168},{48,176},{56,1... | collective-permute-start | bytes 147464 | tf_op jit(solution)/shard_map/ppermute | solution.py:79
  198.2 5.6 %collective-permute-start.5 = (f32[3,32,128]{2,1,0:T(8,128)S(1)}, f32[3,32,128]{2,1,0:T(8,128)S(1)}, u32[]{:S(2)}, u32[]{:S(2)}) collective-permute-start(f32[3,32,128]{2,1,0:T(8,128)S(1)} %get-tuple-element.21), channel_id=1, source_target_pairs={{0,96},{8,104},{16,112},{24,120},{32,64},{40,72},{48,80},{56,88},{... | collective-permute-start | bytes 147464 | tf_op jit(solution)/shard_map/ppermute | solution.py:79
  199.9 7.8 %collective-permute-start.4 = (f32[3,32,128]{2,1,0:T(8,128)S(1)}, f32[3,32,128]{2,1,0:T(8,128)S(1)}, u32[]{:S(2)}, u32[]{:S(2)}) collective-permute-start(f32[3,32,128]{2,1,0:T(8,128)S(1)} %get-tuple-element.22), channel_id=1, source_target_pairs={{0,64},{8,72},{16,80},{24,88},{32,96},{40,104},{48,112},{56,120},{... | collective-permute-start | bytes 147464 | tf_op jit(solution)/shard_map/ppermute | solution.py:79
  200.0 7.6 %collective-permute-start.3 = (f32[3,32,128]{2,1,0:T(8,128)S(1)}, f32[3,32,128]{2,1,0:T(8,128)S(1)}, u32[]{:S(2)}, u32[]{:S(2)}) collective-permute-start(f32[3,32,128]{2,1,0:T(8,128)S(1)} %get-tuple-element.16), channel_id=1, source_target_pairs={{0,32},{8,40},{16,48},{24,56},{32,0},{40,8},{48,16},{56,24},{64,96... | collective-permute-start | bytes 147464 | tf_op jit(solution)/shard_map/ppermute | solution.py:79
  207.7 62.8 %copy-start.2 = (f32[1,3,32,128]{3,2,1,0:T(8,128)}, f32[1,3,32,128]{3,2,1,0:T(8,128)S(1)}, u32[]{:S(2)}) copy-start(f32[1,3,32,128]{3,2,1,0:T(8,128)S(1)} %bitcast_add_fusion.1) | copy-start | bytes 147460
  212.5 1.3 copy-start.1

commit v16 on v15

--- a/solution.py
+++ b/solution.py
@@ -30,7 +30,7 @@
         body,
         out_shape=jax.ShapeDtypeStruct((rows, count * width), blocks.dtype),
         in_specs=[pl.BlockSpec(memory_space=pl.ANY)],
-        out_specs=pl.BlockSpec(memory_space=pl.ANY),
+        out_specs=pl.BlockSpec(memory_space=pltpu.VMEM),
         scratch_shapes=[pltpu.SemaphoreType.DMA((count,))],
     )(blocks)
 

time: 271 us -> 217 us (0.80)
  Pallas kernels: 63 us -> 9.14 us
    pallas_call x1, Pallas kernels: 56.8 us -> 2.85 us  [place_blocks(): pl.pallas_call(body, out_shape=jax.ShapeDtypeStruct((rows, count * width)...]
  transfers between devices with their start and end apart: 12 -> 12, of which waited for: 6 -> 6; matrix products, arithmetic and copies ran while one was open for 6% -> 8% of each run, Pallas kernels for 0% -> 0%
where the time goes in v16:
time: 217 us
  waiting for transfers between devices  148 us (68%)
  starting transfers between devices  30.4 us (14%)
  matrix products  20.8 us (10%)
  Pallas kernels  9.14 us (4%)
  local copies, waits for them, and re-layouts  5.71 us (3%)
    all_to_all x1, waiting for transfers between devices, on_device(): lax.all_to_all(outgoing, 'fsdp', split_axis=0, concat_axis=0, tiled=True)  139 us
    ppermute x7, starting transfers between devices, grouped_scatter(): lax.ppermute(send, 'rep', [(j, j ^ mask * inner) for j in range(replicas)])  15.1 us
    dot_general x1, matrix products, on_device(): jnp.einsum('ptd,hd->pth', gathered, down_weight, preferred_element_type=j...  12.2 us
    pallas_call x1, Pallas kernels, build_outgoing(): pl.pallas_call(body, out_shape=jax.ShapeDtypeStruct((count, rows, width +...  6.29 us
    all_to_all x1, starting transfers between devices, on_device(): lax.all_to_all(outgoing, 'fsdp', split_axis=0, concat_axis=0, tiled=True)  5.86 us
    ppermute x7, waiting for transfers between devices, grouped_scatter(): lax.ppermute(send, 'rep', [(j, j ^ mask * inner) for j in range(replicas)])  5.84 us
    ppermute x3, starting transfers between devices, grouped_scatter(): lax.ppermute(send, 'rep', [(j, j ^ mask) for j in range(replicas)])  5.76 us
    dot_general x1, matrix products, on_device(): jnp.einsum('mpt,ptd->md', pieces.reshape(3 * sketch_rows, shards, tok_row...  5 us
  transfers between devices with their start and end apart: 12, of which 6 were waited for; matrix products, arithmetic and copies ran while one was open for 8% of the time, Pallas kernels for 0%

profile of v16, /device:TPU:1, one launch (start us, length us, event | category | flops | bytes accessed | tf_op | source)
XLA Modules:
  0.0 216.7 jit_solution(9757476946434645318)
XLA Ops:
  0.6 6.3 %shard_map.93 = bf16[8,128,4992]{2,1,0:T(8,128)(2,1)} custom-call(bf16[128,4096]{1,0:T(8,128)(2,1)} %grad_ref.1, bf16[128,7168]{1,0:T(8,128)(2,1)} %hidden_ref.1), custom_call_target="tpu_custom_call" | custom-call | tf_op jit(solution)/shard_map/pallas_call | solution.py:47
  6.9 5.9 %all-to-all-start = ((bf16[8,128,4992]{2,1,0:T(8,128)(2,1)}), bf16[8,128,4992]{2,1,0:T(8,128)(2,1)}, u32[]{:S(2)}, u32[]{:S(2)}) async-start(bf16[8,128,4992]{2,1,0:T(8,128)(2,1)} %shard_map.93), calls=%async_computation | async-start | bytes 20447232 | tf_op jit(solution)/shard_map/all_to_all | solution.py:99
  12.8 139.0 %all-to-all-done = bf16[8,128,4992]{2,1,0:T(8,128)(2,1)} async-done(((bf16[8,128,4992]{2,1,0:T(8,128)(2,1)}), bf16[8,128,4992]{2,1,0:T(8,128)(2,1)}, u32[]{:S(2)}, u32[]{:S(2)}) %all-to-all-start) | async-done | bytes 10223648 | tf_op jit(solution)/shard_map/all_to_all | solution.py:99
  151.8 2.2 %fusion.18 = f32[96,8,128]{2,0,1:T(8,128)S(1)} fusion(bf16[96,896,1]{1,0,2:T(8,128)(2,1)S(1)} %bitcast.89, bf16[8,128,4992]{2,1,0:T(8,128)(2,1)} %all-to-all-done), kind=kOutput, calls=%fused_computation.15 | convolution fusion | flops 176160768 | bytes 2400256 | tf_op jit(solution)/shard_map/ki,pti->kpt/dot_general | solution.py:109
  154.0 0.2 copy.15
  154.5 5.0 %fusion.5 = f32[288,4096]{1,0:T(8,128)S(1)} fusion(bf16[8,128,4992]{2,1,0:T(8,128)(2,1)} %all-to-all-done, bf16[288,8,128]{2,1,0:T(8,128)(2,1)S(1)} %bitcast.93), kind=kOutput, calls=%fused_computation.5 | convolution fusion | flops 2415919104 | bytes 13697024 | tf_op jit(solution)/shard_map/mpt,ptd->md/dot_general | solution.py:116
  159.6 0.3 fusion.16
  159.9 0.3 copy.23
  160.2 1.8 constant_dynamic-slice_fusion.3
  162.0 5.3 %collective-permute-start.2 = (f32[8,3,32,128]{3,2,1,0:T(8,128)S(1)}, f32[8,3,32,128]{3,2,1,0:T(8,128)}, u32[]{:S(2)}, u32[]{:S(2)}) collective-permute-start(f32[8,3,32,128]{3,2,1,0:T(8,128)S(1)} %bitcast.94), channel_id=1, source_target_pairs={{0,24},{8,16},{16,8},{24,0},{32,56},{40,48},{48,40},{56,32},{64,88... | collective-permute-start | bytes 1179656 | tf_op jit(solution)/shard_map/ppermute | solution.py:74
  167.3 0.1 collective-permute-start.1
  167.5 0.8 copy.32
  168.3 0.4 collective-permute-start
  168.7 12.2 %fusion.10 = bf16[8,128,896]{2,1,0:T(8,128)(2,1)} fusion(bf16[896,4096]{1,0:T(8,128)(2,1)S(1)} %bitcast.97, bf16[8,128,4992]{2,1,0:T(8,128)(2,1)} %all-to-all-done), kind=kOutput, calls=%fused_computation.8 | convolution fusion | flops 7517110272 | bytes 17563648 | tf_op jit(solution)/shard_map/ptd,hd->pth/dot_general | solution.py:102
  180.9 3.7 %all-to-all-start.1 = ((bf16[8,128,896]{2,1,0:T(8,128)(2,1)}), bf16[8,128,896]{2,1,0:T(8,128)(2,1)S(1)}, u32[]{:S(2)}, u32[]{:S(2)}) async-start(bf16[8,128,896]{2,1,0:T(8,128)(2,1)} %fusion.10), calls=%async_computation.1 | async-start | bytes 3670016 | tf_op jit(solution)/shard_map/all_to_all | solution.py:106
  184.7 0.5 collective-permute-done.1
  185.2 1.4 fusion.26
  186.7 5.7 %collective-permute-start.9 = (f32[3,32,128]{2,1,0:T(8,128)S(1)}, f32[3,32,128]{2,1,0:T(8,128)S(1)}, u32[]{:S(2)}, u32[]{:S(2)}) collective-permute-start(f32[3,32,128]{2,1,0:T(8,128)S(1)} %get-tuple-element.17), channel_id=1, source_target_pairs={{0,224},{8,232},{16,240},{24,248},{32,192},{40,200},{48,208},{56,2... | collective-permute-start | bytes 147464 | tf_op jit(solution)/shard_map/ppermute | solution.py:79
  192.4 0.7 collective-permute-start.8
  193.1 3.3 %collective-permute-start.7 = (f32[3,32,128]{2,1,0:T(8,128)S(1)}, f32[3,32,128]{2,1,0:T(8,128)S(1)}, u32[]{:S(2)}, u32[]{:S(2)}) collective-permute-start(f32[3,32,128]{2,1,0:T(8,128)S(1)} %get-tuple-element.19), channel_id=1, source_target_pairs={{0,160},{8,168},{16,176},{24,184},{32,128},{40,136},{48,144},{56,1... | collective-permute-start | bytes 147464 | tf_op jit(solution)/shard_map/ppermute | solution.py:79
  196.4 1.8 collective-permute-start.6
  198.2 1.6 collective-permute-start.5
  199.9 0.1 collective-permute-start.4
  200.0 1.8 collective-permute-start.3
  201.8 2.0 collective-permute-done.6
  203.8 3.8 %collective-permute-done.4 = f32[3,32,128]{2,1,0:T(8,128)S(1)} collective-permute-done((f32[3,32,128]{2,1,0:T(8,128)S(1)}, f32[3,32,128]{2,1,0:T(8,128)S(1)}, u32[]{:S(2)}, u32[]{:S(2)}) %collective-permute-start.4) | collective-permute-done | bytes 49184 | tf_op jit(solution)/shard_map/ppermute | solution.py:79
  207.7 0.4 fusion.17
  208.1 1.0 copy.21
  209.1 1.0 fusion.21
  210.1 2.4 %all-to-all-done.1.block_ref = bf16[8,128,896]{2,1,0:T(8,128)(2,1)S(1)} async-done(((bf16[8,128,896]{2,1,0:T(8,128)(2,1)}), bf16[8,128,896]{2,1,0:T(8,128)(2,1)S(1)}, u32[]{:S(2)}, u32[]{:S(2)}) %all-to-all-start.1) | async-done | bytes 1835040 | tf_op jit(solution)/shard_map/all_to_all | solution.py:106
  212.5 1.3 copy-done.1
  213.7 2.9 %shard_map.94 = bf16[128,7168]{1,0:T(8,128)(2,1)} custom-call(bf16[8,128,896]{2,1,0:T(8,128)(2,1)} %copy-done.1), custom_call_target="tpu_custom_call" | custom-call | tf_op jit(solution)/shard_map/pallas_call | solution.py:29
  (29 shorter events, 0.7 us)
Async XLA Ops:
  0.6 151.1 %copy-start = (bf16[3,32,896]{2,1,0:T(8,128)(2,1)S(1)}, bf16[3,32,896]{2,1,0:T(8,128)(2,1)}, u32[]{:S(2)}) copy-start(bf16[3,32,896]{2,1,0:T(8,128)(2,1)} %param.9) | copy-start | bytes 516100
  6.9 144.8 %all-to-all-start = ((bf16[8,128,4992]{2,1,0:T(8,128)(2,1)}), bf16[8,128,4992]{2,1,0:T(8,128)(2,1)}, u32[]{:S(2)}, u32[]{:S(2)}) async-start(bf16[8,128,4992]{2,1,0:T(8,128)(2,1)} %shard_map.93), calls=%async_computation | async-start | bytes 20447232 | tf_op jit(solution)/shard_map/all_to_all | solution.py:99
  159.6 9.1 %slice-start = ((s8[7340032]{0:T(1024)(128)(4,1)}), s8[4194304]{0:T(1024)(128)(4,1)S(1)}, s32[]{:S(2)}) async-start(s8[7340032]{0:T(1024)(128)(4,1)} %bitcast.96), calls=%async_computation.2 | async-start | bytes 8388608
  159.9 8.8 %slice-start.1 = ((s8[7340032]{0:T(1024)(128)(4,1)}), s8[3145728]{0:T(1024)(128)(4,1)S(1)}, s32[]{:S(2)}) async-start(s8[7340032]{0:T(1024)(128)(4,1)} %bitcast.96), calls=%async_computation.3 | async-start | bytes 6291456
  162.0 22.7 %collective-permute-start.2 = (f32[8,3,32,128]{3,2,1,0:T(8,128)S(1)}, f32[8,3,32,128]{3,2,1,0:T(8,128)}, u32[]{:S(2)}, u32[]{:S(2)}) collective-permute-start(f32[8,3,32,128]{3,2,1,0:T(8,128)S(1)} %bitcast.94), channel_id=1, source_target_pairs={{0,24},{8,16},{16,8},{24,0},{32,56},{40,48},{48,40},{56,32},{64,88... | collective-permute-start | bytes 1179656 | tf_op jit(solution)/shard_map/ppermute | solution.py:74
  167.3 17.9 %collective-permute-start.1 = (f32[8,3,32,128]{3,2,1,0:T(8,128)S(1)}, f32[8,3,32,128]{3,2,1,0:T(8,128)}, u32[]{:S(2)}, u32[]{:S(2)}) collective-permute-start(f32[8,3,32,128]{3,2,1,0:T(8,128)S(1)} %bitcast.95), channel_id=1, source_target_pairs={{0,16},{8,24},{16,0},{24,8},{32,48},{40,56},{48,32},{56,40},{64,80... | collective-permute-start | bytes 1179656 | tf_op jit(solution)/shard_map/ppermute | solution.py:74
  168.3 16.9 %collective-permute-start = (f32[8,3,32,128]{3,2,1,0:T(8,128)}, f32[8,3,32,128]{3,2,1,0:T(8,128)}, u32[]{:S(2)}, u32[]{:S(2)}) collective-permute-start(f32[8,3,32,128]{3,2,1,0:T(8,128)} %bitcast.88), channel_id=1, source_target_pairs={{0,8},{8,0},{16,24},{24,16},{32,40},{40,32},{48,56},{56,48},{64,72... | collective-permute-start | bytes 1179656 | tf_op jit(solution)/shard_map/ppermute | solution.py:74
  180.9 26.7 %copy-start.4 = (f32[1,3,32,128]{3,2,1,0:T(8,128)S(1)}, f32[1,3,32,128]{3,2,1,0:T(8,128)}, u32[]{:S(2)}) copy-start(f32[1,3,32,128]{3,2,1,0:T(8,128)} %param.10) | copy-start | bytes 147460
  180.9 26.8 %copy-start.3 = (f32[1,3,32,128]{3,2,1,0:T(8,128)S(1)}, f32[1,3,32,128]{3,2,1,0:T(8,128)}, u32[]{:S(2)}) copy-start(f32[1,3,32,128]{3,2,1,0:T(8,128)} %param.11) | copy-start | bytes 147460
  180.9 31.6 %all-to-all-start.1 = ((bf16[8,128,896]{2,1,0:T(8,128)(2,1)}), bf16[8,128,896]{2,1,0:T(8,128)(2,1)S(1)}, u32[]{:S(2)}, u32[]{:S(2)}) async-start(bf16[8,128,896]{2,1,0:T(8,128)(2,1)} %fusion.10), calls=%async_computation.1 | async-start | bytes 3670016 | tf_op jit(solution)/shard_map/all_to_all | solution.py:106
  186.7 13.2 %collective-permute-start.9 = (f32[3,32,128]{2,1,0:T(8,128)S(1)}, f32[3,32,128]{2,1,0:T(8,128)S(1)}, u32[]{:S(2)}, u32[]{:S(2)}) collective-permute-start(f32[3,32,128]{2,1,0:T(8,128)S(1)} %get-tuple-element.17), channel_id=1, source_target_pairs={{0,224},{8,232},{16,240},{24,248},{32,192},{40,200},{48,208},{56,2... | collective-permute-start | bytes 147464 | tf_op jit(solution)/shard_map/ppermute | solution.py:79
  192.4 7.6 %collective-permute-start.8 = (f32[3,32,128]{2,1,0:T(8,128)S(1)}, f32[3,32,128]{2,1,0:T(8,128)S(1)}, u32[]{:S(2)}, u32[]{:S(2)}) collective-permute-start(f32[3,32,128]{2,1,0:T(8,128)S(1)} %get-tuple-element.18), channel_id=1, source_target_pairs={{0,192},{8,200},{16,208},{24,216},{32,224},{40,232},{48,240},{56,2... | collective-permute-start | bytes 147464 | tf_op jit(solution)/shard_map/ppermute | solution.py:79
  193.1 8.7 %collective-permute-start.7 = (f32[3,32,128]{2,1,0:T(8,128)S(1)}, f32[3,32,128]{2,1,0:T(8,128)S(1)}, u32[]{:S(2)}, u32[]{:S(2)}) collective-permute-start(f32[3,32,128]{2,1,0:T(8,128)S(1)} %get-tuple-element.19), channel_id=1, source_target_pairs={{0,160},{8,168},{16,176},{24,184},{32,128},{40,136},{48,144},{56,1... | collective-permute-start | bytes 147464 | tf_op jit(solution)/shard_map/ppermute | solution.py:79
  196.4 7.3 %collective-permute-start.6 = (f32[3,32,128]{2,1,0:T(8,128)S(1)}, f32[3,32,128]{2,1,0:T(8,128)S(1)}, u32[]{:S(2)}, u32[]{:S(2)}) collective-permute-start(f32[3,32,128]{2,1,0:T(8,128)S(1)} %get-tuple-element.20), channel_id=1, source_target_pairs={{0,128},{8,136},{16,144},{24,152},{32,160},{40,168},{48,176},{56,1... | collective-permute-start | bytes 147464 | tf_op jit(solution)/shard_map/ppermute | solution.py:79
  198.2 5.6 %collective-permute-start.5 = (f32[3,32,128]{2,1,0:T(8,128)S(1)}, f32[3,32,128]{2,1,0:T(8,128)S(1)}, u32[]{:S(2)}, u32[]{:S(2)}) collective-permute-start(f32[3,32,128]{2,1,0:T(8,128)S(1)} %get-tuple-element.21), channel_id=1, source_target_pairs={{0,96},{8,104},{16,112},{24,120},{32,64},{40,72},{48,80},{56,88},{... | collective-permute-start | bytes 147464 | tf_op jit(solution)/shard_map/ppermute | solution.py:79
  199.9 7.8 %collective-permute-start.4 = (f32[3,32,128]{2,1,0:T(8,128)S(1)}, f32[3,32,128]{2,1,0:T(8,128)S(1)}, u32[]{:S(2)}, u32[]{:S(2)}) collective-permute-start(f32[3,32,128]{2,1,0:T(8,128)S(1)} %get-tuple-element.22), channel_id=1, source_target_pairs={{0,64},{8,72},{16,80},{24,88},{32,96},{40,104},{48,112},{56,120},{... | collective-permute-start | bytes 147464 | tf_op jit(solution)/shard_map/ppermute | solution.py:79
  200.0 7.6 %collective-permute-start.3 = (f32[3,32,128]{2,1,0:T(8,128)S(1)}, f32[3,32,128]{2,1,0:T(8,128)S(1)}, u32[]{:S(2)}, u32[]{:S(2)}) collective-permute-start(f32[3,32,128]{2,1,0:T(8,128)S(1)} %get-tuple-element.16), channel_id=1, source_target_pairs={{0,32},{8,40},{16,48},{24,56},{32,0},{40,8},{48,16},{56,24},{64,96... | collective-permute-start | bytes 147464 | tf_op jit(solution)/shard_map/ppermute | solution.py:79
  207.7 8.9 %copy-start.2 = (f32[1,3,32,128]{3,2,1,0:T(8,128)}, f32[1,3,32,128]{3,2,1,0:T(8,128)S(1)}, u32[]{:S(2)}) copy-start(f32[1,3,32,128]{3,2,1,0:T(8,128)S(1)} %bitcast_add_fusion.1) | copy-start | bytes 147460
  212.5 1.3 copy-start.1
